TPU v7x, 768 devices: a whole 4x8x12 slice. The times are simulated.
768 devices in a mesh: ctx: 192 (over y, z_lo, x), dp: 4 (over z_hi, core).
Axes of the slice: x: 4, y: 8, z: 12 (z_hi: 2, z_lo: 6; z = z_hi * 6 + z_lo), core: 2. Of those that a mesh axis runs over, the one named last changes fastest.
Arguments:
- att_query: bfloat16 [98304, 4096], P(('dp', 'ctx')), parts along dimension 0, may hold values from -126 to 126
- att_key: bfloat16 [98304, 4096], P(('dp', 'ctx')), parts along dimension 0, may hold values from -6 to 6
- att_value: bfloat16 [98304, 4096], P(('dp', 'ctx')), parts along dimension 0, may hold values from -6 to 6
Outputs:
- attn_out: bfloat16 [98304, 4096], P(('dp', 'ctx')), parts along dimension 0
- attn_lse: float32 [32, 98304], P(None, ('dp', 'ctx')), parts along dimension 1
There are 4 independent parts, one for each index of `dp`. A program takes and returns all parts, laid end to end along the dimension named above; each array names one. Nothing has to cross between parts.
All inputs are finite; a program needn't handle non-finite values.
Results may differ from a plain program's by a relative error of at most 0.0045.
Values may be sent and summed in bfloat16 or wider, within the bound.
No kernel may reach another device: no remote copies, remote signals or barrier semaphores. Data moves between devices by JAX's collectives and lax.ppermute only.
A program may use at most 32 MiB of HBM per device.

v0:
```python
import math

import jax
import jax.numpy as jnp
from jax import lax
from jax.sharding import PartitionSpec as P

HEAD_DIM = 128
KV_STEPS = 3


def from_behind(block, axis, distance):
    devices = range(lax.axis_size(axis))
    route = [(i - distance, i) for i in devices if i - distance in devices]
    return lax.ppermute(block, axis, route)


def attend(query_rows, key_rows, value_rows, key_start, query_start):
    row_count = query_rows.shape[0]
    key_count = key_rows.shape[0]
    head_count = query_rows.shape[1] // HEAD_DIM
    heads_block = math.gcd(head_count, 8)
    block_width = heads_block * HEAD_DIM
    key_place = key_start + jnp.arange(key_count, dtype=jnp.int32)
    query_place = query_start + jnp.arange(row_count, dtype=jnp.int32)
    allowed = (key_place[None, :] >= 0) & (key_place[None, :] <= query_place[:, None])

    def head_group(group_index):
        column = group_index * block_width
        queries = lax.dynamic_slice_in_dim(query_rows, column, block_width, 1).reshape(
            row_count, heads_block, HEAD_DIM
        )
        key_heads = lax.dynamic_slice_in_dim(key_rows, column, block_width, 1).reshape(
            key_count, heads_block, HEAD_DIM
        )
        value_heads = lax.dynamic_slice_in_dim(value_rows, column, block_width, 1).reshape(
            key_count, heads_block, HEAD_DIM
        )
        scores = jnp.einsum(
            "thd,shd->hts", queries, key_heads, preferred_element_type=jnp.float32
        ) * (1.0 / math.sqrt(HEAD_DIM))
        scores = jnp.where(allowed[None], scores, -jnp.inf)
        row_max = jnp.max(scores, axis=2, keepdims=True)
        weights = jnp.exp(scores - row_max)
        denominator = jnp.sum(weights, axis=2)
        mixed = jnp.einsum(
            "hts,shd->thd",
            weights.astype(jnp.bfloat16),
            value_heads,
            preferred_element_type=jnp.float32,
        )
        output = (
            (mixed / jnp.transpose(denominator)[:, :, None])
            .reshape(row_count, block_width)
            .astype(jnp.bfloat16)
        )
        return (output, row_max[:, :, 0] + jnp.log(denominator))

    outputs, log_total = lax.map(head_group, jnp.arange(head_count // heads_block, dtype=jnp.int32))
    attn_out = jnp.moveaxis(outputs, 0, 1).reshape(row_count, head_count * HEAD_DIM)
    return (attn_out, log_total.reshape(head_count, row_count))


def shards(att_query, att_key, att_value):
    row_count = att_query.shape[0]
    fetched = []
    for distance in range(1, KV_STEPS):
        source = fetched[-1] if fetched else (att_key, att_value)
        arrived = from_behind((source[0], source[1]), "ctx", 1)
        fetched.append(arrived)
    key_rows = jnp.concatenate([received[0] for received in fetched[::-1]] + [att_key], axis=0)
    value_rows = jnp.concatenate([received[1] for received in fetched[::-1]] + [att_value], axis=0)
    block_index = lax.axis_index("ctx")
    attn_out, attn_lse = attend(
        att_query,
        key_rows,
        value_rows,
        (block_index - (KV_STEPS - 1)) * row_count,
        block_index * row_count,
    )
    return (attn_out, attn_lse)


def solution(mesh):
    return jax.shard_map(
        shards,
        mesh=mesh,
        in_specs=(P(("dp", "ctx"), None), P(("dp", "ctx"), None), P(("dp", "ctx"), None)),
        out_specs=(P(("dp", "ctx"), None), P(None, ("dp", "ctx"))),
        check_vma=False,
    )
```

profile of v0, /device:TPU:56, one launch (start us, length us, event | category | flops | bytes accessed | tf_op | source)
XLA Modules:
  0.0 139.0 jit_solution(11220283091633116159)
XLA Ops:
  0.6 1.6 %copy.12 = bf16[128,4096]{0,1:T(8,128)(2,1)S(1)} copy(bf16[128,4096]{1,0:T(8,128)(2,1)} %param.6) | data formatting | bytes 2097152 | tf_op args[1]
  2.3 3.4 %collective-permute-start.2 = (bf16[128,4096]{0,1:T(8,128)(2,1)S(1)}, bf16[128,4096]{0,1:T(8,128)(2,1)}, u32[]{:S(2)}, u32[]{:S(2)}) collective-permute-start(bf16[128,4096]{0,1:T(8,128)(2,1)S(1)} %copy.12), channel_id=1, source_target_pairs={{0,4},{4,8},{8,12},{12,16},{16,20},{20,24},{24,28},{28,32},{32,36}... | collective-permute-start | bytes 3145736 | tf_op jit(solution)/shard_map/ppermute | solution.py:15
  5.7 1.6 %copy.10 = bf16[128,4096]{0,1:T(8,128)(2,1)S(1)} copy(bf16[128,4096]{1,0:T(8,128)(2,1)} %param.7) | data formatting | bytes 2097152 | tf_op args[2]
  7.3 3.4 %collective-permute-start = (bf16[128,4096]{0,1:T(8,128)(2,1)S(1)}, bf16[128,4096]{0,1:T(8,128)(2,1)}, u32[]{:S(2)}, u32[]{:S(2)}) collective-permute-start(bf16[128,4096]{0,1:T(8,128)(2,1)S(1)} %copy.10), channel_id=1, source_target_pairs={{0,4},{4,8},{8,12},{12,16},{16,20},{20,24},{24,28},{28,32},{32,36}... | collective-permute-start | bytes 3145736 | tf_op jit(solution)/shard_map/ppermute | solution.py:15
  10.7 31.3 %collective-permute-done.2 = bf16[128,4096]{0,1:T(8,128)(2,1)} collective-permute-done((bf16[128,4096]{0,1:T(8,128)(2,1)S(1)}, bf16[128,4096]{0,1:T(8,128)(2,1)}, u32[]{:S(2)}, u32[]{:S(2)}) %collective-permute-start.2) | collective-permute-done | bytes 1048608 | tf_op jit(solution)/shard_map/ppermute | solution.py:15
  42.0 1.9 %collective-permute-start.3 = (bf16[128,4096]{0,1:T(8,128)(2,1)}, bf16[128,4096]{0,1:T(8,128)(2,1)}, u32[]{:S(2)}, u32[]{:S(2)}) collective-permute-start(bf16[128,4096]{0,1:T(8,128)(2,1)} %collective-permute-done.2), channel_id=1, source_target_pairs={{0,4},{4,8},{8,12},{12,16},{16,20},{20,24},{24,28},{28,32},{32,36}... | collective-permute-start | bytes 3145736 | tf_op jit(solution)/shard_map/ppermute | solution.py:15
  44.0 20.6 %collective-permute-done = bf16[128,4096]{0,1:T(8,128)(2,1)} collective-permute-done((bf16[128,4096]{0,1:T(8,128)(2,1)S(1)}, bf16[128,4096]{0,1:T(8,128)(2,1)}, u32[]{:S(2)}, u32[]{:S(2)}) %collective-permute-start) | collective-permute-done | bytes 1048608 | tf_op jit(solution)/shard_map/ppermute | solution.py:15
  64.5 1.9 %collective-permute-start.1 = (bf16[128,4096]{0,1:T(8,128)(2,1)}, bf16[128,4096]{0,1:T(8,128)(2,1)}, u32[]{:S(2)}, u32[]{:S(2)}) collective-permute-start(bf16[128,4096]{0,1:T(8,128)(2,1)} %collective-permute-done), channel_id=1, source_target_pairs={{0,4},{4,8},{8,12},{12,16},{16,20},{20,24},{24,28},{28,32},{32,36}... | collective-permute-start | bytes 3145736 | tf_op jit(solution)/shard_map/ppermute | solution.py:15
  66.5 20.5 %collective-permute-done.3 = bf16[128,4096]{0,1:T(8,128)(2,1)} collective-permute-done((bf16[128,4096]{0,1:T(8,128)(2,1)}, bf16[128,4096]{0,1:T(8,128)(2,1)}, u32[]{:S(2)}, u32[]{:S(2)}) %collective-permute-start.3) | collective-permute-done | bytes 1048608 | tf_op jit(solution)/shard_map/ppermute | solution.py:15
  87.0 3.6 %pad_maximum_fusion.1 = bf16[384,4096]{0,1:T(8,128)(2,1)} fusion(bf16[128,4096]{0,1:T(8,128)(2,1)S(1)} %copy.12, bf16[128,4096]{0,1:T(8,128)(2,1)} %collective-permute-done.2, bf16[128,4096]{0,1:T(8,128)(2,1)} %collective-permute-done.3), kind=kLoop, calls=%fused_computation.16 | loop fusion | flops 9437184 | bytes 6291456 | tf_op jit(solution)/shard_map/concatenate | solution.py:71
  90.6 18.0 %collective-permute-done.1 = bf16[128,4096]{0,1:T(8,128)(2,1)} collective-permute-done((bf16[128,4096]{0,1:T(8,128)(2,1)}, bf16[128,4096]{0,1:T(8,128)(2,1)}, u32[]{:S(2)}, u32[]{:S(2)}) %collective-permute-start.1) | collective-permute-done | bytes 1048608 | tf_op jit(solution)/shard_map/ppermute | solution.py:15
  108.6 3.6 %pad_maximum_fusion = bf16[384,4096]{0,1:T(8,128)(2,1)} fusion(bf16[128,4096]{0,1:T(8,128)(2,1)S(1)} %copy.10, bf16[128,4096]{0,1:T(8,128)(2,1)} %collective-permute-done, bf16[128,4096]{0,1:T(8,128)(2,1)} %collective-permute-done.1), kind=kLoop, calls=%fused_computation.15 | loop fusion | flops 9437184 | bytes 6291456 | tf_op jit(solution)/shard_map/concatenate | solution.py:72
  112.3 25.4 %while.13 = (s32[]{:T(128)}, bf16[4,128,1024]{1,2,0:T(8,128)(2,1)S(1)}, f32[4,8,128]{2,1,0:T(8,128)}, s32[4]{0:T(128)S(1)}, bf16[384,4096]{0,1:T(8,128)(2,1)}, /...) while((s32[]{:T(128)}, ...), condition=%wide.region_3.4_spmd.clone, body=%wide.region_0.3_spmd.clone.sunk | while | flops 204438528 | bytes 11668555 | solution.py:59
  112.3 0.6 dynamic_slice.25
  113.6 1.5 %constant_dynamic-slice_fusion.5 = (bf16[384,1024]{0,1:T(8,128)(2,1)S(1)}, bf16[384,1024]{0,1:T(8,128)(2,1)S(1)}) fusion(bf16[384,4096]{0,1:T(8,128)(2,1)} %get-tuple-element.209, s32[]{:T(128)S(6)} %select_n.13, bf16[384,4096]{0,1:T(8,128)(2,1)} %get-tuple-element.207), kind=kLoop, calls=%fused_computation.12.clone.1 | loop fusion | bytes 3145732 | tf_op jit(solution)/shard_map/while/body/eval_jaxpr/dynamic_slice | solution.py:33
  115.1 1.0 constant_dynamic-slice_fusion.6
  117.4 0.6 bitcast_dynamic-update-slice_fusion.2
  118.0 0.5 fusion.25
  118.6 0.7 dynamic_slice.25
  119.9 1.5 %constant_dynamic-slice_fusion.5 = (bf16[384,1024]{0,1:T(8,128)(2,1)S(1)}, bf16[384,1024]{0,1:T(8,128)(2,1)S(1)}) fusion(bf16[384,4096]{0,1:T(8,128)(2,1)} %get-tuple-element.209, s32[]{:T(128)S(6)} %select_n.13, bf16[384,4096]{0,1:T(8,128)(2,1)} %get-tuple-element.207), kind=kLoop, calls=%fused_computation.12.clone.1 | loop fusion | bytes 3145732 | tf_op jit(solution)/shard_map/while/body/eval_jaxpr/dynamic_slice | solution.py:33
  121.4 1.0 constant_dynamic-slice_fusion.6
  123.7 0.6 bitcast_dynamic-update-slice_fusion.2
  124.3 0.5 fusion.25
  125.0 0.7 dynamic_slice.25
  126.3 1.5 %constant_dynamic-slice_fusion.5 = (bf16[384,1024]{0,1:T(8,128)(2,1)S(1)}, bf16[384,1024]{0,1:T(8,128)(2,1)S(1)}) fusion(bf16[384,4096]{0,1:T(8,128)(2,1)} %get-tuple-element.209, s32[]{:T(128)S(6)} %select_n.13, bf16[384,4096]{0,1:T(8,128)(2,1)} %get-tuple-element.207), kind=kLoop, calls=%fused_computation.12.clone.1 | loop fusion | bytes 3145732 | tf_op jit(solution)/shard_map/while/body/eval_jaxpr/dynamic_slice | solution.py:33
  127.8 1.0 constant_dynamic-slice_fusion.6
  130.1 0.6 bitcast_dynamic-update-slice_fusion.2
  131.3 0.7 dynamic_slice.25
  132.6 1.5 %constant_dynamic-slice_fusion.5 = (bf16[384,1024]{0,1:T(8,128)(2,1)S(1)}, bf16[384,1024]{0,1:T(8,128)(2,1)S(1)}) fusion(bf16[384,4096]{0,1:T(8,128)(2,1)} %get-tuple-element.209, s32[]{:T(128)S(6)} %select_n.13, bf16[384,4096]{0,1:T(8,128)(2,1)} %get-tuple-element.207), kind=kLoop, calls=%fused_computation.12.clone.1 | loop fusion | bytes 3145732 | tf_op jit(solution)/shard_map/while/body/eval_jaxpr/dynamic_slice | solution.py:33
  134.1 1.0 constant_dynamic-slice_fusion.6
  136.4 0.6 bitcast_dynamic-update-slice_fusion.2
  137.7 1.3 copy.18
  (28 shorter events, 6.5 us)
Async XLA Ops:
  2.3 39.8 %collective-permute-start.2 = (bf16[128,4096]{0,1:T(8,128)(2,1)S(1)}, bf16[128,4096]{0,1:T(8,128)(2,1)}, u32[]{:S(2)}, u32[]{:S(2)}) collective-permute-start(bf16[128,4096]{0,1:T(8,128)(2,1)S(1)} %copy.12), channel_id=1, source_target_pairs={{0,4},{4,8},{8,12},{12,16},{16,20},{20,24},{24,28},{28,32},{32,36}... | collective-permute-start | bytes 3145736 | tf_op jit(solution)/shard_map/ppermute | solution.py:15
  7.3 57.2 %collective-permute-start = (bf16[128,4096]{0,1:T(8,128)(2,1)S(1)}, bf16[128,4096]{0,1:T(8,128)(2,1)}, u32[]{:S(2)}, u32[]{:S(2)}) collective-permute-start(bf16[128,4096]{0,1:T(8,128)(2,1)S(1)} %copy.10), channel_id=1, source_target_pairs={{0,4},{4,8},{8,12},{12,16},{16,20},{20,24},{24,28},{28,32},{32,36}... | collective-permute-start | bytes 3145736 | tf_op jit(solution)/shard_map/ppermute | solution.py:15
  42.0 44.9 %collective-permute-start.3 = (bf16[128,4096]{0,1:T(8,128)(2,1)}, bf16[128,4096]{0,1:T(8,128)(2,1)}, u32[]{:S(2)}, u32[]{:S(2)}) collective-permute-start(bf16[128,4096]{0,1:T(8,128)(2,1)} %collective-permute-done.2), channel_id=1, source_target_pairs={{0,4},{4,8},{8,12},{12,16},{16,20},{20,24},{24,28},{28,32},{32,36}... | collective-permute-start | bytes 3145736 | tf_op jit(solution)/shard_map/ppermute | solution.py:15
  64.5 44.1 %collective-permute-start.1 = (bf16[128,4096]{0,1:T(8,128)(2,1)}, bf16[128,4096]{0,1:T(8,128)(2,1)}, u32[]{:S(2)}, u32[]{:S(2)}) collective-permute-start(bf16[128,4096]{0,1:T(8,128)(2,1)} %collective-permute-done), channel_id=1, source_target_pairs={{0,4},{4,8},{8,12},{12,16},{16,20},{20,24},{24,28},{28,32},{32,36}... | collective-permute-start | bytes 3145736 | tf_op jit(solution)/shard_map/ppermute | solution.py:15
where the time goes:
time: 140 us; the launch traced here: 139 us
  waiting for transfers between devices  90.4 us (65%)
  local copies, waits for them, and re-layouts  18 us (13%)
  other arithmetic  12.2 us (9%)
  starting transfers between devices  10.6 us (8%)
  matrix products  4.19 us (3%)
  loops' own time  2.77 us (2%)
    ppermute x4, waiting for transfers between devices, from_behind(): return lax.ppermute(block, axis, route)  90.4 us
    ppermute x4, starting transfers between devices, from_behind(): return lax.ppermute(block, axis, route)  10.6 us
    dynamic_slice x4, local copies, waits for them, and re-layouts, head_group(): lax.dynamic_slice_in_dim(key_rows, column, block_width, 1)  6.15 us
    dynamic_slice x8, local copies, waits for them, and re-layouts, head_group(): lax.dynamic_slice_in_dim(query_rows, column, block_width, 1)  4.57 us
    concatenate x1, other arithmetic, shards(): jnp.concatenate([received[1] for received in fetched[::-1]] + [att_value]...  3.63 us
    concatenate x1, other arithmetic, shards(): jnp.concatenate([received[0] for received in fetched[::-1]] + [att_key],...  3.6 us
    unnamed x2, local copies, waits for them, and re-layouts  3.23 us
  transfers between devices with their start and end apart: 4, of which 4 were waited for; matrix products, arithmetic and copies ran while one was open for 4% of the time, Pallas kernels for 0%

commit v1 on v0

v1 whole, which is shorter than its diff:
```python
import math

import jax
import jax.numpy as jnp
from jax import lax
from jax.experimental import pallas as pl
from jax.experimental.pallas import tpu as pltpu
from jax.sharding import PartitionSpec as P

HEAD_DIM = 128
KV_STEPS = 3
HEADS_PER_STEP = 8


def from_behind(block, axis, distance):
    devices = range(lax.axis_size(axis))
    route = [(i - distance, i) for i in devices if i - distance in devices]
    return lax.ppermute(block, axis, route)


def attention_kernel(block_ref, q_ref, k0_ref, k1_ref, k2_ref, v0_ref, v1_ref, v2_ref, out_ref, lse_ref):
    block_index = block_ref[0]
    rows = q_ref.shape[0]
    scale = 1.0 / math.sqrt(HEAD_DIM)
    row_id = lax.broadcasted_iota(jnp.int32, (rows, rows), 0)
    col_id = lax.broadcasted_iota(jnp.int32, (rows, rows), 1)
    causal = col_id <= row_id
    diagonal = col_id == row_id
    has_prev = block_index >= 1
    has_prev2 = block_index >= 2
    dims = (((1,), (1,)), ((), ()))
    for h in range(HEADS_PER_STEP):
        cols = slice(h * HEAD_DIM, (h + 1) * HEAD_DIM)
        q = q_ref[:, cols]
        s0 = lax.dot_general(q, k0_ref[:, cols], dims, preferred_element_type=jnp.float32) * scale
        s1 = lax.dot_general(q, k1_ref[:, cols], dims, preferred_element_type=jnp.float32) * scale
        s2 = lax.dot_general(q, k2_ref[:, cols], dims, preferred_element_type=jnp.float32) * scale
        s0 = jnp.where(has_prev2, s0, -jnp.inf)
        s1 = jnp.where(has_prev, s1, -jnp.inf)
        s2 = jnp.where(causal, s2, -jnp.inf)
        m = jnp.maximum(
            jnp.maximum(jnp.max(s0, axis=1, keepdims=True), jnp.max(s1, axis=1, keepdims=True)),
            jnp.max(s2, axis=1, keepdims=True),
        )
        p0 = jnp.exp(s0 - m)
        p1 = jnp.exp(s1 - m)
        p2 = jnp.exp(s2 - m)
        total = (
            jnp.sum(p0, axis=1, keepdims=True)
            + jnp.sum(p1, axis=1, keepdims=True)
            + jnp.sum(p2, axis=1, keepdims=True)
        )
        mixed = (
            jnp.dot(p0.astype(jnp.bfloat16), v0_ref[:, cols], preferred_element_type=jnp.float32)
            + jnp.dot(p1.astype(jnp.bfloat16), v1_ref[:, cols], preferred_element_type=jnp.float32)
            + jnp.dot(p2.astype(jnp.bfloat16), v2_ref[:, cols], preferred_element_type=jnp.float32)
        )
        out_ref[:, cols] = (mixed / total).astype(out_ref.dtype)
        lse_col = m + jnp.log(total)
        lse_ref[h : h + 1, :] = jnp.sum(jnp.where(diagonal, lse_col, 0.0), axis=0, keepdims=True)


def attend(block_index, query_rows, keys, values):
    rows, width = query_rows.shape
    head_count = width // HEAD_DIM
    step_width = HEADS_PER_STEP * HEAD_DIM
    steps = head_count // HEADS_PER_STEP
    block = pl.BlockSpec((rows, step_width), lambda g, b: (0, g))
    return pl.pallas_call(
        attention_kernel,
        grid_spec=pltpu.PrefetchScalarGridSpec(
            num_scalar_prefetch=1,
            grid=(steps,),
            in_specs=[block] * 7,
            out_specs=[block, pl.BlockSpec((HEADS_PER_STEP, rows), lambda g, b: (g, 0))],
        ),
        out_shape=[
            jax.ShapeDtypeStruct((rows, width), jnp.bfloat16),
            jax.ShapeDtypeStruct((head_count, rows), jnp.float32),
        ],
    )(block_index, query_rows, *keys, *values)


def shards(att_query, att_key, att_value):
    fetched = []
    for distance in range(1, KV_STEPS):
        source = fetched[-1] if fetched else (att_key, att_value)
        arrived = from_behind((source[0], source[1]), "ctx", 1)
        fetched.append(arrived)
    keys = [received[0] for received in fetched[::-1]] + [att_key]
    values = [received[1] for received in fetched[::-1]] + [att_value]
    block_index = lax.axis_index("ctx").astype(jnp.int32).reshape(1)
    return attend(block_index, att_query, keys, values)


def solution(mesh):
    return jax.shard_map(
        shards,
        mesh=mesh,
        in_specs=(P(("dp", "ctx"), None), P(("dp", "ctx"), None), P(("dp", "ctx"), None)),
        out_specs=(P(("dp", "ctx"), None), P(None, ("dp", "ctx"))),
        check_vma=False,
    )
```

time: 140 us -> 119 us (0.85)
  local copies, waits for them, and re-layouts: 18 us -> 0.01 us
  other arithmetic: 12.2 us -> 0 us
  Pallas kernels: 0 us -> 12.1 us
  waiting for transfers between devices: 90.4 us -> 95.9 us
  matrix products: 4.19 us -> 0 us
  loops' own time: 2.77 us -> 0 us
    dynamic_slice x16 -> x0, local copies, waits for them, and re-layouts: 13.3 us -> none  [the longest x4 6.15 us: head_group(): lax.dynamic_slice_in_dim(key_rows, column, block_width, 1)]
    pallas_call x0 -> x1, Pallas kernels: none -> 12.1 us  [attend(): pl.pallas_call(attention_kernel, grid_spec=pltpu.PrefetchScalarGridSpec(n...]
    concatenate x2 -> x0, other arithmetic: 7.24 us -> none  [the longest x1 3.63 us: shards(): jnp.concatenate([received[1] for received in fetched[::-1]] + [att_value]...]
    ppermute x4, waiting for transfers between devices: 90.4 us -> 95.9 us  [from_behind(): return lax.ppermute(block, axis, route)]
    dot_general x8 -> x0, matrix products: 4.19 us -> none  [the longest x4 2.18 us: head_group(): jnp.einsum('hts,shd->thd', weights.astype(jnp.bfloat16), value_heads, pre...]
    unnamed x2 -> x6, local copies, waits for them, and re-layouts: 3.23 us -> 0.01 us
    another operation x1 -> x0, loops' own time: 2.77 us -> none  [attend(): lax.map(head_group, jnp.arange(head_count // heads_block, dtype=jnp.int32))]
    dynamic_update_slice x4 -> x0, other arithmetic: 2.43 us -> none  [attend(): lax.map(head_group, jnp.arange(head_count // heads_block, dtype=jnp.int32))]
  transfers between devices with their start and end apart: 4 -> 4, of which waited for: 4 -> 4; matrix products, arithmetic and copies ran while one was open for 4% -> 0% of each run, Pallas kernels for 0% -> 0%
where the time goes in v1:
time: 119 us
  waiting for transfers between devices  95.9 us (81%)
  Pallas kernels  12.1 us (10%)
  starting transfers between devices  10.6 us (9%)
    ppermute x4, waiting for transfers between devices, from_behind(): return lax.ppermute(block, axis, route)  95.9 us
    pallas_call x1, Pallas kernels, attend(): pl.pallas_call(attention_kernel, grid_spec=pltpu.PrefetchScalarGridSpec(n...  12.1 us
    ppermute x4, starting transfers between devices, from_behind(): return lax.ppermute(block, axis, route)  10.6 us
  transfers between devices with their start and end apart: 4, of which 4 were waited for; matrix products, arithmetic and copies ran while one was open for 0% of the time, Pallas kernels for 0%

profile of v1, /device:TPU:56, one launch (start us, length us, event | category | flops | bytes accessed | tf_op | source)
XLA Modules:
  0.0 119.3 jit_solution(4024128295355557304)
XLA Ops:
  0.6 3.4 %collective-permute-start = (bf16[128,4096]{1,0:T(8,128)(2,1)}, bf16[128,4096]{1,0:T(8,128)(2,1)S(1)}, u32[]{:S(2)}, u32[]{:S(2)}) collective-permute-start(bf16[128,4096]{1,0:T(8,128)(2,1)} %k2_ref.1), channel_id=1, source_target_pairs={{0,4},{4,8},{8,12},{12,16},{16,20},{20,24},{24,28},{28,32},{32,36}... | collective-permute-start | bytes 3145736 | tf_op jit(solution)/shard_map/ppermute | solution.py:18
  4.0 3.4 %collective-permute-start.2 = (bf16[128,4096]{1,0:T(8,128)(2,1)}, bf16[128,4096]{1,0:T(8,128)(2,1)S(1)}, u32[]{:S(2)}, u32[]{:S(2)}) collective-permute-start(bf16[128,4096]{1,0:T(8,128)(2,1)} %v2_ref.1), channel_id=1, source_target_pairs={{0,4},{4,8},{8,12},{12,16},{16,20},{20,24},{24,28},{28,32},{32,36}... | collective-permute-start | bytes 3145736 | tf_op jit(solution)/shard_map/ppermute | solution.py:18
  7.4 33.1 %collective-permute-done.k1_ref = bf16[128,4096]{1,0:T(8,128)(2,1)S(1)} collective-permute-done((bf16[128,4096]{1,0:T(8,128)(2,1)}, bf16[128,4096]{1,0:T(8,128)(2,1)S(1)}, u32[]{:S(2)}, u32[]{:S(2)}) %collective-permute-start) | collective-permute-done | bytes 1048608 | tf_op jit(solution)/shard_map/ppermute | solution.py:18
  40.5 0.0 copy-start
  40.5 1.9 %collective-permute-start.1 = (bf16[128,4096]{1,0:T(8,128)(2,1)S(1)}, bf16[128,4096]{1,0:T(8,128)(2,1)S(1)}, u32[]{:S(2)}, u32[]{:S(2)}) collective-permute-start(bf16[128,4096]{1,0:T(8,128)(2,1)S(1)} %collective-permute-done.k1_ref), channel_id=1, source_target_pairs={{0,4},{4,8},{8,12},{12,16},{16,20},{20,24},{24,28},{28,32},{32,36}... | collective-permute-start | bytes 3145736 | tf_op jit(solution)/shard_map/ppermute | solution.py:18
  42.4 20.6 %collective-permute-done.2.v1_ref = bf16[128,4096]{1,0:T(8,128)(2,1)S(1)} collective-permute-done((bf16[128,4096]{1,0:T(8,128)(2,1)}, bf16[128,4096]{1,0:T(8,128)(2,1)S(1)}, u32[]{:S(2)}, u32[]{:S(2)}) %collective-permute-start.2) | collective-permute-done | bytes 1048608 | tf_op jit(solution)/shard_map/ppermute | solution.py:18
  63.0 0.0 copy-start.1
  63.0 1.9 %collective-permute-start.3 = (bf16[128,4096]{1,0:T(8,128)(2,1)S(1)}, bf16[128,4096]{1,0:T(8,128)(2,1)}, u32[]{:S(2)}, u32[]{:S(2)}) collective-permute-start(bf16[128,4096]{1,0:T(8,128)(2,1)S(1)} %collective-permute-done.2.v1_ref), channel_id=1, source_target_pairs={{0,4},{4,8},{8,12},{12,16},{16,20},{20,24},{24,28},{28,32},{32,36}... | collective-permute-start | bytes 3145736 | tf_op jit(solution)/shard_map/ppermute | solution.py:18
  64.9 20.5 %collective-permute-done.1.k0_ref = bf16[128,4096]{1,0:T(8,128)(2,1)S(1)} collective-permute-done((bf16[128,4096]{1,0:T(8,128)(2,1)S(1)}, bf16[128,4096]{1,0:T(8,128)(2,1)S(1)}, u32[]{:S(2)}, u32[]{:S(2)}) %collective-permute-start.1) | collective-permute-done | bytes 1048608 | tf_op jit(solution)/shard_map/ppermute | solution.py:18
  85.5 0.0 copy-start.2
  85.5 21.7 %collective-permute-done.3.v0_ref = bf16[128,4096]{1,0:T(8,128)(2,1)} collective-permute-done((bf16[128,4096]{1,0:T(8,128)(2,1)S(1)}, bf16[128,4096]{1,0:T(8,128)(2,1)}, u32[]{:S(2)}, u32[]{:S(2)}) %collective-permute-start.3) | collective-permute-done | bytes 1048608 | tf_op jit(solution)/shard_map/ppermute | solution.py:18
  107.2 0.0 copy-done
  107.2 0.0 copy-done.1
  107.2 0.0 copy-done.2
  107.2 12.1 %shard_map.50 = (bf16[128,4096]{1,0:T(8,128)(2,1)}, f32[32,128]{1,0:T(8,128)}) custom-call(s32[1]{0:T(128)} %bitcast.block_ref, bf16[128,4096]{1,0:T(8,128)(2,1)} %q_ref.1, bf16[128,4096]{1,0:T(8,128)(2,1)} %copy-done.2, bf16[128,4096]{1,0:T(8,128)(2,1)} %copy-done, bf16[128,4096]{1,0:T(8,128)(2,1)} %k2_ref.1, ...), custom_call_target="tpu_custom_call" | custom-call | tf_op jit(solution)/shard_map/pallas_call | solution.py:69
Async XLA Ops:
  0.6 39.9 %collective-permute-start = (bf16[128,4096]{1,0:T(8,128)(2,1)}, bf16[128,4096]{1,0:T(8,128)(2,1)S(1)}, u32[]{:S(2)}, u32[]{:S(2)}) collective-permute-start(bf16[128,4096]{1,0:T(8,128)(2,1)} %k2_ref.1), channel_id=1, source_target_pairs={{0,4},{4,8},{8,12},{12,16},{16,20},{20,24},{24,28},{28,32},{32,36}... | collective-permute-start | bytes 3145736 | tf_op jit(solution)/shard_map/ppermute | solution.py:18
  4.0 59.0 %collective-permute-start.2 = (bf16[128,4096]{1,0:T(8,128)(2,1)}, bf16[128,4096]{1,0:T(8,128)(2,1)S(1)}, u32[]{:S(2)}, u32[]{:S(2)}) collective-permute-start(bf16[128,4096]{1,0:T(8,128)(2,1)} %v2_ref.1), channel_id=1, source_target_pairs={{0,4},{4,8},{8,12},{12,16},{16,20},{20,24},{24,28},{28,32},{32,36}... | collective-permute-start | bytes 3145736 | tf_op jit(solution)/shard_map/ppermute | solution.py:18
  40.5 66.7 %copy-start = (bf16[128,4096]{1,0:T(8,128)(2,1)}, bf16[128,4096]{1,0:T(8,128)(2,1)S(1)}, u32[]{:S(2)}) copy-start(bf16[128,4096]{1,0:T(8,128)(2,1)S(1)} %collective-permute-done.k1_ref) | copy-start | bytes 3145732
  40.5 44.9 %collective-permute-start.1 = (bf16[128,4096]{1,0:T(8,128)(2,1)S(1)}, bf16[128,4096]{1,0:T(8,128)(2,1)S(1)}, u32[]{:S(2)}, u32[]{:S(2)}) collective-permute-start(bf16[128,4096]{1,0:T(8,128)(2,1)S(1)} %collective-permute-done.k1_ref), channel_id=1, source_target_pairs={{0,4},{4,8},{8,12},{12,16},{16,20},{20,24},{24,28},{28,32},{32,36}... | collective-permute-start | bytes 3145736 | tf_op jit(solution)/shard_map/ppermute | solution.py:18
  63.0 44.2 %copy-start.1 = (bf16[128,4096]{1,0:T(8,128)(2,1)}, bf16[128,4096]{1,0:T(8,128)(2,1)S(1)}, u32[]{:S(2)}) copy-start(bf16[128,4096]{1,0:T(8,128)(2,1)S(1)} %collective-permute-done.2.v1_ref) | copy-start | bytes 3145732
  63.0 44.2 %collective-permute-start.3 = (bf16[128,4096]{1,0:T(8,128)(2,1)S(1)}, bf16[128,4096]{1,0:T(8,128)(2,1)}, u32[]{:S(2)}, u32[]{:S(2)}) collective-permute-start(bf16[128,4096]{1,0:T(8,128)(2,1)S(1)} %collective-permute-done.2.v1_ref), channel_id=1, source_target_pairs={{0,4},{4,8},{8,12},{12,16},{16,20},{20,24},{24,28},{28,32},{32,36}... | collective-permute-start | bytes 3145736 | tf_op jit(solution)/shard_map/ppermute | solution.py:18
  85.5 21.8 %copy-start.2 = (bf16[128,4096]{1,0:T(8,128)(2,1)}, bf16[128,4096]{1,0:T(8,128)(2,1)S(1)}, u32[]{:S(2)}) copy-start(bf16[128,4096]{1,0:T(8,128)(2,1)S(1)} %collective-permute-done.1.k0_ref) | copy-start | bytes 3145732

commit v2 on v1

v2 whole, which is shorter than its diff:
```python
import math

import jax
import jax.numpy as jnp
from jax import lax
from jax.experimental import pallas as pl
from jax.experimental.pallas import tpu as pltpu
from jax.sharding import PartitionSpec as P

HEAD_DIM = 128
HEADS_PER_STEP = 8
CHUNKS = 2
SCALE = 1.0 / math.sqrt(HEAD_DIM)
NT_DIMS = (((1,), (1,)), ((), ()))


def from_behind(block, axis):
    devices = range(lax.axis_size(axis))
    route = [(i - 1, i) for i in devices if i - 1 in devices]
    return lax.ppermute(block, axis, route)


def from_ahead(block, axis):
    devices = range(lax.axis_size(axis))
    route = [(i + 1, i) for i in devices if i + 1 in devices]
    return lax.ppermute(block, axis, route)


def row_to_column(row, diagonal):
    return jnp.sum(jnp.where(diagonal, row, 0.0), axis=1, keepdims=True)


def column_to_row(column, diagonal):
    return jnp.sum(jnp.where(diagonal, column, 0.0), axis=0, keepdims=True)


def partial_kernel(q_ref, k_ref, v_ref, o_ref, m_ref, l_ref):
    rows = q_ref.shape[0]
    diagonal = lax.broadcasted_iota(jnp.int32, (rows, rows), 0) == lax.broadcasted_iota(
        jnp.int32, (rows, rows), 1
    )
    for h in range(HEADS_PER_STEP):
        cols = slice(h * HEAD_DIM, (h + 1) * HEAD_DIM)
        s = lax.dot_general(q_ref[:, cols], k_ref[:, cols], NT_DIMS, preferred_element_type=jnp.float32) * SCALE
        m = jnp.max(s, axis=1, keepdims=True)
        p = jnp.exp(s - m)
        total = jnp.sum(p, axis=1, keepdims=True)
        mixed = jnp.dot(p.astype(jnp.bfloat16), v_ref[:, cols], preferred_element_type=jnp.float32)
        o_ref[:, cols] = mixed.astype(o_ref.dtype)
        m_ref[h : h + 1, :] = column_to_row(m, diagonal)
        l_ref[h : h + 1, :] = column_to_row(total, diagonal)


def final_kernel(block_ref, q_ref, k_ref, v_ref, kp_ref, vp_ref, o_ref, m_ref, l_ref, *rest):
    out_ref, lse_ref = rest[-2:]
    block_index = block_ref[0]
    rows = q_ref.shape[0]
    row_id = lax.broadcasted_iota(jnp.int32, (rows, rows), 0)
    col_id = lax.broadcasted_iota(jnp.int32, (rows, rows), 1)
    causal = col_id <= row_id
    diagonal = col_id == row_id
    has_prev = block_index >= 1
    has_prev2 = block_index >= 2
    for h in range(HEADS_PER_STEP):
        cols = slice(h * HEAD_DIM, (h + 1) * HEAD_DIM)
        q = q_ref[:, cols]
        s_own = lax.dot_general(q, k_ref[:, cols], NT_DIMS, preferred_element_type=jnp.float32) * SCALE
        s_prev = lax.dot_general(q, kp_ref[:, cols], NT_DIMS, preferred_element_type=jnp.float32) * SCALE
        s_own = jnp.where(causal, s_own, -jnp.inf)
        s_prev = jnp.where(has_prev, s_prev, -jnp.inf)
        m_far = row_to_column(m_ref[h : h + 1, :], diagonal)
        l_far = row_to_column(l_ref[h : h + 1, :], diagonal)
        m_near = jnp.maximum(jnp.max(s_own, axis=1, keepdims=True), jnp.max(s_prev, axis=1, keepdims=True))
        m = jnp.where(has_prev2, jnp.maximum(m_near, m_far), m_near)
        far_scale = jnp.where(has_prev2, jnp.exp(m_far - m), 0.0)
        p_own = jnp.exp(s_own - m)
        p_prev = jnp.exp(s_prev - m)
        total = (
            jnp.sum(p_own, axis=1, keepdims=True)
            + jnp.sum(p_prev, axis=1, keepdims=True)
            + jnp.where(has_prev2, far_scale * l_far, 0.0)
        )
        mixed = (
            jnp.dot(p_own.astype(jnp.bfloat16), v_ref[:, cols], preferred_element_type=jnp.float32)
            + jnp.dot(p_prev.astype(jnp.bfloat16), vp_ref[:, cols], preferred_element_type=jnp.float32)
            + jnp.where(has_prev2, far_scale * o_ref[:, cols].astype(jnp.float32), 0.0)
        )
        out_ref[:, cols] = (mixed / total).astype(out_ref.dtype)
        lse_ref[h : h + 1, :] = column_to_row(m + jnp.log(total), diagonal)


def partial_attention(q, k, v):
    rows, width = q.shape
    step_width = HEADS_PER_STEP * HEAD_DIM
    steps = width // step_width
    block = pl.BlockSpec((rows, step_width), lambda g: (0, g))
    stat = pl.BlockSpec((HEADS_PER_STEP, rows), lambda g: (g, 0))
    return pl.pallas_call(
        partial_kernel,
        grid=(steps,),
        in_specs=[block] * 3,
        out_specs=[block, stat, stat],
        out_shape=[
            jax.ShapeDtypeStruct((rows, width), jnp.bfloat16),
            jax.ShapeDtypeStruct((width // HEAD_DIM, rows), jnp.float32),
            jax.ShapeDtypeStruct((width // HEAD_DIM, rows), jnp.float32),
        ],
    )(q, k, v)


def final_attention(block_index, chunk, q, k, v, k_prev, v_prev, o_far, m_far, l_far, previous):
    rows, width = q.shape
    step_width = HEADS_PER_STEP * HEAD_DIM
    steps = k_prev.shape[1] // step_width
    offset = chunk * steps
    whole = pl.BlockSpec((rows, step_width), lambda g, b: (0, g + offset))
    part = pl.BlockSpec((rows, step_width), lambda g, b: (0, g))
    stat = pl.BlockSpec((HEADS_PER_STEP, rows), lambda g, b: (g, 0))
    out_stat = pl.BlockSpec((HEADS_PER_STEP, rows), lambda g, b: (g + offset, 0))
    operands = [block_index, q, k, v, k_prev, v_prev, o_far, m_far, l_far]
    in_specs = [whole] * 3 + [part] * 3 + [stat] * 2
    aliases = {}
    if previous is not None:
        in_specs = in_specs + [pl.BlockSpec(memory_space=pl.ANY)] * 2
        aliases = {len(operands): 0, len(operands) + 1: 1}
        operands = operands + list(previous)
    return pl.pallas_call(
        final_kernel,
        grid_spec=pltpu.PrefetchScalarGridSpec(
            num_scalar_prefetch=1,
            grid=(steps,),
            in_specs=in_specs,
            out_specs=[whole, out_stat],
        ),
        out_shape=[
            jax.ShapeDtypeStruct((rows, width), jnp.bfloat16),
            jax.ShapeDtypeStruct((width // HEAD_DIM, rows), jnp.float32),
        ],
        input_output_aliases=aliases,
    )(*operands)


def shards(att_query, att_key, att_value):
    width = att_query.shape[1]
    chunk_width = width // CHUNKS
    block_index = lax.axis_index("ctx").astype(jnp.int32).reshape(1)
    arrivals = []
    for chunk in range(CHUNKS):
        cols = slice(chunk * chunk_width, (chunk + 1) * chunk_width)
        k_prev, v_prev = from_behind((att_key[:, cols], att_value[:, cols]), "ctx")
        q_next = from_ahead(att_query[:, cols], "ctx")
        far = partial_attention(q_next, k_prev, v_prev)
        o_far, m_far, l_far = from_behind(far, "ctx")
        arrivals.append((k_prev, v_prev, o_far, m_far, l_far))
    result = None
    for chunk in range(CHUNKS):
        result = final_attention(
            block_index, chunk, att_query, att_key, att_value, *arrivals[chunk], result
        )
    return tuple(result)


def solution(mesh):
    return jax.shard_map(
        shards,
        mesh=mesh,
        in_specs=(P(("dp", "ctx"), None), P(("dp", "ctx"), None), P(("dp", "ctx"), None)),
        out_specs=(P(("dp", "ctx"), None), P(None, ("dp", "ctx"))),
        check_vma=False,
    )
```

time: 119 us -> 130 us (1.092)
  the two profiles are of different devices: /device:TPU:56 before, /device:TPU:32 now
where the time goes in v2:
time: 130 us; the launch traced here: 129 us
  waiting for transfers between devices  49 us (38%)
  starting transfers between devices  47.3 us (36%)
  Pallas kernels  25.1 us (19%)
  local copies, waits for them, and re-layouts  7.15 us (6%)
    ppermute x10, waiting for transfers between devices, from_behind(): return lax.ppermute(block, axis, route)  49 us
    ppermute x2, starting transfers between devices, from_ahead(): return lax.ppermute(block, axis, route)  27.9 us
    ppermute x10, starting transfers between devices, from_behind(): return lax.ppermute(block, axis, route)  19.4 us
    pallas_call x2, Pallas kernels, final_attention(): pl.pallas_call(final_kernel, grid_spec=pltpu.PrefetchScalarGridSpec(num_s...  13.3 us
    pallas_call x2, Pallas kernels, partial_attention(): pl.pallas_call(partial_kernel, grid=(steps,), in_specs=[block] * 3, out_s...  11.8 us
    unnamed x34, local copies, waits for them, and re-layouts  3.2 us
  transfers between devices with their start and end apart: 12, of which 6 were waited for; matrix products, arithmetic and copies ran while one was open for 1% of the time, Pallas kernels for 14%

profile of v2, /device:TPU:32, one launch (start us, length us, event | category | flops | bytes accessed | tf_op | source)
XLA Modules:
  0.0 129.5 jit_solution(13844774815442745053)
XLA Ops:
  0.6 0.0 copy-start
  0.6 2.2 %fusion = (bf16[128,2048]{1,0:T(8,128)(2,1)S(1)}, bf16[128,2048]{1,0:T(8,128)(2,1)}) fusion(bf16[128,4096]{1,0:T(8,128)(2,1)} %q_ref.3), kind=kLoop, calls=%fused_computation | loop fusion | bytes 2097152 | tf_op jit(solution)/shard_map/slice | solution.py:151
  2.8 14.9 %collective-permute-start.8 = (bf16[128,2048]{1,0:T(8,128)(2,1)S(1)}, bf16[128,2048]{1,0:T(8,128)(2,1)S(1)}, u32[]{:S(2)}, u32[]{:S(2)}) collective-permute-start(bf16[128,2048]{1,0:T(8,128)(2,1)S(1)} %get-tuple-element.18), channel_id=1, source_target_pairs={{4,0},{8,4},{12,8},{16,12},{20,16},{24,20},{28,24},{32,28},{36,32}... | collective-permute-start | bytes 1572872 | tf_op jit(solution)/shard_map/ppermute | solution.py:26
  17.8 0.9 fusion.2
  18.6 1.9 %collective-permute-start.6 = (bf16[128,2048]{1,0:T(8,128)(2,1)S(1)}, bf16[128,2048]{1,0:T(8,128)(2,1)S(1)}, u32[]{:S(2)}, u32[]{:S(2)}) collective-permute-start(bf16[128,2048]{1,0:T(8,128)(2,1)S(1)} %get-tuple-element.22), channel_id=1, source_target_pairs={{0,4},{4,8},{8,12},{12,16},{16,20},{20,24},{24,28},{28,32},{32,36}... | collective-permute-start | bytes 1572872 | tf_op jit(solution)/shard_map/ppermute | solution.py:20
  20.6 0.9 fusion.1
  21.5 1.9 %collective-permute-start.7 = (bf16[128,2048]{1,0:T(8,128)(2,1)S(1)}, bf16[128,2048]{1,0:T(8,128)(2,1)S(1)}, u32[]{:S(2)}, u32[]{:S(2)}) collective-permute-start(bf16[128,2048]{1,0:T(8,128)(2,1)S(1)} %get-tuple-element.20), channel_id=1, source_target_pairs={{0,4},{4,8},{8,12},{12,16},{16,20},{20,24},{24,28},{28,32},{32,36}... | collective-permute-start | bytes 1572872 | tf_op jit(solution)/shard_map/ppermute | solution.py:20
  23.4 12.9 %collective-permute-start.2 = (bf16[128,2048]{1,0:T(8,128)(2,1)}, bf16[128,2048]{1,0:T(8,128)(2,1)S(1)}, u32[]{:S(2)}, u32[]{:S(2)}) collective-permute-start(bf16[128,2048]{1,0:T(8,128)(2,1)} %get-tuple-element.19), channel_id=1, source_target_pairs={{4,0},{8,4},{12,8},{16,12},{20,16},{24,20},{28,24},{32,28},{36,32}... | collective-permute-start | bytes 1572872 | tf_op jit(solution)/shard_map/ppermute | solution.py:26
  36.3 1.9 %collective-permute-start = (bf16[128,2048]{1,0:T(8,128)(2,1)}, bf16[128,2048]{1,0:T(8,128)(2,1)S(1)}, u32[]{:S(2)}, u32[]{:S(2)}) collective-permute-start(bf16[128,2048]{1,0:T(8,128)(2,1)} %get-tuple-element.23), channel_id=1, source_target_pairs={{0,4},{4,8},{8,12},{12,16},{16,20},{20,24},{24,28},{28,32},{32,36}... | collective-permute-start | bytes 1572872 | tf_op jit(solution)/shard_map/ppermute | solution.py:20
  38.3 1.9 %collective-permute-start.1 = (bf16[128,2048]{1,0:T(8,128)(2,1)}, bf16[128,2048]{1,0:T(8,128)(2,1)S(1)}, u32[]{:S(2)}, u32[]{:S(2)}) collective-permute-start(bf16[128,2048]{1,0:T(8,128)(2,1)} %get-tuple-element.21), channel_id=1, source_target_pairs={{0,4},{4,8},{8,12},{12,16},{16,20},{20,24},{24,28},{28,32},{32,36}... | collective-permute-start | bytes 1572872 | tf_op jit(solution)/shard_map/ppermute | solution.py:20
  40.2 4.2 %collective-permute-done.6.k_ref.kp_ref = bf16[128,2048]{1,0:T(8,128)(2,1)S(1)} collective-permute-done((bf16[128,2048]{1,0:T(8,128)(2,1)S(1)}, bf16[128,2048]{1,0:T(8,128)(2,1)S(1)}, u32[]{:S(2)}, u32[]{:S(2)}) %collective-permute-start.6) | collective-permute-done | bytes 524320 | tf_op jit(solution)/shard_map/ppermute | solution.py:20
  44.4 11.2 %collective-permute-done.7.v_ref.vp_ref = bf16[128,2048]{1,0:T(8,128)(2,1)S(1)} collective-permute-done((bf16[128,2048]{1,0:T(8,128)(2,1)S(1)}, bf16[128,2048]{1,0:T(8,128)(2,1)S(1)}, u32[]{:S(2)}, u32[]{:S(2)}) %collective-permute-start.7) | collective-permute-done | bytes 524320 | tf_op jit(solution)/shard_map/ppermute | solution.py:20
  55.6 0.8 copy-done.5
  56.4 5.9 %shard_map.51 = (bf16[128,2048]{1,0:T(8,128)(2,1)}, f32[16,128]{1,0:T(8,128)}, f32[16,128]{1,0:T(8,128)}) custom-call(bf16[128,2048]{1,0:T(8,128)(2,1)} %copy-done.9, bf16[128,2048]{1,0:T(8,128)(2,1)} %copy-done.3, bf16[128,2048]{1,0:T(8,128)(2,1)} %copy-done.5), custom_call_target="tpu_custom_call" | custom-call | tf_op jit(solution)/shard_map/pallas_call | solution.py:98
  62.3 2.0 %collective-permute-start.9 = (bf16[128,2048]{1,0:T(8,128)(2,1)}, bf16[128,2048]{1,0:T(8,128)(2,1)S(1)}, u32[]{:S(2)}, u32[]{:S(2)}) collective-permute-start(bf16[128,2048]{1,0:T(8,128)(2,1)} %get-tuple-element.13), channel_id=1, source_target_pairs={{0,4},{4,8},{8,12},{12,16},{16,20},{20,24},{24,28},{28,32},{32,36}... | collective-permute-start | bytes 1572872 | tf_op jit(solution)/shard_map/ppermute | solution.py:20
  64.4 2.5 %collective-permute-done.k_ref.kp_ref = bf16[128,2048]{1,0:T(8,128)(2,1)S(1)} collective-permute-done((bf16[128,2048]{1,0:T(8,128)(2,1)}, bf16[128,2048]{1,0:T(8,128)(2,1)S(1)}, u32[]{:S(2)}, u32[]{:S(2)}) %collective-permute-start) | collective-permute-done | bytes 524320 | tf_op jit(solution)/shard_map/ppermute | solution.py:20
  66.9 11.2 %collective-permute-done.1.v_ref.vp_ref = bf16[128,2048]{1,0:T(8,128)(2,1)S(1)} collective-permute-done((bf16[128,2048]{1,0:T(8,128)(2,1)}, bf16[128,2048]{1,0:T(8,128)(2,1)S(1)}, u32[]{:S(2)}, u32[]{:S(2)}) %collective-permute-start.1) | collective-permute-done | bytes 524320 | tf_op jit(solution)/shard_map/ppermute | solution.py:20
  78.1 0.8 copy-done.4
  78.9 5.9 %shard_map.50 = (bf16[128,2048]{1,0:T(8,128)(2,1)}, f32[16,128]{1,0:T(8,128)}, f32[16,128]{1,0:T(8,128)}) custom-call(bf16[128,2048]{1,0:T(8,128)(2,1)} %copy-done.8, bf16[128,2048]{1,0:T(8,128)(2,1)} %copy-done.2, bf16[128,2048]{1,0:T(8,128)(2,1)} %copy-done.4), custom_call_target="tpu_custom_call" | custom-call | tf_op jit(solution)/shard_map/pallas_call | solution.py:98
  84.8 2.0 %collective-permute-start.3 = (bf16[128,2048]{1,0:T(8,128)(2,1)}, bf16[128,2048]{1,0:T(8,128)(2,1)S(1)}, u32[]{:S(2)}, u32[]{:S(2)}) collective-permute-start(bf16[128,2048]{1,0:T(8,128)(2,1)} %get-tuple-element.10), channel_id=1, source_target_pairs={{0,4},{4,8},{8,12},{12,16},{16,20},{20,24},{24,28},{28,32},{32,36}... | collective-permute-start | bytes 1572872 | tf_op jit(solution)/shard_map/ppermute | solution.py:20
  86.9 1.9 %collective-permute-start.10 = (f32[16,128]{1,0:T(8,128)S(1)}, f32[16,128]{1,0:T(8,128)S(1)}, u32[]{:S(2)}, u32[]{:S(2)}) collective-permute-start(f32[16,128]{1,0:T(8,128)S(1)} %copy-done.16), channel_id=1, source_target_pairs={{0,4},{4,8},{8,12},{12,16},{16,20},{20,24},{24,28},{28,32},{32,36}... | collective-permute-start | bytes 24584 | tf_op jit(solution)/shard_map/ppermute | solution.py:20
  88.8 1.9 %collective-permute-start.11 = (f32[16,128]{1,0:T(8,128)S(1)}, f32[16,128]{1,0:T(8,128)S(1)}, u32[]{:S(2)}, u32[]{:S(2)}) collective-permute-start(f32[16,128]{1,0:T(8,128)S(1)} %copy-done.14), channel_id=1, source_target_pairs={{0,4},{4,8},{8,12},{12,16},{16,20},{20,24},{24,28},{28,32},{32,36}... | collective-permute-start | bytes 24584 | tf_op jit(solution)/shard_map/ppermute | solution.py:20
  90.7 1.9 %collective-permute-start.4 = (f32[16,128]{1,0:T(8,128)}, f32[16,128]{1,0:T(8,128)S(1)}, u32[]{:S(2)}, u32[]{:S(2)}) collective-permute-start(f32[16,128]{1,0:T(8,128)} %get-tuple-element.11), channel_id=1, source_target_pairs={{0,4},{4,8},{8,12},{12,16},{16,20},{20,24},{24,28},{28,32},{32,36}... | collective-permute-start | bytes 24584 | tf_op jit(solution)/shard_map/ppermute | solution.py:20
  92.7 14.8 %collective-permute-done.10.m_ref = f32[16,128]{1,0:T(8,128)S(1)} collective-permute-done((f32[16,128]{1,0:T(8,128)S(1)}, f32[16,128]{1,0:T(8,128)S(1)}, u32[]{:S(2)}, u32[]{:S(2)}) %collective-permute-start.10) | collective-permute-done | bytes 8224 | tf_op jit(solution)/shard_map/ppermute | solution.py:20
  107.4 1.9 %collective-permute-start.5 = (f32[16,128]{1,0:T(8,128)S(1)}, f32[16,128]{1,0:T(8,128)S(1)}, u32[]{:S(2)}, u32[]{:S(2)}) collective-permute-start(f32[16,128]{1,0:T(8,128)S(1)} %copy-done.15), channel_id=1, source_target_pairs={{0,4},{4,8},{8,12},{12,16},{16,20},{20,24},{24,28},{28,32},{32,36}... | collective-permute-start | bytes 24584 | tf_op jit(solution)/shard_map/ppermute | solution.py:20
  109.4 0.6 copy-done.13
  110.0 0.2 copy-done.6
  110.2 6.7 %shard_map.52 = (bf16[128,4096]{1,0:T(8,128)(2,1)}, f32[32,128]{1,0:T(8,128)}) custom-call(s32[1]{0:T(128)} %bitcast.block_ref, bf16[128,4096]{1,0:T(8,128)(2,1)} %q_ref.3, bf16[128,4096]{1,0:T(8,128)(2,1)} %k_ref.3, bf16[128,4096]{1,0:T(8,128)(2,1)} %v_ref.3, bf16[128,2048]{1,0:T(8,128)(2,1)} %copy-done.3, bf16[128,2048]{1,0:T(8,128)(2,1)} %copy-done.5, ...), custom_call_target="tpu_custom_call" | custom-call | tf_op jit(solution)/shard_map/pallas_call | solution.py:127
  116.9 5.1 %collective-permute-done.5.l_ref = f32[16,128]{1,0:T(8,128)S(1)} collective-permute-done((f32[16,128]{1,0:T(8,128)S(1)}, f32[16,128]{1,0:T(8,128)S(1)}, u32[]{:S(2)}, u32[]{:S(2)}) %collective-permute-start.5) | collective-permute-done | bytes 8224 | tf_op jit(solution)/shard_map/ppermute | solution.py:20
  122.0 0.6 copy-done.11
  122.6 0.2 copy-done.7
  122.8 6.7 %shard_map.53 = (bf16[128,4096]{1,0:T(8,128)(2,1)}, f32[32,128]{1,0:T(8,128)}) custom-call(s32[1]{0:T(128)} %bitcast.block_ref, bf16[128,4096]{1,0:T(8,128)(2,1)} %q_ref.3, bf16[128,4096]{1,0:T(8,128)(2,1)} %k_ref.3, bf16[128,4096]{1,0:T(8,128)(2,1)} %v_ref.3, bf16[128,2048]{1,0:T(8,128)(2,1)} %copy-done.2, ...), custom_call_target="tpu_custom_call", output_to_operand_aliasing={{0}: (9, {}), {1}: (10, {})} | custom-call | tf_op jit(solution)/shard_map/pallas_call | solution.py:127
  (33 shorter events, 0.1 us)
Async XLA Ops:
  0.6 17.1 %copy-start = (bf16[128,4096]{1,0:T(8,128)(2,1)S(1)}, bf16[128,4096]{1,0:T(8,128)(2,1)}, u32[]{:S(2)}) copy-start(bf16[128,4096]{1,0:T(8,128)(2,1)} %k_ref.3) | copy-start | bytes 3145732
  2.8 17.7 %copy-start.1 = (bf16[128,4096]{1,0:T(8,128)(2,1)S(1)}, bf16[128,4096]{1,0:T(8,128)(2,1)}, u32[]{:S(2)}) copy-start(bf16[128,4096]{1,0:T(8,128)(2,1)} %v_ref.3) | copy-start | bytes 3145732
  2.8 35.4 %collective-permute-start.8 = (bf16[128,2048]{1,0:T(8,128)(2,1)S(1)}, bf16[128,2048]{1,0:T(8,128)(2,1)S(1)}, u32[]{:S(2)}, u32[]{:S(2)}) collective-permute-start(bf16[128,2048]{1,0:T(8,128)(2,1)S(1)} %get-tuple-element.18), channel_id=1, source_target_pairs={{4,0},{8,4},{12,8},{16,12},{20,16},{24,20},{28,24},{32,28},{36,32}... | collective-permute-start | bytes 1572872 | tf_op jit(solution)/shard_map/ppermute | solution.py:26
  18.6 25.8 %collective-permute-start.6 = (bf16[128,2048]{1,0:T(8,128)(2,1)S(1)}, bf16[128,2048]{1,0:T(8,128)(2,1)S(1)}, u32[]{:S(2)}, u32[]{:S(2)}) collective-permute-start(bf16[128,2048]{1,0:T(8,128)(2,1)S(1)} %get-tuple-element.22), channel_id=1, source_target_pairs={{0,4},{4,8},{8,12},{12,16},{16,20},{20,24},{24,28},{28,32},{32,36}... | collective-permute-start | bytes 1572872 | tf_op jit(solution)/shard_map/ppermute | solution.py:20
  21.5 34.2 %collective-permute-start.7 = (bf16[128,2048]{1,0:T(8,128)(2,1)S(1)}, bf16[128,2048]{1,0:T(8,128)(2,1)S(1)}, u32[]{:S(2)}, u32[]{:S(2)}) collective-permute-start(bf16[128,2048]{1,0:T(8,128)(2,1)S(1)} %get-tuple-element.20), channel_id=1, source_target_pairs={{0,4},{4,8},{8,12},{12,16},{16,20},{20,24},{24,28},{28,32},{32,36}... | collective-permute-start | bytes 1572872 | tf_op jit(solution)/shard_map/ppermute | solution.py:20
  23.4 41.0 %collective-permute-start.2 = (bf16[128,2048]{1,0:T(8,128)(2,1)}, bf16[128,2048]{1,0:T(8,128)(2,1)S(1)}, u32[]{:S(2)}, u32[]{:S(2)}) collective-permute-start(bf16[128,2048]{1,0:T(8,128)(2,1)} %get-tuple-element.19), channel_id=1, source_target_pairs={{4,0},{8,4},{12,8},{16,12},{20,16},{24,20},{28,24},{32,28},{36,32}... | collective-permute-start | bytes 1572872 | tf_op jit(solution)/shard_map/ppermute | solution.py:26
  36.3 30.5 %collective-permute-start = (bf16[128,2048]{1,0:T(8,128)(2,1)}, bf16[128,2048]{1,0:T(8,128)(2,1)S(1)}, u32[]{:S(2)}, u32[]{:S(2)}) collective-permute-start(bf16[128,2048]{1,0:T(8,128)(2,1)} %get-tuple-element.23), channel_id=1, source_target_pairs={{0,4},{4,8},{8,12},{12,16},{16,20},{20,24},{24,28},{28,32},{32,36}... | collective-permute-start | bytes 1572872 | tf_op jit(solution)/shard_map/ppermute | solution.py:20
  38.3 17.4 %copy-start.9 = (bf16[128,2048]{1,0:T(8,128)(2,1)}, bf16[128,2048]{1,0:T(8,128)(2,1)S(1)}, u32[]{:S(2)}) copy-start(bf16[128,2048]{1,0:T(8,128)(2,1)S(1)} %collective-permute-done.8.q_ref) | copy-start | bytes 1572868
  38.3 39.8 %collective-permute-start.1 = (bf16[128,2048]{1,0:T(8,128)(2,1)}, bf16[128,2048]{1,0:T(8,128)(2,1)S(1)}, u32[]{:S(2)}, u32[]{:S(2)}) collective-permute-start(bf16[128,2048]{1,0:T(8,128)(2,1)} %get-tuple-element.21), channel_id=1, source_target_pairs={{0,4},{4,8},{8,12},{12,16},{16,20},{20,24},{24,28},{28,32},{32,36}... | collective-permute-start | bytes 1572872 | tf_op jit(solution)/shard_map/ppermute | solution.py:20
  44.4 11.2 %copy-start.3 = (bf16[128,2048]{1,0:T(8,128)(2,1)}, bf16[128,2048]{1,0:T(8,128)(2,1)S(1)}, u32[]{:S(2)}) copy-start(bf16[128,2048]{1,0:T(8,128)(2,1)S(1)} %collective-permute-done.6.k_ref.kp_ref) | copy-start | bytes 1572868
  55.6 0.8 copy-start.5
  62.3 24.5 %copy-start.16 = (f32[16,128]{1,0:T(8,128)S(1)}, f32[16,128]{1,0:T(8,128)}, u32[]{:S(2)}) copy-start(f32[16,128]{1,0:T(8,128)} %get-tuple-element.14) | copy-start | bytes 24580
  62.3 26.5 %copy-start.14 = (f32[16,128]{1,0:T(8,128)S(1)}, f32[16,128]{1,0:T(8,128)}, u32[]{:S(2)}) copy-start(f32[16,128]{1,0:T(8,128)} %get-tuple-element.15) | copy-start | bytes 24580
  62.3 47.1 %collective-permute-start.9 = (bf16[128,2048]{1,0:T(8,128)(2,1)}, bf16[128,2048]{1,0:T(8,128)(2,1)S(1)}, u32[]{:S(2)}, u32[]{:S(2)}) collective-permute-start(bf16[128,2048]{1,0:T(8,128)(2,1)} %get-tuple-element.13), channel_id=1, source_target_pairs={{0,4},{4,8},{8,12},{12,16},{16,20},{20,24},{24,28},{28,32},{32,36}... | collective-permute-start | bytes 1572872 | tf_op jit(solution)/shard_map/ppermute | solution.py:20
  64.4 13.7 %copy-start.8 = (bf16[128,2048]{1,0:T(8,128)(2,1)}, bf16[128,2048]{1,0:T(8,128)(2,1)S(1)}, u32[]{:S(2)}) copy-start(bf16[128,2048]{1,0:T(8,128)(2,1)S(1)} %collective-permute-done.2.q_ref) | copy-start | bytes 1572868
  66.9 11.2 %copy-start.2 = (bf16[128,2048]{1,0:T(8,128)(2,1)}, bf16[128,2048]{1,0:T(8,128)(2,1)S(1)}, u32[]{:S(2)}) copy-start(bf16[128,2048]{1,0:T(8,128)(2,1)S(1)} %collective-permute-done.k_ref.kp_ref) | copy-start | bytes 1572868
  78.1 0.8 copy-start.4
  84.8 22.6 %copy-start.15 = (f32[16,128]{1,0:T(8,128)S(1)}, f32[16,128]{1,0:T(8,128)}, u32[]{:S(2)}) copy-start(f32[16,128]{1,0:T(8,128)} %get-tuple-element.12) | copy-start | bytes 24580
  84.8 37.2 %collective-permute-start.3 = (bf16[128,2048]{1,0:T(8,128)(2,1)}, bf16[128,2048]{1,0:T(8,128)(2,1)S(1)}, u32[]{:S(2)}, u32[]{:S(2)}) collective-permute-start(bf16[128,2048]{1,0:T(8,128)(2,1)} %get-tuple-element.10), channel_id=1, source_target_pairs={{0,4},{4,8},{8,12},{12,16},{16,20},{20,24},{24,28},{28,32},{32,36}... | collective-permute-start | bytes 1572872 | tf_op jit(solution)/shard_map/ppermute | solution.py:20
  86.9 20.6 %collective-permute-start.10 = (f32[16,128]{1,0:T(8,128)S(1)}, f32[16,128]{1,0:T(8,128)S(1)}, u32[]{:S(2)}, u32[]{:S(2)}) collective-permute-start(f32[16,128]{1,0:T(8,128)S(1)} %copy-done.16), channel_id=1, source_target_pairs={{0,4},{4,8},{8,12},{12,16},{16,20},{20,24},{24,28},{28,32},{32,36}... | collective-permute-start | bytes 24584 | tf_op jit(solution)/shard_map/ppermute | solution.py:20
  88.8 20.6 %collective-permute-start.11 = (f32[16,128]{1,0:T(8,128)S(1)}, f32[16,128]{1,0:T(8,128)S(1)}, u32[]{:S(2)}, u32[]{:S(2)}) collective-permute-start(f32[16,128]{1,0:T(8,128)S(1)} %copy-done.14), channel_id=1, source_target_pairs={{0,4},{4,8},{8,12},{12,16},{16,20},{20,24},{24,28},{28,32},{32,36}... | collective-permute-start | bytes 24584 | tf_op jit(solution)/shard_map/ppermute | solution.py:20
  90.7 26.1 %collective-permute-start.4 = (f32[16,128]{1,0:T(8,128)}, f32[16,128]{1,0:T(8,128)S(1)}, u32[]{:S(2)}, u32[]{:S(2)}) collective-permute-start(f32[16,128]{1,0:T(8,128)} %get-tuple-element.11), channel_id=1, source_target_pairs={{0,4},{4,8},{8,12},{12,16},{16,20},{20,24},{24,28},{28,32},{32,36}... | collective-permute-start | bytes 24584 | tf_op jit(solution)/shard_map/ppermute | solution.py:20
  107.4 2.0 %copy-start.12 = (f32[16,128]{1,0:T(8,128)}, f32[16,128]{1,0:T(8,128)S(1)}, u32[]{:S(2)}) copy-start(f32[16,128]{1,0:T(8,128)S(1)} %collective-permute-done.10.m_ref) | copy-start | bytes 24580
  107.4 14.6 %collective-permute-start.5 = (f32[16,128]{1,0:T(8,128)S(1)}, f32[16,128]{1,0:T(8,128)S(1)}, u32[]{:S(2)}, u32[]{:S(2)}) collective-permute-start(f32[16,128]{1,0:T(8,128)S(1)} %copy-done.15), channel_id=1, source_target_pairs={{0,4},{4,8},{8,12},{12,16},{16,20},{20,24},{24,28},{28,32},{32,36}... | collective-permute-start | bytes 24584 | tf_op jit(solution)/shard_map/ppermute | solution.py:20
  109.4 0.6 copy-start.13
  109.4 0.8 copy-start.6
  116.9 5.2 %copy-start.10 = (f32[16,128]{1,0:T(8,128)}, f32[16,128]{1,0:T(8,128)S(1)}, u32[]{:S(2)}) copy-start(f32[16,128]{1,0:T(8,128)S(1)} %collective-permute-done.4.m_ref) | copy-start | bytes 24580
  122.0 0.6 copy-start.11
  122.0 0.8 copy-start.7

commit v3 on v2

v3 whole, which is shorter than its diff:
```python
import math

import jax
import jax.numpy as jnp
from jax import lax
from jax.experimental import pallas as pl
from jax.experimental.pallas import tpu as pltpu
from jax.sharding import PartitionSpec as P

HEAD_DIM = 128
HEADS_PER_STEP = 8
CHUNKS = 2
SCALE = 1.0 / math.sqrt(HEAD_DIM)
NT_DIMS = (((1,), (1,)), ((), ()))


def from_behind(block, axis):
    devices = range(lax.axis_size(axis))
    route = [(i - 1, i) for i in devices if i - 1 in devices]
    return lax.ppermute(block, axis, route)


def from_ahead(block, axis):
    devices = range(lax.axis_size(axis))
    route = [(i + 1, i) for i in devices if i + 1 in devices]
    return lax.ppermute(block, axis, route)


def scores(q, k):
    return lax.dot_general(q, k, NT_DIMS, preferred_element_type=jnp.float32) * SCALE


def row_sums(weights, ones):
    return jnp.dot(weights, ones, preferred_element_type=jnp.float32)


def partial_kernel(q_ref, k_ref, v_ref, o_ref, stat_ref):
    rows = q_ref.shape[0]
    ones = jnp.ones((rows, HEAD_DIM), jnp.bfloat16)
    for h in range(HEADS_PER_STEP):
        cols = slice(h * HEAD_DIM, (h + 1) * HEAD_DIM)
        s = scores(q_ref[:, cols], k_ref[:, cols])
        m = jnp.max(s, axis=1, keepdims=True)
        p = jnp.exp(s - m).astype(jnp.bfloat16)
        o_ref[:, cols] = jnp.dot(p, v_ref[:, cols], preferred_element_type=jnp.float32).astype(o_ref.dtype)
        stat_ref[:, h : h + 1] = m
        stat_ref[:, HEADS_PER_STEP + h : HEADS_PER_STEP + h + 1] = row_sums(p, ones)[:, 0:1]


def final_kernel(block_ref, q_ref, k_ref, v_ref, kp_ref, vp_ref, o_ref, stat_ref, *rest):
    out_ref, lse_ref = rest[-2:]
    block_index = block_ref[0]
    rows = q_ref.shape[0]
    row_id = lax.broadcasted_iota(jnp.int32, (rows, rows), 0)
    col_id = lax.broadcasted_iota(jnp.int32, (rows, rows), 1)
    causal = col_id <= row_id
    diagonal = col_id == row_id
    has_prev = block_index >= 1
    has_prev2 = block_index >= 2
    ones = jnp.ones((rows, HEAD_DIM), jnp.bfloat16)
    for h in range(HEADS_PER_STEP):
        cols = slice(h * HEAD_DIM, (h + 1) * HEAD_DIM)
        q = q_ref[:, cols]
        s_own = jnp.where(causal, scores(q, k_ref[:, cols]), -jnp.inf)
        s_prev = jnp.where(has_prev, scores(q, kp_ref[:, cols]), -jnp.inf)
        m_near = jnp.max(jnp.maximum(s_own, s_prev), axis=1, keepdims=True)
        m_far = stat_ref[:, h : h + 1]
        l_far = stat_ref[:, HEADS_PER_STEP + h : HEADS_PER_STEP + h + 1]
        m = jnp.where(has_prev2, jnp.maximum(m_near, m_far), m_near)
        far_scale = jnp.where(has_prev2, jnp.exp(m_far - m), 0.0)
        p_own = jnp.exp(s_own - m).astype(jnp.bfloat16)
        p_prev = jnp.exp(s_prev - m).astype(jnp.bfloat16)
        total = row_sums(p_own, ones) + row_sums(p_prev, ones) + far_scale * l_far
        mixed = (
            jnp.dot(p_own, v_ref[:, cols], preferred_element_type=jnp.float32)
            + jnp.dot(p_prev, vp_ref[:, cols], preferred_element_type=jnp.float32)
            + far_scale * o_ref[:, cols].astype(jnp.float32)
        )
        out_ref[:, cols] = (mixed / total).astype(out_ref.dtype)
        lse = m + jnp.log(total[:, 0:1])
        lse_ref[h : h + 1, :] = jnp.sum(jnp.where(diagonal, lse, 0.0), axis=0, keepdims=True)


def partial_attention(q, kv):
    rows, width = q.shape
    step_width = HEADS_PER_STEP * HEAD_DIM
    steps = width // step_width
    block = pl.BlockSpec((rows, step_width), lambda g: (0, g))
    key_block = pl.BlockSpec((None, rows, step_width), lambda g: (0, 0, g))
    value_block = pl.BlockSpec((None, rows, step_width), lambda g: (1, 0, g))
    stat = pl.BlockSpec((None, rows, 2 * HEADS_PER_STEP), lambda g: (g, 0, 0))
    return pl.pallas_call(
        partial_kernel,
        grid=(steps,),
        in_specs=[block, key_block, value_block],
        out_specs=[block, stat],
        out_shape=[
            jax.ShapeDtypeStruct((rows, width), jnp.bfloat16),
            jax.ShapeDtypeStruct((steps, rows, 2 * HEADS_PER_STEP), jnp.float32),
        ],
    )(q, kv, kv)


def final_attention(block_index, chunk, q, k, v, kv_prev, o_far, stat_far, previous):
    rows, width = q.shape
    step_width = HEADS_PER_STEP * HEAD_DIM
    steps = o_far.shape[1] // step_width
    offset = chunk * steps
    whole = pl.BlockSpec((rows, step_width), lambda g, b: (0, g + offset))
    part = pl.BlockSpec((rows, step_width), lambda g, b: (0, g))
    key_block = pl.BlockSpec((None, rows, step_width), lambda g, b: (0, 0, g))
    value_block = pl.BlockSpec((None, rows, step_width), lambda g, b: (1, 0, g))
    stat = pl.BlockSpec((None, rows, 2 * HEADS_PER_STEP), lambda g, b: (g, 0, 0))
    out_stat = pl.BlockSpec((HEADS_PER_STEP, rows), lambda g, b: (g + offset, 0))
    operands = [block_index, q, k, v, kv_prev, kv_prev, o_far, stat_far]
    in_specs = [whole] * 3 + [key_block, value_block, part, stat]
    aliases = {}
    if previous is not None:
        in_specs = in_specs + [pl.BlockSpec(memory_space=pl.ANY)] * 2
        aliases = {len(operands): 0, len(operands) + 1: 1}
        operands = operands + list(previous)
    return pl.pallas_call(
        final_kernel,
        grid_spec=pltpu.PrefetchScalarGridSpec(
            num_scalar_prefetch=1,
            grid=(steps,),
            in_specs=in_specs,
            out_specs=[whole, out_stat],
        ),
        out_shape=[
            jax.ShapeDtypeStruct((rows, width), jnp.bfloat16),
            jax.ShapeDtypeStruct((width // HEAD_DIM, rows), jnp.float32),
        ],
        input_output_aliases=aliases,
    )(*operands)


def shards(att_query, att_key, att_value):
    width = att_query.shape[1]
    chunk_width = width // CHUNKS
    block_index = lax.axis_index("ctx").astype(jnp.int32).reshape(1)
    arrivals = []
    for chunk in range(CHUNKS):
        cols = slice(chunk * chunk_width, (chunk + 1) * chunk_width)
        kv_prev = from_behind(jnp.stack([att_key[:, cols], att_value[:, cols]]), "ctx")
        q_next = from_ahead(att_query[:, cols], "ctx")
        o_far, stat_far = from_behind(partial_attention(q_next, kv_prev), "ctx")
        arrivals.append((kv_prev, o_far, stat_far))
    result = None
    for chunk in range(CHUNKS):
        result = final_attention(block_index, chunk, att_query, att_key, att_value, *arrivals[chunk], result)
    return tuple(result)


def solution(mesh):
    return jax.shard_map(
        shards,
        mesh=mesh,
        in_specs=(P(("dp", "ctx"), None), P(("dp", "ctx"), None), P(("dp", "ctx"), None)),
        out_specs=(P(("dp", "ctx"), None), P(None, ("dp", "ctx"))),
        check_vma=False,
    )
```

time: 130 us -> 117 us (0.900)
  the two profiles are of different devices: /device:TPU:32 before, /device:TPU:56 now
where the time goes in v3:
time: 117 us; the launch traced here: 116 us
  waiting for transfers between devices  50.9 us (44%)
  starting transfers between devices  31.2 us (27%)
  Pallas kernels  26.1 us (22%)
  local copies, waits for them, and re-layouts  6.21 us (5%)
    ppermute x6, waiting for transfers between devices, from_behind(): return lax.ppermute(block, axis, route)  42.5 us
    pallas_call x2, Pallas kernels, final_attention(): pl.pallas_call(final_kernel, grid_spec=pltpu.PrefetchScalarGridSpec(num_s...  19.4 us
    ppermute x2, starting transfers between devices, from_ahead(): return lax.ppermute(block, axis, route)  16.7 us
    ppermute x6, starting transfers between devices, from_behind(): return lax.ppermute(block, axis, route)  14.6 us
    ppermute x2, waiting for transfers between devices, from_ahead(): return lax.ppermute(block, axis, route)  8.38 us
    pallas_call x2, Pallas kernels, partial_attention(): pl.pallas_call(partial_kernel, grid=(steps,), in_specs=[block, key_block,...  6.76 us
    unnamed x20, local copies, waits for them, and re-layouts  3.67 us
  transfers between devices with their start and end apart: 8, of which 4 were waited for; matrix products, arithmetic and copies ran while one was open for 2% of the time, Pallas kernels for 14%

profile of v3, /device:TPU:56, one launch (start us, length us, event | category | flops | bytes accessed | tf_op | source)
XLA Modules:
  0.0 116.4 jit_solution(14048384332492932952)
XLA Ops:
  0.6 1.7 %slice_bitcast_fusion = (bf16[1,128,2048]{2,1,0:T(8,128)(2,1)S(1)}, bf16[1,128,2048]{2,1,0:T(8,128)(2,1)S(1)}, bf16[1,128,2048]{2,1,0:T(8,128)(2,1)S(1)}, bf16[1,128,2048]{2,1,0:T(8,128)(2,1)S(1)}) fusion(bf16[128,4096]{1,0:T(8,128)(2,1)} %v_ref.3, bf16[128,4096]{1,0:T(8,128)(2,1)} %k_ref.3), kind=kLoop, calls=%fused_computation.2 | loop fusion | bytes 4194304 | tf_op jit(solution)/shard_map/stack | solution.py:145
  2.3 0.1 pad_maximum_fusion.1
  2.4 3.4 %collective-permute-start.4 = (bf16[2,128,2048]{2,1,0:T(8,128)(2,1)S(1)}, bf16[2,128,2048]{2,1,0:T(8,128)(2,1)S(1)}, u32[]{:S(2)}, u32[]{:S(2)}) collective-permute-start(bf16[2,128,2048]{2,1,0:T(8,128)(2,1)S(1)} %pad_maximum_fusion.1), channel_id=1, source_target_pairs={{0,4},{4,8},{8,12},{12,16},{16,20},{20,24},{24,28},{28,32},{32,36}... | collective-permute-start | bytes 3145736 | tf_op jit(solution)/shard_map/ppermute | solution.py:20
  5.8 0.0 copy-start.2
  5.8 1.1 pad_maximum_fusion
  6.9 3.4 %collective-permute-start = (bf16[2,128,2048]{2,1,0:T(8,128)(2,1)}, bf16[2,128,2048]{2,1,0:T(8,128)(2,1)S(1)}, u32[]{:S(2)}, u32[]{:S(2)}) collective-permute-start(bf16[2,128,2048]{2,1,0:T(8,128)(2,1)} %pad_maximum_fusion), channel_id=1, source_target_pairs={{0,4},{4,8},{8,12},{12,16},{16,20},{20,24},{24,28},{28,32},{32,36}... | collective-permute-start | bytes 3145736 | tf_op jit(solution)/shard_map/ppermute | solution.py:20
  10.3 0.0 copy-done.2
  10.3 0.9 fusion
  11.2 12.7 %collective-permute-start.5 = (bf16[128,2048]{1,0:T(8,128)(2,1)S(1)}, bf16[128,2048]{1,0:T(8,128)(2,1)S(1)}, u32[]{:S(2)}, u32[]{:S(2)}) collective-permute-start(bf16[128,2048]{1,0:T(8,128)(2,1)S(1)} %get-tuple-element.14), channel_id=1, source_target_pairs={{4,0},{8,4},{12,8},{16,12},{20,16},{24,20},{28,24},{32,28},{36,32}... | collective-permute-start | bytes 1572872 | tf_op jit(solution)/shard_map/ppermute | solution.py:26
  23.9 3.9 %collective-permute-start.1 = (bf16[128,2048]{1,0:T(8,128)(2,1)}, bf16[128,2048]{1,0:T(8,128)(2,1)S(1)}, u32[]{:S(2)}, u32[]{:S(2)}) collective-permute-start(bf16[128,2048]{1,0:T(8,128)(2,1)} %get-tuple-element.15), channel_id=1, source_target_pairs={{4,0},{8,4},{12,8},{16,12},{20,16},{24,20},{28,24},{32,28},{36,32}... | collective-permute-start | bytes 1572872 | tf_op jit(solution)/shard_map/ppermute | solution.py:26
  27.8 8.4 %collective-permute-done.5.q_ref = bf16[128,2048]{1,0:T(8,128)(2,1)S(1)} collective-permute-done((bf16[128,2048]{1,0:T(8,128)(2,1)S(1)}, bf16[128,2048]{1,0:T(8,128)(2,1)S(1)}, u32[]{:S(2)}, u32[]{:S(2)}) %collective-permute-start.5) | collective-permute-done | bytes 524320 | tf_op jit(solution)/shard_map/ppermute | solution.py:26
  36.2 5.9 %collective-permute-done.4.k_ref.v_ref.kp_ref.vp_ref = bf16[2,128,2048]{2,1,0:T(8,128)(2,1)S(1)} collective-permute-done((bf16[2,128,2048]{2,1,0:T(8,128)(2,1)S(1)}, bf16[2,128,2048]{2,1,0:T(8,128)(2,1)S(1)}, u32[]{:S(2)}, u32[]{:S(2)}) %collective-permute-start.4) | collective-permute-done | bytes 1048608 | tf_op jit(solution)/shard_map/ppermute | solution.py:20
  42.1 1.0 copy-done.1
  43.1 3.4 %shard_map.51 = (bf16[128,2048]{1,0:T(8,128)(2,1)}, f32[2,128,16]{2,1,0:T(8,128)}) custom-call(bf16[128,2048]{1,0:T(8,128)(2,1)} %copy-done.5, bf16[2,128,2048]{2,1,0:T(8,128)(2,1)} %copy-done.1, bf16[2,128,2048]{2,1,0:T(8,128)(2,1)} %copy-done.1), custom_call_target="tpu_custom_call" | custom-call | tf_op jit(solution)/shard_map/pallas_call | solution.py:92
  46.4 2.0 %collective-permute-start.6 = (bf16[128,2048]{1,0:T(8,128)(2,1)}, bf16[128,2048]{1,0:T(8,128)(2,1)S(1)}, u32[]{:S(2)}, u32[]{:S(2)}) collective-permute-start(bf16[128,2048]{1,0:T(8,128)(2,1)} %get-tuple-element.10), channel_id=1, source_target_pairs={{0,4},{4,8},{8,12},{12,16},{16,20},{20,24},{24,28},{28,32},{32,36}... | collective-permute-start | bytes 1572872 | tf_op jit(solution)/shard_map/ppermute | solution.py:20
  48.5 0.0 collective-permute-done.1.q_ref
  48.5 16.0 %collective-permute-done.k_ref.v_ref.kp_ref.vp_ref = bf16[2,128,2048]{2,1,0:T(8,128)(2,1)S(1)} collective-permute-done((bf16[2,128,2048]{2,1,0:T(8,128)(2,1)}, bf16[2,128,2048]{2,1,0:T(8,128)(2,1)S(1)}, u32[]{:S(2)}, u32[]{:S(2)}) %collective-permute-start) | collective-permute-done | bytes 1048608 | tf_op jit(solution)/shard_map/ppermute | solution.py:20
  64.6 1.0 copy-done
  65.6 3.4 %shard_map.50 = (bf16[128,2048]{1,0:T(8,128)(2,1)}, f32[2,128,16]{2,1,0:T(8,128)}) custom-call(bf16[128,2048]{1,0:T(8,128)(2,1)} %copy-done.4, bf16[2,128,2048]{2,1,0:T(8,128)(2,1)} %copy-done, bf16[2,128,2048]{2,1,0:T(8,128)(2,1)} %copy-done), custom_call_target="tpu_custom_call" | custom-call | tf_op jit(solution)/shard_map/pallas_call | solution.py:92
  68.9 1.9 %collective-permute-start.2 = (bf16[128,2048]{1,0:T(8,128)(2,1)}, bf16[128,2048]{1,0:T(8,128)(2,1)S(1)}, u32[]{:S(2)}, u32[]{:S(2)}) collective-permute-start(bf16[128,2048]{1,0:T(8,128)(2,1)} %get-tuple-element.8), channel_id=1, source_target_pairs={{0,4},{4,8},{8,12},{12,16},{16,20},{20,24},{24,28},{28,32},{32,36}... | collective-permute-start | bytes 1572872 | tf_op jit(solution)/shard_map/ppermute | solution.py:20
  70.9 1.9 %collective-permute-start.7 = (f32[2,128,16]{2,1,0:T(8,128)S(1)}, f32[2,128,16]{2,1,0:T(8,128)S(1)}, u32[]{:S(2)}, u32[]{:S(2)}) collective-permute-start(f32[2,128,16]{2,1,0:T(8,128)S(1)} %copy-done.9), channel_id=1, source_target_pairs={{0,4},{4,8},{8,12},{12,16},{16,20},{20,24},{24,28},{28,32},{32,36}... | collective-permute-start | bytes 49160 | tf_op jit(solution)/shard_map/ppermute | solution.py:20
  72.8 1.9 %collective-permute-start.3 = (f32[2,128,16]{2,1,0:T(8,128)}, f32[2,128,16]{2,1,0:T(8,128)S(1)}, u32[]{:S(2)}, u32[]{:S(2)}) collective-permute-start(f32[2,128,16]{2,1,0:T(8,128)} %get-tuple-element.9), channel_id=1, source_target_pairs={{0,4},{4,8},{8,12},{12,16},{16,20},{20,24},{24,28},{28,32},{32,36}... | collective-permute-start | bytes 49160 | tf_op jit(solution)/shard_map/ppermute | solution.py:20
  74.7 20.6 %collective-permute-done.7.stat_ref = f32[2,128,16]{2,1,0:T(8,128)S(1)} collective-permute-done((f32[2,128,16]{2,1,0:T(8,128)S(1)}, f32[2,128,16]{2,1,0:T(8,128)S(1)}, u32[]{:S(2)}, u32[]{:S(2)}) %collective-permute-start.7) | collective-permute-done | bytes 16416 | tf_op jit(solution)/shard_map/ppermute | solution.py:20
  95.3 0.0 collective-permute-done.6.o_ref
  95.3 0.6 copy-done.8
  96.0 0.2 copy-done.3
  96.2 9.7 %shard_map.52 = (bf16[128,4096]{1,0:T(8,128)(2,1)}, f32[32,128]{1,0:T(8,128)}) custom-call(s32[1]{0:T(128)} %bitcast.block_ref, bf16[128,4096]{1,0:T(8,128)(2,1)} %q_ref.3, bf16[128,4096]{1,0:T(8,128)(2,1)} %k_ref.3, bf16[128,4096]{1,0:T(8,128)(2,1)} %v_ref.3, bf16[2,128,2048]{2,1,0:T(8,128)(2,1)} %copy-done.1, bf16[2,128,2048]{2,1,0:T(8,128)(2,1)} %copy-done.1, ...), custom_call_target="tpu_custom_call" | custom-call | tf_op jit(solution)/shard_map/pallas_call | solution.py:122
  105.8 0.0 collective-permute-done.3.stat_ref
  105.9 0.0 collective-permute-done.2.o_ref
  105.9 0.6 copy-done.7
  106.5 0.2 copy-done.6
  106.7 9.7 %shard_map.53 = (bf16[128,4096]{1,0:T(8,128)(2,1)}, f32[32,128]{1,0:T(8,128)}) custom-call(s32[1]{0:T(128)} %bitcast.block_ref, bf16[128,4096]{1,0:T(8,128)(2,1)} %q_ref.3, bf16[128,4096]{1,0:T(8,128)(2,1)} %k_ref.3, bf16[128,4096]{1,0:T(8,128)(2,1)} %v_ref.3, bf16[2,128,2048]{2,1,0:T(8,128)(2,1)} %copy-done, ...), custom_call_target="tpu_custom_call", output_to_operand_aliasing={{0}: (8, {}), {1}: (9, {})} | custom-call | tf_op jit(solution)/shard_map/pallas_call | solution.py:122
  (12 shorter events, 0.0 us)
Async XLA Ops:
  2.4 39.7 %collective-permute-start.4 = (bf16[2,128,2048]{2,1,0:T(8,128)(2,1)S(1)}, bf16[2,128,2048]{2,1,0:T(8,128)(2,1)S(1)}, u32[]{:S(2)}, u32[]{:S(2)}) collective-permute-start(bf16[2,128,2048]{2,1,0:T(8,128)(2,1)S(1)} %pad_maximum_fusion.1), channel_id=1, source_target_pairs={{0,4},{4,8},{8,12},{12,16},{16,20},{20,24},{24,28},{28,32},{32,36}... | collective-permute-start | bytes 3145736 | tf_op jit(solution)/shard_map/ppermute | solution.py:20
  5.8 4.5 %copy-start.2 = (bf16[128,4096]{1,0:T(8,128)(2,1)S(1)}, bf16[128,4096]{1,0:T(8,128)(2,1)}, u32[]{:S(2)}) copy-start(bf16[128,4096]{1,0:T(8,128)(2,1)} %q_ref.3) | copy-start | bytes 3145732
  6.9 57.7 %collective-permute-start = (bf16[2,128,2048]{2,1,0:T(8,128)(2,1)}, bf16[2,128,2048]{2,1,0:T(8,128)(2,1)S(1)}, u32[]{:S(2)}, u32[]{:S(2)}) collective-permute-start(bf16[2,128,2048]{2,1,0:T(8,128)(2,1)} %pad_maximum_fusion), channel_id=1, source_target_pairs={{0,4},{4,8},{8,12},{12,16},{16,20},{20,24},{24,28},{28,32},{32,36}... | collective-permute-start | bytes 3145736 | tf_op jit(solution)/shard_map/ppermute | solution.py:20
  11.2 25.0 %collective-permute-start.5 = (bf16[128,2048]{1,0:T(8,128)(2,1)S(1)}, bf16[128,2048]{1,0:T(8,128)(2,1)S(1)}, u32[]{:S(2)}, u32[]{:S(2)}) collective-permute-start(bf16[128,2048]{1,0:T(8,128)(2,1)S(1)} %get-tuple-element.14), channel_id=1, source_target_pairs={{4,0},{8,4},{12,8},{16,12},{20,16},{24,20},{28,24},{32,28},{36,32}... | collective-permute-start | bytes 1572872 | tf_op jit(solution)/shard_map/ppermute | solution.py:26
  23.9 24.6 %collective-permute-start.1 = (bf16[128,2048]{1,0:T(8,128)(2,1)}, bf16[128,2048]{1,0:T(8,128)(2,1)S(1)}, u32[]{:S(2)}, u32[]{:S(2)}) collective-permute-start(bf16[128,2048]{1,0:T(8,128)(2,1)} %get-tuple-element.15), channel_id=1, source_target_pairs={{4,0},{8,4},{12,8},{16,12},{20,16},{24,20},{28,24},{32,28},{36,32}... | collective-permute-start | bytes 1572872 | tf_op jit(solution)/shard_map/ppermute | solution.py:26
  36.2 5.9 %copy-start.5 = (bf16[128,2048]{1,0:T(8,128)(2,1)}, bf16[128,2048]{1,0:T(8,128)(2,1)S(1)}, u32[]{:S(2)}) copy-start(bf16[128,2048]{1,0:T(8,128)(2,1)S(1)} %collective-permute-done.5.q_ref) | copy-start | bytes 1572868
  42.1 1.0 copy-start.1
  46.4 24.4 %copy-start.9 = (f32[2,128,16]{2,1,0:T(8,128)S(1)}, f32[2,128,16]{2,1,0:T(8,128)}, u32[]{:S(2)}) copy-start(f32[2,128,16]{2,1,0:T(8,128)} %get-tuple-element.11) | copy-start | bytes 49156
  46.4 48.9 %collective-permute-start.6 = (bf16[128,2048]{1,0:T(8,128)(2,1)}, bf16[128,2048]{1,0:T(8,128)(2,1)S(1)}, u32[]{:S(2)}, u32[]{:S(2)}) collective-permute-start(bf16[128,2048]{1,0:T(8,128)(2,1)} %get-tuple-element.10), channel_id=1, source_target_pairs={{0,4},{4,8},{8,12},{12,16},{16,20},{20,24},{24,28},{28,32},{32,36}... | collective-permute-start | bytes 1572872 | tf_op jit(solution)/shard_map/ppermute | solution.py:20
  48.5 16.1 %copy-start.4 = (bf16[128,2048]{1,0:T(8,128)(2,1)}, bf16[128,2048]{1,0:T(8,128)(2,1)S(1)}, u32[]{:S(2)}) copy-start(bf16[128,2048]{1,0:T(8,128)(2,1)S(1)} %collective-permute-done.1.q_ref) | copy-start | bytes 1572868
  64.6 1.0 copy-start
  68.9 36.9 %collective-permute-start.2 = (bf16[128,2048]{1,0:T(8,128)(2,1)}, bf16[128,2048]{1,0:T(8,128)(2,1)S(1)}, u32[]{:S(2)}, u32[]{:S(2)}) collective-permute-start(bf16[128,2048]{1,0:T(8,128)(2,1)} %get-tuple-element.8), channel_id=1, source_target_pairs={{0,4},{4,8},{8,12},{12,16},{16,20},{20,24},{24,28},{28,32},{32,36}... | collective-permute-start | bytes 1572872 | tf_op jit(solution)/shard_map/ppermute | solution.py:20
  70.9 24.5 %collective-permute-start.7 = (f32[2,128,16]{2,1,0:T(8,128)S(1)}, f32[2,128,16]{2,1,0:T(8,128)S(1)}, u32[]{:S(2)}, u32[]{:S(2)}) collective-permute-start(f32[2,128,16]{2,1,0:T(8,128)S(1)} %copy-done.9), channel_id=1, source_target_pairs={{0,4},{4,8},{8,12},{12,16},{16,20},{20,24},{24,28},{28,32},{32,36}... | collective-permute-start | bytes 49160 | tf_op jit(solution)/shard_map/ppermute | solution.py:20
  72.8 33.1 %collective-permute-start.3 = (f32[2,128,16]{2,1,0:T(8,128)}, f32[2,128,16]{2,1,0:T(8,128)S(1)}, u32[]{:S(2)}, u32[]{:S(2)}) collective-permute-start(f32[2,128,16]{2,1,0:T(8,128)} %get-tuple-element.9), channel_id=1, source_target_pairs={{0,4},{4,8},{8,12},{12,16},{16,20},{20,24},{24,28},{28,32},{32,36}... | collective-permute-start | bytes 49160 | tf_op jit(solution)/shard_map/ppermute | solution.py:20
  95.3 0.6 copy-start.8
  95.3 0.8 copy-start.3
  105.8 0.7 copy-start.7
  105.9 0.9 copy-start.6

commit v4 on v3

v4 whole, which is shorter than its diff:
```python
import math

import jax
import jax.numpy as jnp
from jax import lax
from jax.experimental import pallas as pl
from jax.experimental.pallas import tpu as pltpu
from jax.sharding import PartitionSpec as P

HEAD_DIM = 128
HEADS_PER_STEP = 8
SCALE = 1.0 / math.sqrt(HEAD_DIM)
NT_DIMS = (((1,), (1,)), ((), ()))


def from_behind(block, axis):
    devices = range(lax.axis_size(axis))
    route = [(i - 1, i) for i in devices if i - 1 in devices]
    return lax.ppermute(block, axis, route)


def from_ahead(block, axis):
    devices = range(lax.axis_size(axis))
    route = [(i + 1, i) for i in devices if i + 1 in devices]
    return lax.ppermute(block, axis, route)


def weighted_values(weights, values):
    ones = jnp.ones((values.shape[0], HEAD_DIM), values.dtype)
    result = jnp.dot(weights, jnp.concatenate([values, ones], axis=1), preferred_element_type=jnp.float32)
    return result[:, :HEAD_DIM], result[:, HEAD_DIM : HEAD_DIM + 1]


def partial_kernel(q_ref, k_ref, v_ref, o_ref, stat_ref):
    for h in range(HEADS_PER_STEP):
        cols = slice(h * HEAD_DIM, (h + 1) * HEAD_DIM)
        s = lax.dot_general(q_ref[:, cols], k_ref[:, cols], NT_DIMS, preferred_element_type=jnp.float32) * SCALE
        m = jnp.max(s, axis=1, keepdims=True)
        p = jnp.exp(s - m).astype(jnp.bfloat16)
        mixed, total = weighted_values(p, v_ref[:, cols])
        o_ref[:, cols] = mixed.astype(o_ref.dtype)
        stat_ref[:, h : h + 1] = m
        stat_ref[:, HEADS_PER_STEP + h : HEADS_PER_STEP + h + 1] = total


def near_kernel(block_ref, q_ref, k_ref, v_ref, kp_ref, vp_ref, mixed_ref, stat_ref):
    rows = q_ref.shape[0]
    row_id = lax.broadcasted_iota(jnp.int32, (rows, 2 * rows), 0)
    col_id = lax.broadcasted_iota(jnp.int32, (rows, 2 * rows), 1)
    first_prev = jnp.where(block_ref[0] >= 1, rows, 2 * rows)
    allowed = (col_id <= row_id) | (col_id >= first_prev)
    for h in range(HEADS_PER_STEP):
        cols = slice(h * HEAD_DIM, (h + 1) * HEAD_DIM)
        keys = jnp.concatenate([k_ref[:, cols], kp_ref[:, cols]], axis=0)
        values = jnp.concatenate([v_ref[:, cols], vp_ref[:, cols]], axis=0)
        s = lax.dot_general(q_ref[:, cols], keys, NT_DIMS, preferred_element_type=jnp.float32) * SCALE
        s = jnp.where(allowed, s, -jnp.inf)
        m = jnp.max(s, axis=1, keepdims=True)
        p = jnp.exp(s - m).astype(jnp.bfloat16)
        mixed, total = weighted_values(p, values)
        mixed_ref[:, cols] = mixed
        stat_ref[:, h : h + 1] = m
        stat_ref[:, HEADS_PER_STEP + h : HEADS_PER_STEP + h + 1] = total


def stat_spec(rows):
    return pl.BlockSpec((None, rows, 2 * HEADS_PER_STEP), lambda g, *_: (g, 0, 0))


def partial_attention(q, kv):
    rows, width = q.shape
    step_width = HEADS_PER_STEP * HEAD_DIM
    steps = width // step_width
    block = pl.BlockSpec((rows, step_width), lambda g: (0, g))
    key_block = pl.BlockSpec((None, rows, step_width), lambda g: (0, 0, g))
    value_block = pl.BlockSpec((None, rows, step_width), lambda g: (1, 0, g))
    return pl.pallas_call(
        partial_kernel,
        grid=(steps,),
        in_specs=[block, key_block, value_block],
        out_specs=[block, stat_spec(rows)],
        out_shape=[
            jax.ShapeDtypeStruct((rows, width), jnp.bfloat16),
            jax.ShapeDtypeStruct((steps, rows, 2 * HEADS_PER_STEP), jnp.float32),
        ],
    )(q, kv, kv)


def near_attention(block_index, q, k, v, kv_prev):
    rows, width = q.shape
    step_width = HEADS_PER_STEP * HEAD_DIM
    steps = width // step_width
    block = pl.BlockSpec((rows, step_width), lambda g, b: (0, g))
    key_block = pl.BlockSpec((None, rows, step_width), lambda g, b: (0, 0, g))
    value_block = pl.BlockSpec((None, rows, step_width), lambda g, b: (1, 0, g))
    return pl.pallas_call(
        near_kernel,
        grid_spec=pltpu.PrefetchScalarGridSpec(
            num_scalar_prefetch=1,
            grid=(steps,),
            in_specs=[block] * 3 + [key_block, value_block],
            out_specs=[block, stat_spec(rows)],
        ),
        out_shape=[
            jax.ShapeDtypeStruct((rows, width), jnp.float32),
            jax.ShapeDtypeStruct((steps, rows, 2 * HEADS_PER_STEP), jnp.float32),
        ],
    )(block_index, q, k, v, kv_prev, kv_prev)


def per_head(stat):
    steps, rows, _ = stat.shape
    stat = jnp.transpose(stat.reshape(steps, rows, 2, HEADS_PER_STEP), (2, 1, 0, 3))
    return stat[0].reshape(rows, steps * HEADS_PER_STEP), stat[1].reshape(rows, steps * HEADS_PER_STEP)


def merge(block_index, mixed_near, stat_near, o_far, stat_far):
    rows, width = mixed_near.shape
    heads = width // HEAD_DIM
    m_near, l_near = per_head(stat_near)
    m_far, l_far = per_head(stat_far)
    has_far = block_index >= 2
    m = jnp.where(has_far, jnp.maximum(m_near, m_far), m_near)
    near_scale = jnp.exp(m_near - m)
    far_scale = jnp.where(has_far, jnp.exp(m_far - m), 0.0)
    total = near_scale * l_near + far_scale * l_far
    mixed = (
        near_scale[:, :, None] * mixed_near.reshape(rows, heads, HEAD_DIM)
        + far_scale[:, :, None] * o_far.reshape(rows, heads, HEAD_DIM).astype(jnp.float32)
    )
    out = (mixed / total[:, :, None]).reshape(rows, width).astype(jnp.bfloat16)
    return out, jnp.transpose(m + jnp.log(total))


def shards(att_query, att_key, att_value):
    block_index = lax.axis_index("ctx").astype(jnp.int32)
    kv_prev = from_behind(jnp.stack([att_key, att_value]), "ctx")
    q_next = from_ahead(att_query, "ctx")
    o_far, stat_far = from_behind(partial_attention(q_next, kv_prev), "ctx")
    mixed_near, stat_near = near_attention(block_index.reshape(1), att_query, att_key, att_value, kv_prev)
    return merge(block_index, mixed_near, stat_near, o_far, stat_far)


def solution(mesh):
    return jax.shard_map(
        shards,
        mesh=mesh,
        in_specs=(P(("dp", "ctx"), None), P(("dp", "ctx"), None), P(("dp", "ctx"), None)),
        out_specs=(P(("dp", "ctx"), None), P(None, ("dp", "ctx"))),
        check_vma=False,
    )
```

time: 117 us -> 124 us (1.060)
  waiting for transfers between devices: 50.9 us -> 72.9 us
  Pallas kernels: 26.1 us -> 16.1 us
  starting transfers between devices: 31.2 us -> 21.5 us
  other arithmetic: 1.16 us -> 7.28 us
  local copies, waits for them, and re-layouts: 6.21 us -> 4.96 us
    ppermute x2 -> x1, waiting for transfers between devices: 8.38 us -> 22.4 us  [from_ahead(): return lax.ppermute(block, axis, route)]
    pallas_call x2 -> x1, Pallas kernels: 19.4 us -> 5.78 us  [near_attention(): pl.pallas_call(near_kernel, grid_spec=pltpu.PrefetchScalarGridSpec(num_sc...]
    ppermute x6 -> x3, waiting for transfers between devices: 42.5 us -> 50.5 us  [from_behind(): return lax.ppermute(block, axis, route)]
    ppermute x6 -> x3, starting transfers between devices: 14.6 us -> 7.23 us  [from_behind(): return lax.ppermute(block, axis, route)]
    convert_element_type x0 -> x1, other arithmetic: none -> 4.82 us  [merge(): out = (mixed / total[:, :, None]).reshape(rows, width).astype(jnp.bfloat16)]
    pallas_call x2 -> x1, Pallas kernels: 6.76 us -> 10.3 us  [partial_attention(): pl.pallas_call(partial_kernel, grid=(steps,), in_specs=[block, key_block,...]
    ppermute x2 -> x1, starting transfers between devices: 16.7 us -> 14.2 us  [from_ahead(): return lax.ppermute(block, axis, route)]
    unnamed x20 -> x8, local copies, waits for them, and re-layouts: 3.67 us -> 1.72 us
  transfers between devices with their start and end apart: 8 -> 4, of which waited for: 4 -> 3; matrix products, arithmetic and copies ran while one was open for 2% -> 2% of each run, Pallas kernels for 14% -> 5%
where the time goes in v4:
time: 124 us; the launch traced here: 123 us
  waiting for transfers between devices  72.9 us (59%)
  starting transfers between devices  21.5 us (17%)
  Pallas kernels  16.1 us (13%)
  other arithmetic  7.28 us (6%)
  local copies, waits for them, and re-layouts  4.96 us (4%)
    ppermute x3, waiting for transfers between devices, from_behind(): return lax.ppermute(block, axis, route)  50.5 us
    ppermute x1, waiting for transfers between devices, from_ahead(): return lax.ppermute(block, axis, route)  22.4 us
    ppermute x1, starting transfers between devices, from_ahead(): return lax.ppermute(block, axis, route)  14.2 us
    pallas_call x1, Pallas kernels, partial_attention(): pl.pallas_call(partial_kernel, grid=(steps,), in_specs=[block, key_block,...  10.3 us
    ppermute x3, starting transfers between devices, from_behind(): return lax.ppermute(block, axis, route)  7.23 us
    pallas_call x1, Pallas kernels, near_attention(): pl.pallas_call(near_kernel, grid_spec=pltpu.PrefetchScalarGridSpec(num_sc...  5.78 us
    convert_element_type x1, other arithmetic, merge(): out = (mixed / total[:, :, None]).reshape(rows, width).astype(jnp.bfloat16)  4.82 us
  transfers between devices with their start and end apart: 4, of which 3 were waited for; matrix products, arithmetic and copies ran while one was open for 2% of the time, Pallas kernels for 5%

profile of v4, /device:TPU:56, one launch (start us, length us, event | category | flops | bytes accessed | tf_op | source)
XLA Modules:
  0.0 123.4 jit_solution(10091510363360470154)
XLA Ops:
  0.6 0.0 copy-start.3
  0.6 1.8 %pad_maximum_fusion = bf16[2,128,4096]{2,1,0:T(8,128)(2,1)S(1)} fusion(bf16[1,128,4096]{2,1,0:T(8,128)(2,1)} %bitcast.63, bf16[1,128,4096]{2,1,0:T(8,128)(2,1)} %bitcast.64), kind=kLoop, calls=%fused_computation.5 | loop fusion | flops 1048576 | bytes 4194304 | tf_op jit(solution)/shard_map/stack | solution.py:137
  2.5 3.4 %collective-permute-start = (bf16[2,128,4096]{2,1,0:T(8,128)(2,1)S(1)}, bf16[2,128,4096]{2,1,0:T(8,128)(2,1)S(1)}, u32[]{:S(2)}, u32[]{:S(2)}) collective-permute-start(bf16[2,128,4096]{2,1,0:T(8,128)(2,1)S(1)} %pad_maximum_fusion), channel_id=1, source_target_pairs={{0,4},{4,8},{8,12},{12,16},{16,20},{20,24},{24,28},{28,32},{32,36}... | collective-permute-start | bytes 6291464 | tf_op jit(solution)/shard_map/ppermute | solution.py:19
  5.9 0.0 copy-done.3
  5.9 14.2 %collective-permute-start.1 = (bf16[128,4096]{1,0:T(8,128)(2,1)S(1)}, bf16[128,4096]{1,0:T(8,128)(2,1)S(1)}, u32[]{:S(2)}, u32[]{:S(2)}) collective-permute-start(bf16[128,4096]{1,0:T(8,128)(2,1)S(1)} %copy-done.3), channel_id=1, source_target_pairs={{4,0},{8,4},{12,8},{16,12},{20,16},{24,20},{28,24},{32,28},{36,32}... | collective-permute-start | bytes 3145736 | tf_op jit(solution)/shard_map/ppermute | solution.py:25
  20.1 22.4 %collective-permute-done.1.q_ref = bf16[128,4096]{1,0:T(8,128)(2,1)S(1)} collective-permute-done((bf16[128,4096]{1,0:T(8,128)(2,1)S(1)}, bf16[128,4096]{1,0:T(8,128)(2,1)S(1)}, u32[]{:S(2)}, u32[]{:S(2)}) %collective-permute-start.1) | collective-permute-done | bytes 1048608 | tf_op jit(solution)/shard_map/ppermute | solution.py:25
  42.5 0.0 copy-start.2
  42.5 21.3 %collective-permute-done.kp_ref.vp_ref.k_ref.v_ref = bf16[2,128,4096]{2,1,0:T(8,128)(2,1)S(1)} collective-permute-done((bf16[2,128,4096]{2,1,0:T(8,128)(2,1)S(1)}, bf16[2,128,4096]{2,1,0:T(8,128)(2,1)S(1)}, u32[]{:S(2)}, u32[]{:S(2)}) %collective-permute-start) | collective-permute-done | bytes 2097184 | tf_op jit(solution)/shard_map/ppermute | solution.py:19
  63.8 0.0 copy-done.2
  63.8 0.0 copy-start
  63.8 1.3 %copy-done = bf16[2,128,4096]{2,1,0:T(8,128)(2,1)} copy-done((bf16[2,128,4096]{2,1,0:T(8,128)(2,1)}, bf16[2,128,4096]{2,1,0:T(8,128)(2,1)S(1)}, u32[]{:S(2)}) %copy-start) | copy-done | bytes 2097176
  65.1 10.3 %shard_map.51 = (bf16[128,4096]{1,0:T(8,128)(2,1)}, f32[4,128,16]{2,1,0:T(8,128)}) custom-call(bf16[128,4096]{1,0:T(8,128)(2,1)} %copy-done.2, bf16[2,128,4096]{2,1,0:T(8,128)(2,1)} %copy-done, bf16[2,128,4096]{2,1,0:T(8,128)(2,1)} %copy-done), custom_call_target="tpu_custom_call" | custom-call | tf_op jit(solution)/shard_map/pallas_call | solution.py:77
  75.4 1.9 %collective-permute-start.3 = (bf16[128,4096]{1,0:T(8,128)(2,1)}, bf16[128,4096]{1,0:T(8,128)(2,1)S(1)}, u32[]{:S(2)}, u32[]{:S(2)}) collective-permute-start(bf16[128,4096]{1,0:T(8,128)(2,1)} %get-tuple-element.9), channel_id=1, source_target_pairs={{0,4},{4,8},{8,12},{12,16},{16,20},{20,24},{24,28},{28,32},{32,36}... | collective-permute-start | bytes 3145736 | tf_op jit(solution)/shard_map/ppermute | solution.py:19
  77.3 1.9 %collective-permute-start.2 = (f32[4,128,16]{2,1,0:T(8,128)}, f32[4,128,16]{2,1,0:T(8,128)S(1)}, u32[]{:S(2)}, u32[]{:S(2)}) collective-permute-start(f32[4,128,16]{2,1,0:T(8,128)} %get-tuple-element.7), channel_id=1, source_target_pairs={{0,4},{4,8},{8,12},{12,16},{16,20},{20,24},{24,28},{28,32},{32,36}... | collective-permute-start | bytes 98312 | tf_op jit(solution)/shard_map/ppermute | solution.py:19
  79.3 5.8 %shard_map.50 = (f32[128,4096]{1,0:T(8,128)}, f32[4,128,16]{2,1,0:T(8,128)}) custom-call(s32[1]{0:T(128)} %bitcast.block_ref, bf16[128,4096]{1,0:T(8,128)(2,1)} %q_ref.1, bf16[128,4096]{1,0:T(8,128)(2,1)} %k_ref.1, bf16[128,4096]{1,0:T(8,128)(2,1)} %v_ref.1, bf16[2,128,4096]{2,1,0:T(8,128)(2,1)} %copy-done, bf16[2,128,4096]{2,1,0:T(8,128)(2,1)} %copy-done), custom_call_target="tpu_custom_call" | custom-call | tf_op jit(solution)/shard_map/pallas_call | solution.py:96
  85.1 1.0 copy.12
  86.1 29.2 %collective-permute-done.2 = f32[4,128,16]{2,1,0:T(8,128)S(1)} collective-permute-done((f32[4,128,16]{2,1,0:T(8,128)}, f32[4,128,16]{2,1,0:T(8,128)S(1)}, u32[]{:S(2)}, u32[]{:S(2)}) %collective-permute-start.2) | collective-permute-done | bytes 32800 | tf_op jit(solution)/shard_map/ppermute | solution.py:19
  115.3 0.1 copy.13
  115.4 0.6 add_bitcast_fusion
  116.0 0.1 copy.16
  116.1 0.1 copy.14
  116.2 0.1 copy.15
  116.3 0.0 collective-permute-done.3
  116.3 0.6 mul.39
  117.0 0.0 copy-start.1
  117.0 0.6 mul.36
  117.6 0.6 div.11
  118.2 0.4 copy-done.1
  118.5 4.8 %fusion = bf16[128,4096]{1,0:T(8,128)(2,1)} fusion(f32[16,8,32,128]{3,2,1,0:T(8,128)S(1)} %bitcast.62, f32[16,8,32,128]{3,2,1,0:T(8,128)S(1)} %bitcast.60, f32[128,4096]{1,0:T(8,128)S(1)} %copy-done.1, f32[16,8,32,128]{3,2,1,0:T(8,128)S(1)} %bitcast.61, bf16[128,4096]{1,0:T(8,128)(2,1)S(1)} %collective-permute-done.3), kind=kLoop, calls=%fused_computation.1 | loop fusion | flops 3145728 | bytes 10485760 | tf_op jit(solution)/shard_map/convert_element_type | solution.py:131
Async XLA Ops:
  0.6 5.2 %copy-start.3 = (bf16[128,4096]{1,0:T(8,128)(2,1)S(1)}, bf16[128,4096]{1,0:T(8,128)(2,1)}, u32[]{:S(2)}) copy-start(bf16[128,4096]{1,0:T(8,128)(2,1)} %q_ref.1) | copy-start | bytes 3145732
  2.5 61.3 %collective-permute-start = (bf16[2,128,4096]{2,1,0:T(8,128)(2,1)S(1)}, bf16[2,128,4096]{2,1,0:T(8,128)(2,1)S(1)}, u32[]{:S(2)}, u32[]{:S(2)}) collective-permute-start(bf16[2,128,4096]{2,1,0:T(8,128)(2,1)S(1)} %pad_maximum_fusion), channel_id=1, source_target_pairs={{0,4},{4,8},{8,12},{12,16},{16,20},{20,24},{24,28},{28,32},{32,36}... | collective-permute-start | bytes 6291464 | tf_op jit(solution)/shard_map/ppermute | solution.py:19
  5.9 36.6 %collective-permute-start.1 = (bf16[128,4096]{1,0:T(8,128)(2,1)S(1)}, bf16[128,4096]{1,0:T(8,128)(2,1)S(1)}, u32[]{:S(2)}, u32[]{:S(2)}) collective-permute-start(bf16[128,4096]{1,0:T(8,128)(2,1)S(1)} %copy-done.3), channel_id=1, source_target_pairs={{4,0},{8,4},{12,8},{16,12},{20,16},{24,20},{28,24},{32,28},{36,32}... | collective-permute-start | bytes 3145736 | tf_op jit(solution)/shard_map/ppermute | solution.py:25
  42.5 21.3 %copy-start.2 = (bf16[128,4096]{1,0:T(8,128)(2,1)}, bf16[128,4096]{1,0:T(8,128)(2,1)S(1)}, u32[]{:S(2)}) copy-start(bf16[128,4096]{1,0:T(8,128)(2,1)S(1)} %collective-permute-done.1.q_ref) | copy-start | bytes 3145732
  63.8 1.3 %copy-start = (bf16[2,128,4096]{2,1,0:T(8,128)(2,1)}, bf16[2,128,4096]{2,1,0:T(8,128)(2,1)S(1)}, u32[]{:S(2)}) copy-start(bf16[2,128,4096]{2,1,0:T(8,128)(2,1)S(1)} %collective-permute-done.kp_ref.vp_ref.k_ref.v_ref) | copy-start | bytes 6291460
  75.4 40.9 %collective-permute-start.3 = (bf16[128,4096]{1,0:T(8,128)(2,1)}, bf16[128,4096]{1,0:T(8,128)(2,1)S(1)}, u32[]{:S(2)}, u32[]{:S(2)}) collective-permute-start(bf16[128,4096]{1,0:T(8,128)(2,1)} %get-tuple-element.9), channel_id=1, source_target_pairs={{0,4},{4,8},{8,12},{12,16},{16,20},{20,24},{24,28},{28,32},{32,36}... | collective-permute-start | bytes 3145736 | tf_op jit(solution)/shard_map/ppermute | solution.py:19
  77.3 38.0 %collective-permute-start.2 = (f32[4,128,16]{2,1,0:T(8,128)}, f32[4,128,16]{2,1,0:T(8,128)S(1)}, u32[]{:S(2)}, u32[]{:S(2)}) collective-permute-start(f32[4,128,16]{2,1,0:T(8,128)} %get-tuple-element.7), channel_id=1, source_target_pairs={{0,4},{4,8},{8,12},{12,16},{16,20},{20,24},{24,28},{28,32},{32,36}... | collective-permute-start | bytes 98312 | tf_op jit(solution)/shard_map/ppermute | solution.py:19
  117.0 1.6 %copy-start.1 = (f32[128,4096]{1,0:T(8,128)S(1)}, f32[128,4096]{1,0:T(8,128)}, u32[]{:S(2)}) copy-start(f32[128,4096]{1,0:T(8,128)} %get-tuple-element.8) | copy-start | bytes 6291460

commit v5 on v4

--- a/solution.py
+++ b/solution.py
@@ -9,6 +9,7 @@
 
 HEAD_DIM = 128
 HEADS_PER_STEP = 8
+CHUNKS = 2
 SCALE = 1.0 / math.sqrt(HEAD_DIM)
 NT_DIMS = (((1,), (1,)), ((), ()))
 
@@ -31,16 +32,18 @@
     return result[:, :HEAD_DIM], result[:, HEAD_DIM : HEAD_DIM + 1]
 
 
-def partial_kernel(q_ref, k_ref, v_ref, o_ref, stat_ref):
+def partial_kernel(q_ref, k_ref, v_ref, *rest):
+    o_ref, stat_ref = rest[-2:]
+    ones = jnp.ones((q_ref.shape[0], HEAD_DIM), jnp.bfloat16)
     for h in range(HEADS_PER_STEP):
         cols = slice(h * HEAD_DIM, (h + 1) * HEAD_DIM)
         s = lax.dot_general(q_ref[:, cols], k_ref[:, cols], NT_DIMS, preferred_element_type=jnp.float32) * SCALE
         m = jnp.max(s, axis=1, keepdims=True)
         p = jnp.exp(s - m).astype(jnp.bfloat16)
-        mixed, total = weighted_values(p, v_ref[:, cols])
-        o_ref[:, cols] = mixed.astype(o_ref.dtype)
+        o_ref[:, cols] = jnp.dot(p, v_ref[:, cols], preferred_element_type=jnp.float32).astype(o_ref.dtype)
         stat_ref[:, h : h + 1] = m
-        stat_ref[:, HEADS_PER_STEP + h : HEADS_PER_STEP + h + 1] = total
+        total = jnp.dot(p, ones, preferred_element_type=jnp.float32)
+        stat_ref[:, HEADS_PER_STEP + h : HEADS_PER_STEP + h + 1] = total[:, 0:1]
 
 
 def near_kernel(block_ref, q_ref, k_ref, v_ref, kp_ref, vp_ref, mixed_ref, stat_ref):
@@ -67,7 +70,7 @@
     return pl.BlockSpec((None, rows, 2 * HEADS_PER_STEP), lambda g, *_: (g, 0, 0))
 
 
-def partial_attention(q, kv):
+def partial_attention(q, kv, after=()):
     rows, width = q.shape
     step_width = HEADS_PER_STEP * HEAD_DIM
     steps = width // step_width
@@ -77,13 +80,13 @@
     return pl.pallas_call(
         partial_kernel,
         grid=(steps,),
-        in_specs=[block, key_block, value_block],
+        in_specs=[block, key_block, value_block] + [pl.BlockSpec(memory_space=pl.ANY)] * len(after),
         out_specs=[block, stat_spec(rows)],
         out_shape=[
             jax.ShapeDtypeStruct((rows, width), jnp.bfloat16),
             jax.ShapeDtypeStruct((steps, rows, 2 * HEADS_PER_STEP), jnp.float32),
         ],
-    )(q, kv, kv)
+    )(q, kv, kv, *after)
 
 
 def near_attention(block_index, q, k, v, kv_prev):
@@ -108,37 +111,86 @@
     )(block_index, q, k, v, kv_prev, kv_prev)
 
 
+def merge_kernel(block_ref, mixed_ref, near_ref, o_ref, far_ref, *rest):
+    out_ref = rest[-1]
+    has_far = block_ref[0] >= 2
+    for h in range(HEADS_PER_STEP):
+        cols = slice(h * HEAD_DIM, (h + 1) * HEAD_DIM)
+        m_near = near_ref[:, h : h + 1]
+        m_far = far_ref[:, h : h + 1]
+        l_near = near_ref[:, HEADS_PER_STEP + h : HEADS_PER_STEP + h + 1]
+        l_far = far_ref[:, HEADS_PER_STEP + h : HEADS_PER_STEP + h + 1]
+        m = jnp.where(has_far, jnp.maximum(m_near, m_far), m_near)
+        near_scale = jnp.exp(m_near - m)
+        far_scale = jnp.where(has_far, jnp.exp(m_far - m), 0.0)
+        total = near_scale * l_near + far_scale * l_far
+        mixed = near_scale * mixed_ref[:, cols] + far_scale * o_ref[:, cols].astype(jnp.float32)
+        out_ref[:, cols] = (mixed / total).astype(out_ref.dtype)
+
+
+def merged_output(block_index, chunk, width, mixed_near, stat_near, o_far, stat_far, previous):
+    rows, chunk_width = mixed_near.shape
+    step_width = HEADS_PER_STEP * HEAD_DIM
+    steps = chunk_width // step_width
+    offset = chunk * steps
+    part = pl.BlockSpec((rows, step_width), lambda g, b: (0, g))
+    whole = pl.BlockSpec((rows, step_width), lambda g, b: (0, g + offset))
+    operands = [block_index, mixed_near, stat_near, o_far, stat_far]
+    in_specs = [part, stat_spec(rows), part, stat_spec(rows)]
+    aliases = {}
+    if previous is not None:
+        in_specs = in_specs + [pl.BlockSpec(memory_space=pl.ANY)]
+        aliases = {len(operands): 0}
+        operands = operands + [previous]
+    return pl.pallas_call(
+        merge_kernel,
+        grid_spec=pltpu.PrefetchScalarGridSpec(
+            num_scalar_prefetch=1,
+            grid=(steps,),
+            in_specs=in_specs,
+            out_specs=whole,
+        ),
+        out_shape=jax.ShapeDtypeStruct((rows, width), jnp.bfloat16),
+        input_output_aliases=aliases,
+    )(*operands)
+
+
 def per_head(stat):
     steps, rows, _ = stat.shape
     stat = jnp.transpose(stat.reshape(steps, rows, 2, HEADS_PER_STEP), (2, 1, 0, 3))
     return stat[0].reshape(rows, steps * HEADS_PER_STEP), stat[1].reshape(rows, steps * HEADS_PER_STEP)
 
 
-def merge(block_index, mixed_near, stat_near, o_far, stat_far):
-    rows, width = mixed_near.shape
-    heads = width // HEAD_DIM
+def log_total(block_index, stat_near, stat_far):
     m_near, l_near = per_head(stat_near)
     m_far, l_far = per_head(stat_far)
     has_far = block_index >= 2
     m = jnp.where(has_far, jnp.maximum(m_near, m_far), m_near)
-    near_scale = jnp.exp(m_near - m)
-    far_scale = jnp.where(has_far, jnp.exp(m_far - m), 0.0)
-    total = near_scale * l_near + far_scale * l_far
-    mixed = (
-        near_scale[:, :, None] * mixed_near.reshape(rows, heads, HEAD_DIM)
-        + far_scale[:, :, None] * o_far.reshape(rows, heads, HEAD_DIM).astype(jnp.float32)
-    )
-    out = (mixed / total[:, :, None]).reshape(rows, width).astype(jnp.bfloat16)
-    return out, jnp.transpose(m + jnp.log(total))
+    total = jnp.exp(m_near - m) * l_near + jnp.where(has_far, jnp.exp(m_far - m), 0.0) * l_far
+    return jnp.transpose(m + jnp.log(total))
 
 
 def shards(att_query, att_key, att_value):
+    width = att_query.shape[1]
+    chunk_width = width // CHUNKS
     block_index = lax.axis_index("ctx").astype(jnp.int32)
-    kv_prev = from_behind(jnp.stack([att_key, att_value]), "ctx")
-    q_next = from_ahead(att_query, "ctx")
-    o_far, stat_far = from_behind(partial_attention(q_next, kv_prev), "ctx")
-    mixed_near, stat_near = near_attention(block_index.reshape(1), att_query, att_key, att_value, kv_prev)
-    return merge(block_index, mixed_near, stat_near, o_far, stat_far)
+    index_ref = block_index.reshape(1)
+    pieces = []
+    for chunk in range(CHUNKS):
+        cols = slice(chunk * chunk_width, (chunk + 1) * chunk_width)
+        q, k, v = att_query[:, cols], att_key[:, cols], att_value[:, cols]
+        kv_prev = from_behind(jnp.stack([k, v]), "ctx")
+        q_next = from_ahead(q, "ctx")
+        after = (pieces[-1][1], pieces[-1][3]) if pieces else ()
+        o_far, stat_far = from_behind(partial_attention(q_next, kv_prev, after), "ctx")
+        mixed_near, stat_near = near_attention(index_ref, q, k, v, kv_prev)
+        pieces.append((mixed_near, stat_near, o_far, stat_far))
+    out = None
+    for chunk in range(CHUNKS):
+        out = merged_output(index_ref, chunk, width, *pieces[chunk], out)
+    stat_near = jnp.concatenate([piece[1] for piece in pieces], axis=0)
+    stat_far = jnp.concatenate([piece[3] for piece in pieces], axis=0)
+    return out, log_total(block_index, stat_near, stat_far)
 
 
 def solution(mesh):

time: 124 us -> 108 us (0.87)
  waiting for transfers between devices: 72.9 us -> 44.2 us
  starting transfers between devices: 21.5 us -> 31.1 us
  other arithmetic: 7.28 us -> 1.82 us
  Pallas kernels: 16.1 us -> 21.3 us
  local copies, waits for them, and re-layouts: 4.96 us -> 7.69 us
    ppermute x3 -> x6, waiting for transfers between devices: 50.5 us -> 35.8 us  [from_behind(): return lax.ppermute(block, axis, route)]
    ppermute x1 -> x2, waiting for transfers between devices: 22.4 us -> 8.38 us  [from_ahead(): return lax.ppermute(block, axis, route)]
    pallas_call x0 -> x2, Pallas kernels: none -> 7.47 us  [merged_output(): pl.pallas_call(merge_kernel, grid_spec=pltpu.PrefetchScalarGridSpec(num_s...]
    ppermute x3 -> x6, starting transfers between devices: 7.23 us -> 14.4 us  [from_behind(): return lax.ppermute(block, axis, route)]
    convert_element_type x1 -> x0, other arithmetic: 4.82 us -> none  [merge(): out = (mixed / total[:, :, None]).reshape(rows, width).astype(jnp.bfloat16)]
    pallas_call x1 -> x2, Pallas kernels: 10.3 us -> 6.79 us  [partial_attention(): pl.pallas_call(partial_kernel, grid=(steps,), in_specs=[block, key_block,...]
    another operation x0 -> x1, local copies, waits for them, and re-layouts: none -> 3.21 us  [shards(): kv_prev = from_behind(jnp.stack([k, v]), 'ctx')]
    ppermute x1 -> x2, starting transfers between devices: 14.2 us -> 16.7 us  [from_ahead(): return lax.ppermute(block, axis, route)]
  transfers between devices with their start and end apart: 4 -> 8, of which waited for: 3 -> 5; matrix products, arithmetic and copies ran while one was open for 2% -> 3% of each run, Pallas kernels for 5% -> 16%
where the time goes in v5:
time: 108 us; the launch traced here: 107 us
  waiting for transfers between devices  44.2 us (41%)
  starting transfers between devices  31.1 us (29%)
  Pallas kernels  21.3 us (20%)
  local copies, waits for them, and re-layouts  7.69 us (7%)
  other arithmetic  1.82 us (2%)
    ppermute x6, waiting for transfers between devices, from_behind(): return lax.ppermute(block, axis, route)  35.8 us
    ppermute x2, starting transfers between devices, from_ahead(): return lax.ppermute(block, axis, route)  16.7 us
    ppermute x6, starting transfers between devices, from_behind(): return lax.ppermute(block, axis, route)  14.4 us
    ppermute x2, waiting for transfers between devices, from_ahead(): return lax.ppermute(block, axis, route)  8.38 us
    pallas_call x2, Pallas kernels, merged_output(): pl.pallas_call(merge_kernel, grid_spec=pltpu.PrefetchScalarGridSpec(num_s...  7.47 us
    pallas_call x2, Pallas kernels, near_attention(): pl.pallas_call(near_kernel, grid_spec=pltpu.PrefetchScalarGridSpec(num_sc...  7.04 us
    pallas_call x2, Pallas kernels, partial_attention(): pl.pallas_call(partial_kernel, grid=(steps,), in_specs=[block, key_block,...  6.79 us
    unnamed x24, local copies, waits for them, and re-layouts  3.24 us
  transfers between devices with their start and end apart: 8, of which 5 were waited for; matrix products, arithmetic and copies ran while one was open for 3% of the time, Pallas kernels for 16%

profile of v5, /device:TPU:56, one launch (start us, length us, event | category | flops | bytes accessed | tf_op | source)
XLA Modules:
  0.0 107.0 jit_solution(11575979175025579255)
XLA Ops:
  0.6 3.2 %slice_bitcast_fusion.4 = (bf16[1,128,2048]{2,1,0:T(8,128)(2,1)S(1)}, bf16[1,128,2048]{2,1,0:T(8,128)(2,1)S(1)}, bf16[128,2048]{1,0:T(8,128)(2,1)}, bf16[128,204...) fusion(bf16[128,4096]{1,0:T(8,128)(2,1)} %param.5, ...), kind=kLoop, calls=%fused_computation.17 | loop fusion | bytes 6291456 | tf_op jit(solution)/shard_map/stack | solution.py:182
  3.8 0.1 pad_maximum_fusion.1
  3.9 3.4 %collective-permute-start.2 = (bf16[2,128,2048]{2,1,0:T(8,128)(2,1)S(1)}, bf16[2,128,2048]{2,1,0:T(8,128)(2,1)S(1)}, u32[]{:S(2)}, u32[]{:S(2)}) collective-permute-start(bf16[2,128,2048]{2,1,0:T(8,128)(2,1)S(1)} %pad_maximum_fusion.1), channel_id=1, source_target_pairs={{0,4},{4,8},{8,12},{12,16},{16,20},{20,24},{24,28},{28,32},{32,36}... | collective-permute-start | bytes 3145736 | tf_op jit(solution)/shard_map/ppermute | solution.py:20
  7.4 1.1 pad_maximum_fusion
  8.4 3.4 %collective-permute-start = (bf16[2,128,2048]{2,1,0:T(8,128)(2,1)}, bf16[2,128,2048]{2,1,0:T(8,128)(2,1)S(1)}, u32[]{:S(2)}, u32[]{:S(2)}) collective-permute-start(bf16[2,128,2048]{2,1,0:T(8,128)(2,1)} %pad_maximum_fusion), channel_id=1, source_target_pairs={{0,4},{4,8},{8,12},{12,16},{16,20},{20,24},{24,28},{28,32},{32,36}... | collective-permute-start | bytes 3145736 | tf_op jit(solution)/shard_map/ppermute | solution.py:20
  11.8 0.1 fusion.8
  11.9 12.7 %collective-permute-start.3 = (bf16[128,2048]{1,0:T(8,128)(2,1)S(1)}, bf16[128,2048]{1,0:T(8,128)(2,1)S(1)}, u32[]{:S(2)}, u32[]{:S(2)}) collective-permute-start(bf16[128,2048]{1,0:T(8,128)(2,1)S(1)} %get-tuple-element.26.q_ref), channel_id=1, source_target_pairs={{4,0},{8,4},{12,8},{16,12},{20,16},{24,20},{28,24},{32,28},{36,32}... | collective-permute-start | bytes 1572872 | tf_op jit(solution)/shard_map/ppermute | solution.py:26
  24.7 3.9 %collective-permute-start.1 = (bf16[128,2048]{1,0:T(8,128)(2,1)S(1)}, bf16[128,2048]{1,0:T(8,128)(2,1)}, u32[]{:S(2)}, u32[]{:S(2)}) collective-permute-start(bf16[128,2048]{1,0:T(8,128)(2,1)S(1)} %get-tuple-element.27.q_ref), channel_id=1, source_target_pairs={{4,0},{8,4},{12,8},{16,12},{20,16},{24,20},{28,24},{32,28},{36,32}... | collective-permute-start | bytes 1572872 | tf_op jit(solution)/shard_map/ppermute | solution.py:26
  28.6 8.4 %collective-permute-done.3.q_ref = bf16[128,2048]{1,0:T(8,128)(2,1)S(1)} collective-permute-done((bf16[128,2048]{1,0:T(8,128)(2,1)S(1)}, bf16[128,2048]{1,0:T(8,128)(2,1)S(1)}, u32[]{:S(2)}, u32[]{:S(2)}) %collective-permute-start.3) | collective-permute-done | bytes 524320 | tf_op jit(solution)/shard_map/ppermute | solution.py:26
  37.0 0.8 copy-done.9
  37.8 5.8 %collective-permute-done.2.kp_ref.vp_ref.k_ref.v_ref = bf16[2,128,2048]{2,1,0:T(8,128)(2,1)S(1)} collective-permute-done((bf16[2,128,2048]{2,1,0:T(8,128)(2,1)S(1)}, bf16[2,128,2048]{2,1,0:T(8,128)(2,1)S(1)}, u32[]{:S(2)}, u32[]{:S(2)}) %collective-permute-start.2) | collective-permute-done | bytes 1048608 | tf_op jit(solution)/shard_map/ppermute | solution.py:20
  43.6 1.0 copy-done
  44.6 3.4 %shard_map.52 = (bf16[128,2048]{1,0:T(8,128)(2,1)}, f32[2,128,16]{2,1,0:T(8,128)}) custom-call(bf16[128,2048]{1,0:T(8,128)(2,1)} %copy-done.9, bf16[2,128,2048]{2,1,0:T(8,128)(2,1)} %copy-done, bf16[2,128,2048]{2,1,0:T(8,128)(2,1)} %copy-done), custom_call_target="tpu_custom_call" | custom-call | tf_op jit(solution)/shard_map/pallas_call | solution.py:80
  48.0 1.9 %collective-permute-start.4 = (f32[2,128,16]{2,1,0:T(8,128)}, f32[2,128,16]{2,1,0:T(8,128)S(1)}, u32[]{:S(2)}, u32[]{:S(2)}) collective-permute-start(f32[2,128,16]{2,1,0:T(8,128)} %get-tuple-element.13), channel_id=1, source_target_pairs={{0,4},{4,8},{8,12},{12,16},{16,20},{20,24},{24,28},{28,32},{32,36}... | collective-permute-start | bytes 49160 | tf_op jit(solution)/shard_map/ppermute | solution.py:20
  49.9 1.9 %collective-permute-start.7 = (bf16[128,2048]{1,0:T(8,128)(2,1)}, bf16[128,2048]{1,0:T(8,128)(2,1)}, u32[]{:S(2)}, u32[]{:S(2)}) collective-permute-start(bf16[128,2048]{1,0:T(8,128)(2,1)} %get-tuple-element.17), channel_id=1, source_target_pairs={{0,4},{4,8},{8,12},{12,16},{16,20},{20,24},{24,28},{28,32},{32,36}... | collective-permute-start | bytes 1572872 | tf_op jit(solution)/shard_map/ppermute | solution.py:20
  51.8 3.5 %shard_map.51 = (f32[128,2048]{1,0:T(8,128)}, f32[2,128,16]{2,1,0:T(8,128)}) custom-call(s32[1]{0:T(128)} %bitcast.block_ref, bf16[128,2048]{1,0:T(8,128)(2,1)} %copy-done.3, bf16[128,2048]{1,0:T(8,128)(2,1)} %get-tuple-element.29.k_ref, bf16[128,2048]{1,0:T(8,128)(2,1)} %get-tuple-element.24.v_ref, bf16[2,128,2048]{2,1,0:T(8,128)(2,1)} %copy-done, ...), custom_call_target="tpu_custom_call" | custom-call | tf_op jit(solution)/shard_map/pallas_call | solution.py:99
  55.4 10.7 %collective-permute-done.kp_ref.vp_ref.k_ref.v_ref = bf16[2,128,2048]{2,1,0:T(8,128)(2,1)S(1)} collective-permute-done((bf16[2,128,2048]{2,1,0:T(8,128)(2,1)}, bf16[2,128,2048]{2,1,0:T(8,128)(2,1)S(1)}, u32[]{:S(2)}, u32[]{:S(2)}) %collective-permute-start) | collective-permute-done | bytes 1048608 | tf_op jit(solution)/shard_map/ppermute | solution.py:20
  66.1 2.8 %collective-permute-done.4.rest_1_.far_ref = f32[2,128,16]{2,1,0:T(8,128)S(1)} collective-permute-done((f32[2,128,16]{2,1,0:T(8,128)}, f32[2,128,16]{2,1,0:T(8,128)S(1)}, u32[]{:S(2)}, u32[]{:S(2)}) %collective-permute-start.4) | collective-permute-done | bytes 16416 | tf_op jit(solution)/shard_map/ppermute | solution.py:20
  68.9 0.6 copy-done.4
  69.5 3.4 %shard_map.53 = (bf16[128,2048]{1,0:T(8,128)(2,1)}, f32[2,128,16]{2,1,0:T(8,128)}) custom-call(bf16[128,2048]{1,0:T(8,128)(2,1)} %collective-permute-done.1.q_ref, bf16[2,128,2048]{2,1,0:T(8,128)(2,1)} %copy-done.1, bf16[2,128,2048]{2,1,0:T(8,128)(2,1)} %copy-done.1, f32[2,128,16]{2,1,0:T(8,128)} %get-tuple-element.12.rest_0_.near_ref, f32[2,128,16]{2,1,0:T(8,128)} %copy-done.4), custom_call_target="tpu_custom_call" | custom-call | tf_op jit(solution)/shard_map/pallas_call | solution.py:80
  73.0 1.9 %collective-permute-start.5 = (bf16[128,2048]{1,0:T(8,128)(2,1)}, bf16[128,2048]{1,0:T(8,128)(2,1)S(1)}, u32[]{:S(2)}, u32[]{:S(2)}) collective-permute-start(bf16[128,2048]{1,0:T(8,128)(2,1)} %get-tuple-element.14), channel_id=1, source_target_pairs={{0,4},{4,8},{8,12},{12,16},{16,20},{20,24},{24,28},{28,32},{32,36}... | collective-permute-start | bytes 1572872 | tf_op jit(solution)/shard_map/ppermute | solution.py:20
  74.9 0.1 copy.12
  75.0 3.5 %shard_map.50 = (f32[128,2048]{1,0:T(8,128)}, f32[2,128,16]{2,1,0:T(8,128)}) custom-call(s32[1]{0:T(128)} %bitcast.block_ref, bf16[128,2048]{1,0:T(8,128)(2,1)} %copy-done.2, bf16[128,2048]{1,0:T(8,128)(2,1)} %get-tuple-element.28.k_ref, bf16[128,2048]{1,0:T(8,128)(2,1)} %get-tuple-element.25.v_ref, bf16[2,128,2048]{2,1,0:T(8,128)(2,1)} %copy-done.1, ...), custom_call_target="tpu_custom_call" | custom-call | tf_op jit(solution)/shard_map/pallas_call | solution.py:99
  78.5 1.0 copy.13
  79.5 1.9 %collective-permute-start.6 = (f32[2,128,16]{2,1,0:T(8,128)S(1)}, f32[2,128,16]{2,1,0:T(8,128)S(1)}, u32[]{:S(2)}, u32[]{:S(2)}) collective-permute-start(f32[2,128,16]{2,1,0:T(8,128)S(1)} %copy-done.11), channel_id=1, source_target_pairs={{0,4},{4,8},{8,12},{12,16},{16,20},{20,24},{24,28},{28,32},{32,36}... | collective-permute-start | bytes 49160 | tf_op jit(solution)/shard_map/ppermute | solution.py:20
  81.4 0.1 copy.14
  81.5 16.4 %collective-permute-done.6.far_ref = f32[2,128,16]{2,1,0:T(8,128)S(1)} collective-permute-done((f32[2,128,16]{2,1,0:T(8,128)S(1)}, f32[2,128,16]{2,1,0:T(8,128)S(1)}, u32[]{:S(2)}, u32[]{:S(2)}) %collective-permute-start.6) | collective-permute-done | bytes 16416 | tf_op jit(solution)/shard_map/ppermute | solution.py:20
  98.0 0.1 copy.15
  98.0 0.6 fusion.4
  98.7 3.7 %shard_map.54.rest_0_ = bf16[128,4096]{1,0:T(8,128)(2,1)} custom-call(s32[1]{0:T(128)} %bitcast.block_ref, f32[128,2048]{1,0:T(8,128)} %get-tuple-element.16.mixed_ref, f32[2,128,16]{2,1,0:T(8,128)} %get-tuple-element.12.rest_0_.near_ref, bf16[128,2048]{1,0:T(8,128)(2,1)} %collective-permute-done.7.o_ref, f32[2,128,16]{2,1,0:T(8,128)} %copy-done.4), custom_call_target="tpu_custom_call" | custom-call | tf_op jit(solution)/shard_map/pallas_call | solution.py:145
  102.4 0.8 copy-done.8
  103.2 3.7 %shard_map.55 = bf16[128,4096]{1,0:T(8,128)(2,1)} custom-call(s32[1]{0:T(128)} %bitcast.block_ref, f32[128,2048]{1,0:T(8,128)} %get-tuple-element.10.mixed_ref, f32[2,128,16]{2,1,0:T(8,128)} %get-tuple-element.11.near_ref, bf16[128,2048]{1,0:T(8,128)(2,1)} %copy-done.8, f32[2,128,16]{2,1,0:T(8,128)} %copy-done.10, ...), custom_call_target="tpu_custom_call", output_to_operand_aliasing={{}: (5, {})} | custom-call | tf_op jit(solution)/shard_map/pallas_call | solution.py:145
  (25 shorter events, 0.1 us)
Async XLA Ops:
  3.9 39.7 %collective-permute-start.2 = (bf16[2,128,2048]{2,1,0:T(8,128)(2,1)S(1)}, bf16[2,128,2048]{2,1,0:T(8,128)(2,1)S(1)}, u32[]{:S(2)}, u32[]{:S(2)}) collective-permute-start(bf16[2,128,2048]{2,1,0:T(8,128)(2,1)S(1)} %pad_maximum_fusion.1), channel_id=1, source_target_pairs={{0,4},{4,8},{8,12},{12,16},{16,20},{20,24},{24,28},{28,32},{32,36}... | collective-permute-start | bytes 3145736 | tf_op jit(solution)/shard_map/ppermute | solution.py:20
  7.3 4.5 %copy-start.7 = (bf16[128,4096]{1,0:T(8,128)(2,1)S(1)}, bf16[128,4096]{1,0:T(8,128)(2,1)}, u32[]{:S(2)}) copy-start(bf16[128,4096]{1,0:T(8,128)(2,1)} %param.3) | copy-start | bytes 3145732
  8.4 57.7 %collective-permute-start = (bf16[2,128,2048]{2,1,0:T(8,128)(2,1)}, bf16[2,128,2048]{2,1,0:T(8,128)(2,1)S(1)}, u32[]{:S(2)}, u32[]{:S(2)}) collective-permute-start(bf16[2,128,2048]{2,1,0:T(8,128)(2,1)} %pad_maximum_fusion), channel_id=1, source_target_pairs={{0,4},{4,8},{8,12},{12,16},{16,20},{20,24},{24,28},{28,32},{32,36}... | collective-permute-start | bytes 3145736 | tf_op jit(solution)/shard_map/ppermute | solution.py:20
  11.9 39.9 %copy-start.3 = (bf16[128,2048]{1,0:T(8,128)(2,1)}, bf16[128,2048]{1,0:T(8,128)(2,1)S(1)}, u32[]{:S(2)}) copy-start(bf16[128,2048]{1,0:T(8,128)(2,1)S(1)} %get-tuple-element.26.q_ref) | copy-start | bytes 1572868
  11.9 43.4 %copy-start.2 = (bf16[128,2048]{1,0:T(8,128)(2,1)}, bf16[128,2048]{1,0:T(8,128)(2,1)S(1)}, u32[]{:S(2)}) copy-start(bf16[128,2048]{1,0:T(8,128)(2,1)S(1)} %get-tuple-element.27.q_ref) | copy-start | bytes 1572868
  11.9 25.1 %collective-permute-start.3 = (bf16[128,2048]{1,0:T(8,128)(2,1)S(1)}, bf16[128,2048]{1,0:T(8,128)(2,1)S(1)}, u32[]{:S(2)}, u32[]{:S(2)}) collective-permute-start(bf16[128,2048]{1,0:T(8,128)(2,1)S(1)} %get-tuple-element.26.q_ref), channel_id=1, source_target_pairs={{4,0},{8,4},{12,8},{16,12},{20,16},{24,20},{28,24},{32,28},{36,32}... | collective-permute-start | bytes 1572872 | tf_op jit(solution)/shard_map/ppermute | solution.py:26
  24.7 30.7 %collective-permute-start.1 = (bf16[128,2048]{1,0:T(8,128)(2,1)S(1)}, bf16[128,2048]{1,0:T(8,128)(2,1)}, u32[]{:S(2)}, u32[]{:S(2)}) collective-permute-start(bf16[128,2048]{1,0:T(8,128)(2,1)S(1)} %get-tuple-element.27.q_ref), channel_id=1, source_target_pairs={{4,0},{8,4},{12,8},{16,12},{20,16},{24,20},{28,24},{32,28},{36,32}... | collective-permute-start | bytes 1572872 | tf_op jit(solution)/shard_map/ppermute | solution.py:26
  37.0 0.8 copy-start.9
  43.6 1.0 copy-start
  48.0 20.9 %collective-permute-start.4 = (f32[2,128,16]{2,1,0:T(8,128)}, f32[2,128,16]{2,1,0:T(8,128)S(1)}, u32[]{:S(2)}, u32[]{:S(2)}) collective-permute-start(f32[2,128,16]{2,1,0:T(8,128)} %get-tuple-element.13), channel_id=1, source_target_pairs={{0,4},{4,8},{8,12},{12,16},{16,20},{20,24},{24,28},{28,32},{32,36}... | collective-permute-start | bytes 49160 | tf_op jit(solution)/shard_map/ppermute | solution.py:20
  49.9 48.8 %collective-permute-start.7 = (bf16[128,2048]{1,0:T(8,128)(2,1)}, bf16[128,2048]{1,0:T(8,128)(2,1)}, u32[]{:S(2)}, u32[]{:S(2)}) collective-permute-start(bf16[128,2048]{1,0:T(8,128)(2,1)} %get-tuple-element.17), channel_id=1, source_target_pairs={{0,4},{4,8},{8,12},{12,16},{16,20},{20,24},{24,28},{28,32},{32,36}... | collective-permute-start | bytes 1572872 | tf_op jit(solution)/shard_map/ppermute | solution.py:20
  66.1 2.8 %copy-start.1 = (bf16[2,128,2048]{2,1,0:T(8,128)(2,1)}, bf16[2,128,2048]{2,1,0:T(8,128)(2,1)S(1)}, u32[]{:S(2)}) copy-start(bf16[2,128,2048]{2,1,0:T(8,128)(2,1)S(1)} %collective-permute-done.kp_ref.vp_ref.k_ref.v_ref) | copy-start | bytes 3145732
  68.9 0.6 copy-start.4
  69.5 5.3 %copy-start.6 = (f32[2,128,16]{2,1,0:T(8,128)S(1)}, f32[2,128,16]{2,1,0:T(8,128)}, u32[]{:S(2)}) copy-start(f32[2,128,16]{2,1,0:T(8,128)} %get-tuple-element.12.rest_0_.near_ref) | copy-start | bytes 49156
  73.0 29.5 %collective-permute-start.5 = (bf16[128,2048]{1,0:T(8,128)(2,1)}, bf16[128,2048]{1,0:T(8,128)(2,1)S(1)}, u32[]{:S(2)}, u32[]{:S(2)}) collective-permute-start(bf16[128,2048]{1,0:T(8,128)(2,1)} %get-tuple-element.14), channel_id=1, source_target_pairs={{0,4},{4,8},{8,12},{12,16},{16,20},{20,24},{24,28},{28,32},{32,36}... | collective-permute-start | bytes 1572872 | tf_op jit(solution)/shard_map/ppermute | solution.py:20
  74.9 4.5 %copy-start.11 = (f32[2,128,16]{2,1,0:T(8,128)S(1)}, f32[2,128,16]{2,1,0:T(8,128)}, u32[]{:S(2)}) copy-start(f32[2,128,16]{2,1,0:T(8,128)} %get-tuple-element.15) | copy-start | bytes 49156
  78.5 2.9 %copy-start.5 = (f32[2,128,16]{2,1,0:T(8,128)S(1)}, f32[2,128,16]{2,1,0:T(8,128)}, u32[]{:S(2)}) copy-start(f32[2,128,16]{2,1,0:T(8,128)} %copy-done.4) | copy-start | bytes 49156
  79.5 18.5 %collective-permute-start.6 = (f32[2,128,16]{2,1,0:T(8,128)S(1)}, f32[2,128,16]{2,1,0:T(8,128)S(1)}, u32[]{:S(2)}, u32[]{:S(2)}) collective-permute-start(f32[2,128,16]{2,1,0:T(8,128)S(1)} %copy-done.11), channel_id=1, source_target_pairs={{0,4},{4,8},{8,12},{12,16},{16,20},{20,24},{24,28},{28,32},{32,36}... | collective-permute-start | bytes 49160 | tf_op jit(solution)/shard_map/ppermute | solution.py:20
  98.0 0.7 copy-start.10
  102.4 0.8 copy-start.8

commit v6 on v5

--- a/solution.py
+++ b/solution.py
@@ -114,18 +114,23 @@
 def merge_kernel(block_ref, mixed_ref, near_ref, o_ref, far_ref, *rest):
     out_ref = rest[-1]
     has_far = block_ref[0] >= 2
-    for h in range(HEADS_PER_STEP):
+    n = HEADS_PER_STEP
+    near = near_ref[...]
+    far = far_ref[...]
+    m_near, l_near = near[:, :n], near[:, n:]
+    m_far, l_far = far[:, :n], far[:, n:]
+    m = jnp.where(has_far, jnp.maximum(m_near, m_far), m_near)
+    near_scale = jnp.exp(m_near - m)
+    far_scale = jnp.where(has_far, jnp.exp(m_far - m), 0.0)
+    inverse = 1.0 / (near_scale * l_near + far_scale * l_far)
+    near_scale = near_scale * inverse
+    far_scale = far_scale * inverse
+    for h in range(n):
         cols = slice(h * HEAD_DIM, (h + 1) * HEAD_DIM)
-        m_near = near_ref[:, h : h + 1]
-        m_far = far_ref[:, h : h + 1]
-        l_near = near_ref[:, HEADS_PER_STEP + h : HEADS_PER_STEP + h + 1]
-        l_far = far_ref[:, HEADS_PER_STEP + h : HEADS_PER_STEP + h + 1]
-        m = jnp.where(has_far, jnp.maximum(m_near, m_far), m_near)
-        near_scale = jnp.exp(m_near - m)
-        far_scale = jnp.where(has_far, jnp.exp(m_far - m), 0.0)
-        total = near_scale * l_near + far_scale * l_far
-        mixed = near_scale * mixed_ref[:, cols] + far_scale * o_ref[:, cols].astype(jnp.float32)
-        out_ref[:, cols] = (mixed / total).astype(out_ref.dtype)
+        mixed = near_scale[:, h : h + 1] * mixed_ref[:, cols] + far_scale[:, h : h + 1] * o_ref[:, cols].astype(
+            jnp.float32
+        )
+        out_ref[:, cols] = mixed.astype(out_ref.dtype)
 
 
 def merged_output(block_index, chunk, width, mixed_near, stat_near, o_far, stat_far, previous):
@@ -176,18 +181,22 @@
     block_index = lax.axis_index("ctx").astype(jnp.int32)
     index_ref = block_index.reshape(1)
     pieces = []
+    out = None
     for chunk in range(CHUNKS):
         cols = slice(chunk * chunk_width, (chunk + 1) * chunk_width)
         q, k, v = att_query[:, cols], att_key[:, cols], att_value[:, cols]
         kv_prev = from_behind(jnp.stack([k, v]), "ctx")
         q_next = from_ahead(q, "ctx")
         after = (pieces[-1][1], pieces[-1][3]) if pieces else ()
-        o_far, stat_far = from_behind(partial_attention(q_next, kv_prev, after), "ctx")
+        o_part, stat_part = partial_attention(q_next, kv_prev, after)
+        o_far = from_behind(o_part, "ctx")
         mixed_near, stat_near = near_attention(index_ref, q, k, v, kv_prev)
+        if pieces:
+            out = merged_output(index_ref, chunk - 1, width, *pieces[-1], out)
+            stat_part, out = lax.optimization_barrier((stat_part, out))
+        stat_far = from_behind(stat_part, "ctx")
         pieces.append((mixed_near, stat_near, o_far, stat_far))
-    out = None
-    for chunk in range(CHUNKS):
-        out = merged_output(index_ref, chunk, width, *pieces[chunk], out)
+    out = merged_output(index_ref, CHUNKS - 1, width, *pieces[-1], out)
     stat_near = jnp.concatenate([piece[1] for piece in pieces], axis=0)
     stat_far = jnp.concatenate([piece[3] for piece in pieces], axis=0)
     return out, log_total(block_index, stat_near, stat_far)

time: 108 us -> 114 us (1.056)
  waiting for transfers between devices: 44.2 us -> 52.6 us
  Pallas kernels: 21.3 us -> 19.5 us
    ppermute x6, waiting for transfers between devices: 35.8 us -> 44.2 us  [from_behind(): return lax.ppermute(block, axis, route)]
    pallas_call x2, Pallas kernels: 7.47 us -> 5.67 us  [merged_output(): pl.pallas_call(merge_kernel, grid_spec=pltpu.PrefetchScalarGridSpec(num_s...]
  transfers between devices with their start and end apart: 8 -> 8, of which waited for: 5 -> 5; matrix products, arithmetic and copies ran while one was open for 3% -> 3% of each run, Pallas kernels for 16% -> 15%
where the time goes in v6:
time: 114 us; the launch traced here: 113 us
  waiting for transfers between devices  52.6 us (46%)
  starting transfers between devices  31.1 us (27%)
  Pallas kernels  19.5 us (17%)
  local copies, waits for them, and re-layouts  7.67 us (7%)
  other arithmetic  1.82 us (2%)
    ppermute x6, waiting for transfers between devices, from_behind(): return lax.ppermute(block, axis, route)  44.2 us
    ppermute x2, starting transfers between devices, from_ahead(): return lax.ppermute(block, axis, route)  16.7 us
    ppermute x6, starting transfers between devices, from_behind(): return lax.ppermute(block, axis, route)  14.4 us
    ppermute x2, waiting for transfers between devices, from_ahead(): return lax.ppermute(block, axis, route)  8.38 us
    pallas_call x2, Pallas kernels, near_attention(): pl.pallas_call(near_kernel, grid_spec=pltpu.PrefetchScalarGridSpec(num_sc...  7 us
    pallas_call x2, Pallas kernels, partial_attention(): pl.pallas_call(partial_kernel, grid=(steps,), in_specs=[block, key_block,...  6.8 us
    pallas_call x2, Pallas kernels, merged_output(): pl.pallas_call(merge_kernel, grid_spec=pltpu.PrefetchScalarGridSpec(num_s...  5.67 us
    unnamed x24, local copies, waits for them, and re-layouts  3.25 us
  transfers between devices with their start and end apart: 8, of which 5 were waited for; matrix products, arithmetic and copies ran while one was open for 3% of the time, Pallas kernels for 15%

profile of v6, /device:TPU:56, one launch (start us, length us, event | category | flops | bytes accessed | tf_op | source)
XLA Modules:
  0.0 113.5 jit_solution(6847722192649264340)
XLA Ops:
  0.6 3.2 %slice_bitcast_fusion.4 = (bf16[1,128,2048]{2,1,0:T(8,128)(2,1)S(1)}, bf16[1,128,2048]{2,1,0:T(8,128)(2,1)S(1)}, bf16[128,2048]{1,0:T(8,128)(2,1)}, bf16[128,204...) fusion(bf16[128,4096]{1,0:T(8,128)(2,1)} %param.5, ...), kind=kLoop, calls=%fused_computation.17 | loop fusion | bytes 6291456 | tf_op jit(solution)/shard_map/stack | solution.py:188
  3.8 0.1 pad_maximum_fusion.1
  3.9 3.4 %collective-permute-start.2 = (bf16[2,128,2048]{2,1,0:T(8,128)(2,1)S(1)}, bf16[2,128,2048]{2,1,0:T(8,128)(2,1)S(1)}, u32[]{:S(2)}, u32[]{:S(2)}) collective-permute-start(bf16[2,128,2048]{2,1,0:T(8,128)(2,1)S(1)} %pad_maximum_fusion.1), channel_id=1, source_target_pairs={{0,4},{4,8},{8,12},{12,16},{16,20},{20,24},{24,28},{28,32},{32,36}... | collective-permute-start | bytes 3145736 | tf_op jit(solution)/shard_map/ppermute | solution.py:20
  7.4 1.1 pad_maximum_fusion
  8.4 3.4 %collective-permute-start = (bf16[2,128,2048]{2,1,0:T(8,128)(2,1)}, bf16[2,128,2048]{2,1,0:T(8,128)(2,1)S(1)}, u32[]{:S(2)}, u32[]{:S(2)}) collective-permute-start(bf16[2,128,2048]{2,1,0:T(8,128)(2,1)} %pad_maximum_fusion), channel_id=1, source_target_pairs={{0,4},{4,8},{8,12},{12,16},{16,20},{20,24},{24,28},{28,32},{32,36}... | collective-permute-start | bytes 3145736 | tf_op jit(solution)/shard_map/ppermute | solution.py:20
  11.8 0.1 fusion.8
  11.9 12.7 %collective-permute-start.3 = (bf16[128,2048]{1,0:T(8,128)(2,1)S(1)}, bf16[128,2048]{1,0:T(8,128)(2,1)S(1)}, u32[]{:S(2)}, u32[]{:S(2)}) collective-permute-start(bf16[128,2048]{1,0:T(8,128)(2,1)S(1)} %get-tuple-element.30.q_ref), channel_id=1, source_target_pairs={{4,0},{8,4},{12,8},{16,12},{20,16},{24,20},{28,24},{32,28},{36,32}... | collective-permute-start | bytes 1572872 | tf_op jit(solution)/shard_map/ppermute | solution.py:26
  24.7 3.9 %collective-permute-start.1 = (bf16[128,2048]{1,0:T(8,128)(2,1)S(1)}, bf16[128,2048]{1,0:T(8,128)(2,1)}, u32[]{:S(2)}, u32[]{:S(2)}) collective-permute-start(bf16[128,2048]{1,0:T(8,128)(2,1)S(1)} %get-tuple-element.31.q_ref), channel_id=1, source_target_pairs={{4,0},{8,4},{12,8},{16,12},{20,16},{24,20},{28,24},{32,28},{36,32}... | collective-permute-start | bytes 1572872 | tf_op jit(solution)/shard_map/ppermute | solution.py:26
  28.6 8.4 %collective-permute-done.3.q_ref = bf16[128,2048]{1,0:T(8,128)(2,1)S(1)} collective-permute-done((bf16[128,2048]{1,0:T(8,128)(2,1)S(1)}, bf16[128,2048]{1,0:T(8,128)(2,1)S(1)}, u32[]{:S(2)}, u32[]{:S(2)}) %collective-permute-start.3) | collective-permute-done | bytes 524320 | tf_op jit(solution)/shard_map/ppermute | solution.py:26
  37.0 0.8 copy-done.9
  37.8 5.8 %collective-permute-done.2.kp_ref.vp_ref.k_ref.v_ref = bf16[2,128,2048]{2,1,0:T(8,128)(2,1)S(1)} collective-permute-done((bf16[2,128,2048]{2,1,0:T(8,128)(2,1)S(1)}, bf16[2,128,2048]{2,1,0:T(8,128)(2,1)S(1)}, u32[]{:S(2)}, u32[]{:S(2)}) %collective-permute-start.2) | collective-permute-done | bytes 1048608 | tf_op jit(solution)/shard_map/ppermute | solution.py:20
  43.6 1.0 copy-done
  44.6 3.4 %shard_map.52 = (bf16[128,2048]{1,0:T(8,128)(2,1)}, f32[2,128,16]{2,1,0:T(8,128)}) custom-call(bf16[128,2048]{1,0:T(8,128)(2,1)} %copy-done.9, bf16[2,128,2048]{2,1,0:T(8,128)(2,1)} %copy-done, bf16[2,128,2048]{2,1,0:T(8,128)(2,1)} %copy-done), custom_call_target="tpu_custom_call" | custom-call | tf_op jit(solution)/shard_map/pallas_call | solution.py:80
  48.0 1.9 %collective-permute-start.6 = (bf16[128,2048]{1,0:T(8,128)(2,1)}, bf16[128,2048]{1,0:T(8,128)(2,1)}, u32[]{:S(2)}, u32[]{:S(2)}) collective-permute-start(bf16[128,2048]{1,0:T(8,128)(2,1)} %get-tuple-element.19), channel_id=1, source_target_pairs={{0,4},{4,8},{8,12},{12,16},{16,20},{20,24},{24,28},{28,32},{32,36}... | collective-permute-start | bytes 1572872 | tf_op jit(solution)/shard_map/ppermute | solution.py:20
  49.9 1.9 %collective-permute-start.4 = (f32[2,128,16]{2,1,0:T(8,128)}, f32[2,128,16]{2,1,0:T(8,128)S(1)}, u32[]{:S(2)}, u32[]{:S(2)}) collective-permute-start(f32[2,128,16]{2,1,0:T(8,128)} %get-tuple-element.15), channel_id=1, source_target_pairs={{0,4},{4,8},{8,12},{12,16},{16,20},{20,24},{24,28},{28,32},{32,36}... | collective-permute-start | bytes 49160 | tf_op jit(solution)/shard_map/ppermute | solution.py:20
  51.8 3.5 %shard_map.51 = (f32[128,2048]{1,0:T(8,128)}, f32[2,128,16]{2,1,0:T(8,128)}) custom-call(s32[1]{0:T(128)} %bitcast.block_ref, bf16[128,2048]{1,0:T(8,128)(2,1)} %copy-done.3, bf16[128,2048]{1,0:T(8,128)(2,1)} %get-tuple-element.33.k_ref, bf16[128,2048]{1,0:T(8,128)(2,1)} %get-tuple-element.28.v_ref, bf16[2,128,2048]{2,1,0:T(8,128)(2,1)} %copy-done, ...), custom_call_target="tpu_custom_call" | custom-call | tf_op jit(solution)/shard_map/pallas_call | solution.py:99
  55.4 10.7 %collective-permute-done.kp_ref.vp_ref.k_ref.v_ref = bf16[2,128,2048]{2,1,0:T(8,128)(2,1)S(1)} collective-permute-done((bf16[2,128,2048]{2,1,0:T(8,128)(2,1)}, bf16[2,128,2048]{2,1,0:T(8,128)(2,1)S(1)}, u32[]{:S(2)}, u32[]{:S(2)}) %collective-permute-start) | collective-permute-done | bytes 1048608 | tf_op jit(solution)/shard_map/ppermute | solution.py:20
  66.1 13.2 %collective-permute-done.4.rest_1_.far_ref = f32[2,128,16]{2,1,0:T(8,128)S(1)} collective-permute-done((f32[2,128,16]{2,1,0:T(8,128)}, f32[2,128,16]{2,1,0:T(8,128)S(1)}, u32[]{:S(2)}, u32[]{:S(2)}) %collective-permute-start.4) | collective-permute-done | bytes 16416 | tf_op jit(solution)/shard_map/ppermute | solution.py:20
  79.3 0.6 copy-done.4
  80.0 3.4 %shard_map.53 = (bf16[128,2048]{1,0:T(8,128)(2,1)}, f32[2,128,16]{2,1,0:T(8,128)}) custom-call(bf16[128,2048]{1,0:T(8,128)(2,1)} %collective-permute-done.1.q_ref, bf16[2,128,2048]{2,1,0:T(8,128)(2,1)} %copy-done.1, bf16[2,128,2048]{2,1,0:T(8,128)(2,1)} %copy-done.1, f32[2,128,16]{2,1,0:T(8,128)} %get-tuple-element.14.rest_0_.near_ref, f32[2,128,16]{2,1,0:T(8,128)} %copy-done.4), custom_call_target="tpu_custom_call" | custom-call | tf_op jit(solution)/shard_map/pallas_call | solution.py:80
  83.4 1.9 %collective-permute-start.5 = (bf16[128,2048]{1,0:T(8,128)(2,1)}, bf16[128,2048]{1,0:T(8,128)(2,1)S(1)}, u32[]{:S(2)}, u32[]{:S(2)}) collective-permute-start(bf16[128,2048]{1,0:T(8,128)(2,1)} %get-tuple-element.16), channel_id=1, source_target_pairs={{0,4},{4,8},{8,12},{12,16},{16,20},{20,24},{24,28},{28,32},{32,36}... | collective-permute-start | bytes 1572872 | tf_op jit(solution)/shard_map/ppermute | solution.py:20
  85.3 0.1 copy.12
  85.4 3.5 %shard_map.50 = (f32[128,2048]{1,0:T(8,128)}, f32[2,128,16]{2,1,0:T(8,128)}) custom-call(s32[1]{0:T(128)} %bitcast.block_ref, bf16[128,2048]{1,0:T(8,128)(2,1)} %copy-done.2, bf16[128,2048]{1,0:T(8,128)(2,1)} %get-tuple-element.32.k_ref, bf16[128,2048]{1,0:T(8,128)(2,1)} %get-tuple-element.29.v_ref, bf16[2,128,2048]{2,1,0:T(8,128)(2,1)} %copy-done.1, ...), custom_call_target="tpu_custom_call" | custom-call | tf_op jit(solution)/shard_map/pallas_call | solution.py:99
  88.9 1.0 copy.13
  89.8 2.9 %shard_map.54.rest_0_ = bf16[128,4096]{1,0:T(8,128)(2,1)} custom-call(s32[1]{0:T(128)} %bitcast.block_ref, f32[128,2048]{1,0:T(8,128)} %get-tuple-element.18.mixed_ref, f32[2,128,16]{2,1,0:T(8,128)} %get-tuple-element.14.rest_0_.near_ref, bf16[128,2048]{1,0:T(8,128)(2,1)} %collective-permute-done.6.o_ref, f32[2,128,16]{2,1,0:T(8,128)} %copy-done.4), custom_call_target="tpu_custom_call" | custom-call | tf_op jit(solution)/shard_map/pallas_call | solution.py:150
  92.7 1.9 %collective-permute-start.7 = (f32[2,128,16]{2,1,0:T(8,128)S(1)}, f32[2,128,16]{2,1,0:T(8,128)S(1)}, u32[]{:S(2)}, u32[]{:S(2)}) collective-permute-start(f32[2,128,16]{2,1,0:T(8,128)S(1)} %copy-done.11), channel_id=1, source_target_pairs={{0,4},{4,8},{8,12},{12,16},{16,20},{20,24},{24,28},{28,32},{32,36}... | collective-permute-start | bytes 49160 | tf_op jit(solution)/shard_map/ppermute | solution.py:20
  94.7 0.1 copy.14
  94.7 14.5 %collective-permute-done.7.far_ref = f32[2,128,16]{2,1,0:T(8,128)S(1)} collective-permute-done((f32[2,128,16]{2,1,0:T(8,128)S(1)}, f32[2,128,16]{2,1,0:T(8,128)S(1)}, u32[]{:S(2)}, u32[]{:S(2)}) %collective-permute-start.7) | collective-permute-done | bytes 16416 | tf_op jit(solution)/shard_map/ppermute | solution.py:20
  109.2 0.1 copy.15
  109.3 0.6 fusion.4
  109.9 0.8 copy-done.8
  110.7 2.8 %shard_map.55 = bf16[128,4096]{1,0:T(8,128)(2,1)} custom-call(s32[1]{0:T(128)} %bitcast.block_ref, f32[128,2048]{1,0:T(8,128)} %get-tuple-element.12.mixed_ref, f32[2,128,16]{2,1,0:T(8,128)} %get-tuple-element.13.near_ref, bf16[128,2048]{1,0:T(8,128)(2,1)} %copy-done.8, f32[2,128,16]{2,1,0:T(8,128)} %copy-done.10, ...), custom_call_target="tpu_custom_call", output_to_operand_aliasing={{}: (5, {})} | custom-call | tf_op jit(solution)/shard_map/pallas_call | solution.py:150
  (25 shorter events, 0.1 us)
Async XLA Ops:
  3.9 39.7 %collective-permute-start.2 = (bf16[2,128,2048]{2,1,0:T(8,128)(2,1)S(1)}, bf16[2,128,2048]{2,1,0:T(8,128)(2,1)S(1)}, u32[]{:S(2)}, u32[]{:S(2)}) collective-permute-start(bf16[2,128,2048]{2,1,0:T(8,128)(2,1)S(1)} %pad_maximum_fusion.1), channel_id=1, source_target_pairs={{0,4},{4,8},{8,12},{12,16},{16,20},{20,24},{24,28},{28,32},{32,36}... | collective-permute-start | bytes 3145736 | tf_op jit(solution)/shard_map/ppermute | solution.py:20
  7.3 4.5 %copy-start.7 = (bf16[128,4096]{1,0:T(8,128)(2,1)S(1)}, bf16[128,4096]{1,0:T(8,128)(2,1)}, u32[]{:S(2)}) copy-start(bf16[128,4096]{1,0:T(8,128)(2,1)} %param.3) | copy-start | bytes 3145732
  8.4 57.7 %collective-permute-start = (bf16[2,128,2048]{2,1,0:T(8,128)(2,1)}, bf16[2,128,2048]{2,1,0:T(8,128)(2,1)S(1)}, u32[]{:S(2)}, u32[]{:S(2)}) collective-permute-start(bf16[2,128,2048]{2,1,0:T(8,128)(2,1)} %pad_maximum_fusion), channel_id=1, source_target_pairs={{0,4},{4,8},{8,12},{12,16},{16,20},{20,24},{24,28},{28,32},{32,36}... | collective-permute-start | bytes 3145736 | tf_op jit(solution)/shard_map/ppermute | solution.py:20
  11.9 39.9 %copy-start.3 = (bf16[128,2048]{1,0:T(8,128)(2,1)}, bf16[128,2048]{1,0:T(8,128)(2,1)S(1)}, u32[]{:S(2)}) copy-start(bf16[128,2048]{1,0:T(8,128)(2,1)S(1)} %get-tuple-element.30.q_ref) | copy-start | bytes 1572868
  11.9 43.4 %copy-start.2 = (bf16[128,2048]{1,0:T(8,128)(2,1)}, bf16[128,2048]{1,0:T(8,128)(2,1)S(1)}, u32[]{:S(2)}) copy-start(bf16[128,2048]{1,0:T(8,128)(2,1)S(1)} %get-tuple-element.31.q_ref) | copy-start | bytes 1572868
  11.9 25.1 %collective-permute-start.3 = (bf16[128,2048]{1,0:T(8,128)(2,1)S(1)}, bf16[128,2048]{1,0:T(8,128)(2,1)S(1)}, u32[]{:S(2)}, u32[]{:S(2)}) collective-permute-start(bf16[128,2048]{1,0:T(8,128)(2,1)S(1)} %get-tuple-element.30.q_ref), channel_id=1, source_target_pairs={{4,0},{8,4},{12,8},{16,12},{20,16},{24,20},{28,24},{32,28},{36,32}... | collective-permute-start | bytes 1572872 | tf_op jit(solution)/shard_map/ppermute | solution.py:26
  24.7 30.7 %collective-permute-start.1 = (bf16[128,2048]{1,0:T(8,128)(2,1)S(1)}, bf16[128,2048]{1,0:T(8,128)(2,1)}, u32[]{:S(2)}, u32[]{:S(2)}) collective-permute-start(bf16[128,2048]{1,0:T(8,128)(2,1)S(1)} %get-tuple-element.31.q_ref), channel_id=1, source_target_pairs={{4,0},{8,4},{12,8},{16,12},{20,16},{24,20},{28,24},{32,28},{36,32}... | collective-permute-start | bytes 1572872 | tf_op jit(solution)/shard_map/ppermute | solution.py:26
  37.0 0.8 copy-start.9
  43.6 1.0 copy-start
  48.0 41.8 %collective-permute-start.6 = (bf16[128,2048]{1,0:T(8,128)(2,1)}, bf16[128,2048]{1,0:T(8,128)(2,1)}, u32[]{:S(2)}, u32[]{:S(2)}) collective-permute-start(bf16[128,2048]{1,0:T(8,128)(2,1)} %get-tuple-element.19), channel_id=1, source_target_pairs={{0,4},{4,8},{8,12},{12,16},{16,20},{20,24},{24,28},{28,32},{32,36}... | collective-permute-start | bytes 1572872 | tf_op jit(solution)/shard_map/ppermute | solution.py:20
  49.9 29.4 %collective-permute-start.4 = (f32[2,128,16]{2,1,0:T(8,128)}, f32[2,128,16]{2,1,0:T(8,128)S(1)}, u32[]{:S(2)}, u32[]{:S(2)}) collective-permute-start(f32[2,128,16]{2,1,0:T(8,128)} %get-tuple-element.15), channel_id=1, source_target_pairs={{0,4},{4,8},{8,12},{12,16},{16,20},{20,24},{24,28},{28,32},{32,36}... | collective-permute-start | bytes 49160 | tf_op jit(solution)/shard_map/ppermute | solution.py:20
  66.1 13.2 %copy-start.1 = (bf16[2,128,2048]{2,1,0:T(8,128)(2,1)}, bf16[2,128,2048]{2,1,0:T(8,128)(2,1)S(1)}, u32[]{:S(2)}) copy-start(bf16[2,128,2048]{2,1,0:T(8,128)(2,1)S(1)} %collective-permute-done.kp_ref.vp_ref.k_ref.v_ref) | copy-start | bytes 3145732
  79.3 0.6 copy-start.4
  80.0 5.3 %copy-start.6 = (f32[2,128,16]{2,1,0:T(8,128)S(1)}, f32[2,128,16]{2,1,0:T(8,128)}, u32[]{:S(2)}) copy-start(f32[2,128,16]{2,1,0:T(8,128)} %get-tuple-element.14.rest_0_.near_ref) | copy-start | bytes 49156
  83.4 26.5 %collective-permute-start.5 = (bf16[128,2048]{1,0:T(8,128)(2,1)}, bf16[128,2048]{1,0:T(8,128)(2,1)S(1)}, u32[]{:S(2)}, u32[]{:S(2)}) collective-permute-start(bf16[128,2048]{1,0:T(8,128)(2,1)} %get-tuple-element.16), channel_id=1, source_target_pairs={{0,4},{4,8},{8,12},{12,16},{16,20},{20,24},{24,28},{28,32},{32,36}... | collective-permute-start | bytes 1572872 | tf_op jit(solution)/shard_map/ppermute | solution.py:20
  89.8 2.9 %copy-start.11 = (f32[2,128,16]{2,1,0:T(8,128)S(1)}, f32[2,128,16]{2,1,0:T(8,128)}, u32[]{:S(2)}) copy-start(f32[2,128,16]{2,1,0:T(8,128)} %get-tuple-element.20) | copy-start | bytes 49156
  89.8 4.8 %copy-start.5 = (f32[2,128,16]{2,1,0:T(8,128)S(1)}, f32[2,128,16]{2,1,0:T(8,128)}, u32[]{:S(2)}) copy-start(f32[2,128,16]{2,1,0:T(8,128)} %copy-done.4) | copy-start | bytes 49156
  92.7 16.5 %collective-permute-start.7 = (f32[2,128,16]{2,1,0:T(8,128)S(1)}, f32[2,128,16]{2,1,0:T(8,128)S(1)}, u32[]{:S(2)}, u32[]{:S(2)}) collective-permute-start(f32[2,128,16]{2,1,0:T(8,128)S(1)} %copy-done.11), channel_id=1, source_target_pairs={{0,4},{4,8},{8,12},{12,16},{16,20},{20,24},{24,28},{28,32},{32,36}... | collective-permute-start | bytes 49160 | tf_op jit(solution)/shard_map/ppermute | solution.py:20
  109.2 0.7 copy-start.10
  109.9 0.8 copy-start.8

commit v7 on v6

--- a/solution.py
+++ b/solution.py
@@ -46,7 +46,8 @@
         stat_ref[:, HEADS_PER_STEP + h : HEADS_PER_STEP + h + 1] = total[:, 0:1]
 
 
-def near_kernel(block_ref, q_ref, k_ref, v_ref, kp_ref, vp_ref, mixed_ref, stat_ref):
+def near_kernel(block_ref, q_ref, k_ref, v_ref, kp_ref, vp_ref, *rest):
+    mixed_ref, stat_ref = rest[-2:]
     rows = q_ref.shape[0]
     row_id = lax.broadcasted_iota(jnp.int32, (rows, 2 * rows), 0)
     col_id = lax.broadcasted_iota(jnp.int32, (rows, 2 * rows), 1)
@@ -89,7 +90,7 @@
     )(q, kv, kv, *after)
 
 
-def near_attention(block_index, q, k, v, kv_prev):
+def near_attention(block_index, q, k, v, kv_prev, after=()):
     rows, width = q.shape
     step_width = HEADS_PER_STEP * HEAD_DIM
     steps = width // step_width
@@ -101,14 +102,14 @@
         grid_spec=pltpu.PrefetchScalarGridSpec(
             num_scalar_prefetch=1,
             grid=(steps,),
-            in_specs=[block] * 3 + [key_block, value_block],
+            in_specs=[block] * 3 + [key_block, value_block] + [pl.BlockSpec(memory_space=pl.ANY)] * len(after),
             out_specs=[block, stat_spec(rows)],
         ),
         out_shape=[
             jax.ShapeDtypeStruct((rows, width), jnp.float32),
             jax.ShapeDtypeStruct((steps, rows, 2 * HEADS_PER_STEP), jnp.float32),
         ],
-    )(block_index, q, k, v, kv_prev, kv_prev)
+    )(block_index, q, k, v, kv_prev, kv_prev, *after)
 
 
 def merge_kernel(block_ref, mixed_ref, near_ref, o_ref, far_ref, *rest):
@@ -189,16 +190,18 @@
         q_next = from_ahead(q, "ctx")
         after = (pieces[-1][1], pieces[-1][3]) if pieces else ()
         o_part, stat_part = partial_attention(q_next, kv_prev, after)
-        o_far = from_behind(o_part, "ctx")
-        mixed_near, stat_near = near_attention(index_ref, q, k, v, kv_prev)
+        stat_far = from_behind(stat_part, "ctx")
         if pieces:
             out = merged_output(index_ref, chunk - 1, width, *pieces[-1], out)
-            stat_part, out = lax.optimization_barrier((stat_part, out))
-        stat_far = from_behind(stat_part, "ctx")
+        mixed_near, stat_near = near_attention(index_ref, q, k, v, kv_prev, () if out is None else (out,))
+        if chunk < CHUNKS - 1:
+            o_part, stat_far, mixed_near, stat_near = lax.optimization_barrier((o_part, stat_far, mixed_near, stat_near))
+        o_far = from_behind(o_part, "ctx")
         pieces.append((mixed_near, stat_near, o_far, stat_far))
     out = merged_output(index_ref, CHUNKS - 1, width, *pieces[-1], out)
-    stat_near = jnp.concatenate([piece[1] for piece in pieces], axis=0)
-    stat_far = jnp.concatenate([piece[3] for piece in pieces], axis=0)
+    out, stats = lax.optimization_barrier((out, [(piece[1], piece[3]) for piece in pieces]))
+    stat_near = jnp.concatenate([piece[0] for piece in stats], axis=0)
+    stat_far = jnp.concatenate([piece[1] for piece in stats], axis=0)
     return out, log_total(block_index, stat_near, stat_far)
 
 

time: 114 us -> 111 us (0.974)
  waiting for transfers between devices: 52.6 us -> 48.4 us
    ppermute x6, waiting for transfers between devices: 44.2 us -> 40 us  [from_behind(): return lax.ppermute(block, axis, route)]
    another operation x1 -> x0, local copies, waits for them, and re-layouts: 3.21 us -> none  [shards(): kv_prev = from_behind(jnp.stack([k, v]), 'ctx')]
    slice x1 -> x2, local copies, waits for them, and re-layouts: 0.07 us -> 3.11 us  [shards(): q, k, v = (att_query[:, cols], att_key[:, cols], att_value[:, cols])]
    unnamed x24 -> x30, local copies, waits for them, and re-layouts: 3.25 us -> 5.18 us
  transfers between devices with their start and end apart: 8 -> 8, of which waited for: 5 -> 5; matrix products, arithmetic and copies ran while one was open for 3% -> 1% of each run, Pallas kernels for 15% -> 15%
where the time goes in v7:
time: 111 us; the launch traced here: 110 us
  waiting for transfers between devices  48.4 us (44%)
  starting transfers between devices  31.1 us (28%)
  Pallas kernels  19.5 us (18%)
  local copies, waits for them, and re-layouts  8.53 us (8%)
  other arithmetic  1.81 us (2%)
    ppermute x6, waiting for transfers between devices, from_behind(): return lax.ppermute(block, axis, route)  40 us
    ppermute x2, starting transfers between devices, from_ahead(): return lax.ppermute(block, axis, route)  16.7 us
    ppermute x6, starting transfers between devices, from_behind(): return lax.ppermute(block, axis, route)  14.4 us
    ppermute x2, waiting for transfers between devices, from_ahead(): return lax.ppermute(block, axis, route)  8.38 us
    pallas_call x2, Pallas kernels, near_attention(): pl.pallas_call(near_kernel, grid_spec=pltpu.PrefetchScalarGridSpec(num_sc...  7.11 us
    pallas_call x2, Pallas kernels, partial_attention(): pl.pallas_call(partial_kernel, grid=(steps,), in_specs=[block, key_block,...  6.76 us
    pallas_call x2, Pallas kernels, merged_output(): pl.pallas_call(merge_kernel, grid_spec=pltpu.PrefetchScalarGridSpec(num_s...  5.6 us
    unnamed x30, local copies, waits for them, and re-layouts  5.18 us
  transfers between devices with their start and end apart: 8, of which 5 were waited for; matrix products, arithmetic and copies ran while one was open for 1% of the time, Pallas kernels for 15%

profile of v7, /device:TPU:56, one launch (start us, length us, event | category | flops | bytes accessed | tf_op | source)
XLA Modules:
  0.0 110.1 jit_solution(7312670846903931293)
XLA Ops:
  0.6 3.0 %fusion.8 = (bf16[128,2048]{1,0:T(8,128)(2,1)}, bf16[1,128,2048]{2,1,0:T(8,128)(2,1)S(1)}, bf16[1,128,2048]{2,1,0:T(8,128)(2,1)S(1)}, bf16[128,2048]{1,0:T(8,128...) fusion(bf16[128,4096]{1,0:T(8,128)(2,1)} %param.5, ...), kind=kLoop, calls=%fused_computation.21 | loop fusion | bytes 6291456 | tf_op jit(solution)/shard_map/slice | solution.py:188
  3.6 0.1 pad_maximum_fusion.1
  3.7 3.4 %collective-permute-start.2 = (bf16[2,128,2048]{2,1,0:T(8,128)(2,1)S(1)}, bf16[2,128,2048]{2,1,0:T(8,128)(2,1)S(1)}, u32[]{:S(2)}, u32[]{:S(2)}) collective-permute-start(bf16[2,128,2048]{2,1,0:T(8,128)(2,1)S(1)} %pad_maximum_fusion.1), channel_id=1, source_target_pairs={{0,4},{4,8},{8,12},{12,16},{16,20},{20,24},{24,28},{28,32},{32,36}... | collective-permute-start | bytes 3145736 | tf_op jit(solution)/shard_map/ppermute | solution.py:20
  7.2 1.1 pad_maximum_fusion
  8.2 3.4 %collective-permute-start = (bf16[2,128,2048]{2,1,0:T(8,128)(2,1)}, bf16[2,128,2048]{2,1,0:T(8,128)(2,1)S(1)}, u32[]{:S(2)}, u32[]{:S(2)}) collective-permute-start(bf16[2,128,2048]{2,1,0:T(8,128)(2,1)} %pad_maximum_fusion), channel_id=1, source_target_pairs={{0,4},{4,8},{8,12},{12,16},{16,20},{20,24},{24,28},{28,32},{32,36}... | collective-permute-start | bytes 3145736 | tf_op jit(solution)/shard_map/ppermute | solution.py:20
  11.6 0.1 fusion.10
  11.8 12.7 %collective-permute-start.1 = (bf16[128,2048]{1,0:T(8,128)(2,1)S(1)}, bf16[128,2048]{1,0:T(8,128)(2,1)S(1)}, u32[]{:S(2)}, u32[]{:S(2)}) collective-permute-start(bf16[128,2048]{1,0:T(8,128)(2,1)S(1)} %get-tuple-element.44.q_ref), channel_id=1, source_target_pairs={{4,0},{8,4},{12,8},{16,12},{20,16},{24,20},{28,24},{32,28},{36,32}... | collective-permute-start | bytes 1572872 | tf_op jit(solution)/shard_map/ppermute | solution.py:26
  24.5 3.9 %collective-permute-start.5 = (bf16[128,2048]{1,0:T(8,128)(2,1)S(1)}, bf16[128,2048]{1,0:T(8,128)(2,1)}, u32[]{:S(2)}, u32[]{:S(2)}) collective-permute-start(bf16[128,2048]{1,0:T(8,128)(2,1)S(1)} %get-tuple-element.45.q_ref), channel_id=1, source_target_pairs={{4,0},{8,4},{12,8},{16,12},{20,16},{24,20},{28,24},{32,28},{36,32}... | collective-permute-start | bytes 1572872 | tf_op jit(solution)/shard_map/ppermute | solution.py:26
  28.4 8.4 %collective-permute-done.1.q_ref = bf16[128,2048]{1,0:T(8,128)(2,1)S(1)} collective-permute-done((bf16[128,2048]{1,0:T(8,128)(2,1)S(1)}, bf16[128,2048]{1,0:T(8,128)(2,1)S(1)}, u32[]{:S(2)}, u32[]{:S(2)}) %collective-permute-start.1) | collective-permute-done | bytes 524320 | tf_op jit(solution)/shard_map/ppermute | solution.py:26
  36.8 0.8 copy-done.9
  37.6 5.8 %collective-permute-done.2.k_ref.v_ref.kp_ref.vp_ref = bf16[2,128,2048]{2,1,0:T(8,128)(2,1)S(1)} collective-permute-done((bf16[2,128,2048]{2,1,0:T(8,128)(2,1)S(1)}, bf16[2,128,2048]{2,1,0:T(8,128)(2,1)S(1)}, u32[]{:S(2)}, u32[]{:S(2)}) %collective-permute-start.2) | collective-permute-done | bytes 1048608 | tf_op jit(solution)/shard_map/ppermute | solution.py:20
  43.4 1.0 copy-done.1
  44.4 3.4 %shard_map.50 = (bf16[128,2048]{1,0:T(8,128)(2,1)}, f32[2,128,16]{2,1,0:T(8,128)}) custom-call(bf16[128,2048]{1,0:T(8,128)(2,1)} %copy-done.9, bf16[2,128,2048]{2,1,0:T(8,128)(2,1)} %copy-done.1, bf16[2,128,2048]{2,1,0:T(8,128)(2,1)} %copy-done.1), custom_call_target="tpu_custom_call" | custom-call | tf_op jit(solution)/shard_map/pallas_call | solution.py:81
  47.7 1.9 %collective-permute-start.3 = (f32[2,128,16]{2,1,0:T(8,128)}, f32[2,128,16]{2,1,0:T(8,128)S(1)}, u32[]{:S(2)}, u32[]{:S(2)}) collective-permute-start(f32[2,128,16]{2,1,0:T(8,128)} %get-tuple-element.20), channel_id=1, source_target_pairs={{0,4},{4,8},{8,12},{12,16},{16,20},{20,24},{24,28},{28,32},{32,36}... | collective-permute-start | bytes 49160 | tf_op jit(solution)/shard_map/ppermute | solution.py:20
  49.7 3.6 %shard_map.51 = (f32[128,2048]{1,0:T(8,128)}, f32[2,128,16]{2,1,0:T(8,128)}) custom-call(s32[1]{0:T(128)} %bitcast.block_ref, bf16[128,2048]{1,0:T(8,128)(2,1)} %copy-done.3, bf16[128,2048]{1,0:T(8,128)(2,1)} %get-tuple-element.49.k_ref, bf16[128,2048]{1,0:T(8,128)(2,1)} %get-tuple-element.36.v_ref, bf16[2,128,2048]{2,1,0:T(8,128)(2,1)} %copy-done.1, ...), custom_call_target="tpu_custom_call" | custom-call | tf_op jit(solution)/shard_map/pallas_call | solution.py:100
  53.3 14.6 %collective-permute-done.3.far_ref.rest_1_ = f32[2,128,16]{2,1,0:T(8,128)S(1)} collective-permute-done((f32[2,128,16]{2,1,0:T(8,128)}, f32[2,128,16]{2,1,0:T(8,128)S(1)}, u32[]{:S(2)}, u32[]{:S(2)}) %collective-permute-start.3) | collective-permute-done | bytes 16416 | tf_op jit(solution)/shard_map/ppermute | solution.py:20
  67.9 1.9 %collective-permute-start.4 = (bf16[128,2048]{1,0:T(8,128)(2,1)S(1)}, bf16[128,2048]{1,0:T(8,128)(2,1)S(1)}, u32[]{:S(2)}, u32[]{:S(2)}) collective-permute-start(bf16[128,2048]{1,0:T(8,128)(2,1)S(1)} %copy-done.14), channel_id=1, source_target_pairs={{0,4},{4,8},{8,12},{12,16},{16,20},{20,24},{24,28},{28,32},{32,36}... | collective-permute-start | bytes 1572872 | tf_op jit(solution)/shard_map/ppermute | solution.py:20
  69.8 0.9 copy-done
  70.8 3.4 %shard_map.54 = (bf16[128,2048]{1,0:T(8,128)(2,1)}, f32[2,128,16]{2,1,0:T(8,128)}) custom-call(bf16[128,2048]{1,0:T(8,128)(2,1)} %collective-permute-done.5.q_ref, bf16[2,128,2048]{2,1,0:T(8,128)(2,1)} %copy-done, bf16[2,128,2048]{2,1,0:T(8,128)(2,1)} %copy-done, f32[2,128,16]{2,1,0:T(8,128)} %get-tuple-element.32.near_ref.rest_0_, f32[2,128,16]{2,1,0:T(8,128)} %copy-done.4), custom_call_target="tpu_custom_call" | custom-call | tf_op jit(solution)/shard_map/pallas_call | solution.py:81
  74.2 1.9 %collective-permute-start.6 = (bf16[128,2048]{1,0:T(8,128)(2,1)}, bf16[128,2048]{1,0:T(8,128)(2,1)S(1)}, u32[]{:S(2)}, u32[]{:S(2)}) collective-permute-start(bf16[128,2048]{1,0:T(8,128)(2,1)} %get-tuple-element.29), channel_id=1, source_target_pairs={{0,4},{4,8},{8,12},{12,16},{16,20},{20,24},{24,28},{28,32},{32,36}... | collective-permute-start | bytes 1572872 | tf_op jit(solution)/shard_map/ppermute | solution.py:20
  76.1 1.9 %collective-permute-start.7 = (f32[2,128,16]{2,1,0:T(8,128)}, f32[2,128,16]{2,1,0:T(8,128)S(1)}, u32[]{:S(2)}, u32[]{:S(2)}) collective-permute-start(f32[2,128,16]{2,1,0:T(8,128)} %get-tuple-element.30), channel_id=1, source_target_pairs={{0,4},{4,8},{8,12},{12,16},{16,20},{20,24},{24,28},{28,32},{32,36}... | collective-permute-start | bytes 49160 | tf_op jit(solution)/shard_map/ppermute | solution.py:20
  78.0 14.4 %collective-permute-done.4.o_ref = bf16[128,2048]{1,0:T(8,128)(2,1)S(1)} collective-permute-done((bf16[128,2048]{1,0:T(8,128)(2,1)S(1)}, bf16[128,2048]{1,0:T(8,128)(2,1)S(1)}, u32[]{:S(2)}, u32[]{:S(2)}) %collective-permute-start.4) | collective-permute-done | bytes 524320 | tf_op jit(solution)/shard_map/ppermute | solution.py:20
  92.4 0.8 copy-done.13
  93.2 2.8 %shard_map.52.rest_0_ = bf16[128,4096]{1,0:T(8,128)(2,1)} custom-call(s32[1]{0:T(128)} %bitcast.block_ref, f32[128,2048]{1,0:T(8,128)} %get-tuple-element.23.mixed_ref, f32[2,128,16]{2,1,0:T(8,128)} %get-tuple-element.32.near_ref.rest_0_, bf16[128,2048]{1,0:T(8,128)(2,1)} %copy-done.13, f32[2,128,16]{2,1,0:T(8,128)} %copy-done.4), custom_call_target="tpu_custom_call" | custom-call | tf_op jit(solution)/shard_map/pallas_call | solution.py:151
  96.0 3.5 %shard_map.53 = (f32[128,2048]{1,0:T(8,128)}, f32[2,128,16]{2,1,0:T(8,128)}) custom-call(s32[1]{0:T(128)} %bitcast.block_ref, bf16[128,2048]{1,0:T(8,128)(2,1)} %copy-done.2, bf16[128,2048]{1,0:T(8,128)(2,1)} %get-tuple-element.46.k_ref, bf16[128,2048]{1,0:T(8,128)(2,1)} %get-tuple-element.39.v_ref, bf16[2,128,2048]{2,1,0:T(8,128)(2,1)} %copy-done, ...), custom_call_target="tpu_custom_call" | custom-call | tf_op jit(solution)/shard_map/pallas_call | solution.py:100
  99.5 5.2 %collective-permute-done.7.far_ref = f32[2,128,16]{2,1,0:T(8,128)S(1)} collective-permute-done((f32[2,128,16]{2,1,0:T(8,128)}, f32[2,128,16]{2,1,0:T(8,128)S(1)}, u32[]{:S(2)}, u32[]{:S(2)}) %collective-permute-start.7) | collective-permute-done | bytes 16416 | tf_op jit(solution)/shard_map/ppermute | solution.py:20
  104.7 0.6 copy-done.10
  105.4 0.2 copy-done.8
  105.6 2.8 %shard_map.55 = bf16[128,4096]{1,0:T(8,128)(2,1)} custom-call(s32[1]{0:T(128)} %bitcast.block_ref, f32[128,2048]{1,0:T(8,128)} %get-tuple-element.27.mixed_ref, f32[2,128,16]{2,1,0:T(8,128)} %get-tuple-element.33.near_ref, bf16[128,2048]{1,0:T(8,128)(2,1)} %copy-done.8, f32[2,128,16]{2,1,0:T(8,128)} %copy-done.10, ...), custom_call_target="tpu_custom_call", output_to_operand_aliasing={{}: (5, {})} | custom-call | tf_op jit(solution)/shard_map/pallas_call | solution.py:151
  108.5 0.1 copy.13
  108.6 0.8 copy-done.5
  109.5 0.6 fusion.4
  (31 shorter events, 0.3 us)
Async XLA Ops:
  3.7 39.7 %collective-permute-start.2 = (bf16[2,128,2048]{2,1,0:T(8,128)(2,1)S(1)}, bf16[2,128,2048]{2,1,0:T(8,128)(2,1)S(1)}, u32[]{:S(2)}, u32[]{:S(2)}) collective-permute-start(bf16[2,128,2048]{2,1,0:T(8,128)(2,1)S(1)} %pad_maximum_fusion.1), channel_id=1, source_target_pairs={{0,4},{4,8},{8,12},{12,16},{16,20},{20,24},{24,28},{28,32},{32,36}... | collective-permute-start | bytes 3145736 | tf_op jit(solution)/shard_map/ppermute | solution.py:20
  7.1 4.5 %copy-start.7 = (bf16[128,4096]{1,0:T(8,128)(2,1)S(1)}, bf16[128,4096]{1,0:T(8,128)(2,1)}, u32[]{:S(2)}) copy-start(bf16[128,4096]{1,0:T(8,128)(2,1)} %param.3) | copy-start | bytes 3145732
  8.2 61.6 %collective-permute-start = (bf16[2,128,2048]{2,1,0:T(8,128)(2,1)}, bf16[2,128,2048]{2,1,0:T(8,128)(2,1)S(1)}, u32[]{:S(2)}, u32[]{:S(2)}) collective-permute-start(bf16[2,128,2048]{2,1,0:T(8,128)(2,1)} %pad_maximum_fusion), channel_id=1, source_target_pairs={{0,4},{4,8},{8,12},{12,16},{16,20},{20,24},{24,28},{28,32},{32,36}... | collective-permute-start | bytes 3145736 | tf_op jit(solution)/shard_map/ppermute | solution.py:20
  11.7 37.9 %copy-start.3 = (bf16[128,2048]{1,0:T(8,128)(2,1)}, bf16[128,2048]{1,0:T(8,128)(2,1)S(1)}, u32[]{:S(2)}) copy-start(bf16[128,2048]{1,0:T(8,128)(2,1)S(1)} %get-tuple-element.44.q_ref) | copy-start | bytes 1572868
  11.7 41.5 %copy-start.2 = (bf16[128,2048]{1,0:T(8,128)(2,1)}, bf16[128,2048]{1,0:T(8,128)(2,1)S(1)}, u32[]{:S(2)}) copy-start(bf16[128,2048]{1,0:T(8,128)(2,1)S(1)} %get-tuple-element.45.q_ref) | copy-start | bytes 1572868
  11.8 25.1 %collective-permute-start.1 = (bf16[128,2048]{1,0:T(8,128)(2,1)S(1)}, bf16[128,2048]{1,0:T(8,128)(2,1)S(1)}, u32[]{:S(2)}, u32[]{:S(2)}) collective-permute-start(bf16[128,2048]{1,0:T(8,128)(2,1)S(1)} %get-tuple-element.44.q_ref), channel_id=1, source_target_pairs={{4,0},{8,4},{12,8},{16,12},{20,16},{24,20},{28,24},{32,28},{36,32}... | collective-permute-start | bytes 1572872 | tf_op jit(solution)/shard_map/ppermute | solution.py:26
  24.5 45.3 %collective-permute-start.5 = (bf16[128,2048]{1,0:T(8,128)(2,1)S(1)}, bf16[128,2048]{1,0:T(8,128)(2,1)}, u32[]{:S(2)}, u32[]{:S(2)}) collective-permute-start(bf16[128,2048]{1,0:T(8,128)(2,1)S(1)} %get-tuple-element.45.q_ref), channel_id=1, source_target_pairs={{4,0},{8,4},{12,8},{16,12},{20,16},{24,20},{28,24},{32,28},{36,32}... | collective-permute-start | bytes 1572872 | tf_op jit(solution)/shard_map/ppermute | solution.py:26
  36.8 0.8 copy-start.9
  43.4 1.0 copy-start.1
  47.7 20.1 %collective-permute-start.3 = (f32[2,128,16]{2,1,0:T(8,128)}, f32[2,128,16]{2,1,0:T(8,128)S(1)}, u32[]{:S(2)}, u32[]{:S(2)}) collective-permute-start(f32[2,128,16]{2,1,0:T(8,128)} %get-tuple-element.20), channel_id=1, source_target_pairs={{0,4},{4,8},{8,12},{12,16},{16,20},{20,24},{24,28},{28,32},{32,36}... | collective-permute-start | bytes 49160 | tf_op jit(solution)/shard_map/ppermute | solution.py:20
  49.7 18.2 %copy-start.14 = (bf16[128,2048]{1,0:T(8,128)(2,1)S(1)}, bf16[128,2048]{1,0:T(8,128)(2,1)}, u32[]{:S(2)}) copy-start(bf16[128,2048]{1,0:T(8,128)(2,1)} %get-tuple-element.25) | copy-start | bytes 1572868
  67.9 1.9 %copy-start.4 = (f32[2,128,16]{2,1,0:T(8,128)}, f32[2,128,16]{2,1,0:T(8,128)S(1)}, u32[]{:S(2)}) copy-start(f32[2,128,16]{2,1,0:T(8,128)S(1)} %collective-permute-done.3.far_ref.rest_1_) | copy-start | bytes 49156
  67.9 24.6 %collective-permute-start.4 = (bf16[128,2048]{1,0:T(8,128)(2,1)S(1)}, bf16[128,2048]{1,0:T(8,128)(2,1)S(1)}, u32[]{:S(2)}, u32[]{:S(2)}) collective-permute-start(bf16[128,2048]{1,0:T(8,128)(2,1)S(1)} %copy-done.14), channel_id=1, source_target_pairs={{0,4},{4,8},{8,12},{12,16},{16,20},{20,24},{24,28},{28,32},{32,36}... | collective-permute-start | bytes 1572872 | tf_op jit(solution)/shard_map/ppermute | solution.py:20
  69.8 1.0 copy-start
  74.2 30.6 %collective-permute-start.6 = (bf16[128,2048]{1,0:T(8,128)(2,1)}, bf16[128,2048]{1,0:T(8,128)(2,1)S(1)}, u32[]{:S(2)}, u32[]{:S(2)}) collective-permute-start(bf16[128,2048]{1,0:T(8,128)(2,1)} %get-tuple-element.29), channel_id=1, source_target_pairs={{0,4},{4,8},{8,12},{12,16},{16,20},{20,24},{24,28},{28,32},{32,36}... | collective-permute-start | bytes 1572872 | tf_op jit(solution)/shard_map/ppermute | solution.py:20
  76.1 28.6 %collective-permute-start.7 = (f32[2,128,16]{2,1,0:T(8,128)}, f32[2,128,16]{2,1,0:T(8,128)S(1)}, u32[]{:S(2)}, u32[]{:S(2)}) collective-permute-start(f32[2,128,16]{2,1,0:T(8,128)} %get-tuple-element.30), channel_id=1, source_target_pairs={{0,4},{4,8},{8,12},{12,16},{16,20},{20,24},{24,28},{28,32},{32,36}... | collective-permute-start | bytes 49160 | tf_op jit(solution)/shard_map/ppermute | solution.py:20
  92.4 0.8 copy-start.13
  104.7 0.6 copy-start.10
  104.7 0.8 copy-start.8
  105.6 2.8 %copy-start.6 = (f32[2,128,16]{2,1,0:T(8,128)S(1)}, f32[2,128,16]{2,1,0:T(8,128)}, u32[]{:S(2)}) copy-start(f32[2,128,16]{2,1,0:T(8,128)} %get-tuple-element.32.near_ref.rest_0_) | copy-start | bytes 49156
  105.6 2.9 %copy-start.12 = (f32[2,128,16]{2,1,0:T(8,128)S(1)}, f32[2,128,16]{2,1,0:T(8,128)}, u32[]{:S(2)}) copy-start(f32[2,128,16]{2,1,0:T(8,128)} %get-tuple-element.33.near_ref) | copy-start | bytes 49156
  108.4 0.9 copy-start.5
  108.5 0.9 copy-start.11

commit v8 on v6

--- a/solution.py
+++ b/solution.py
@@ -181,22 +181,18 @@
     block_index = lax.axis_index("ctx").astype(jnp.int32)
     index_ref = block_index.reshape(1)
     pieces = []
-    out = None
     for chunk in range(CHUNKS):
         cols = slice(chunk * chunk_width, (chunk + 1) * chunk_width)
         q, k, v = att_query[:, cols], att_key[:, cols], att_value[:, cols]
         kv_prev = from_behind(jnp.stack([k, v]), "ctx")
         q_next = from_ahead(q, "ctx")
         after = (pieces[-1][1], pieces[-1][3]) if pieces else ()
-        o_part, stat_part = partial_attention(q_next, kv_prev, after)
-        o_far = from_behind(o_part, "ctx")
+        o_far, stat_far = from_behind(partial_attention(q_next, kv_prev, after), "ctx")
         mixed_near, stat_near = near_attention(index_ref, q, k, v, kv_prev)
-        if pieces:
-            out = merged_output(index_ref, chunk - 1, width, *pieces[-1], out)
-            stat_part, out = lax.optimization_barrier((stat_part, out))
-        stat_far = from_behind(stat_part, "ctx")
         pieces.append((mixed_near, stat_near, o_far, stat_far))
-    out = merged_output(index_ref, CHUNKS - 1, width, *pieces[-1], out)
+    out = None
+    for chunk in range(CHUNKS):
+        out = merged_output(index_ref, chunk, width, *pieces[chunk], out)
     stat_near = jnp.concatenate([piece[1] for piece in pieces], axis=0)
     stat_far = jnp.concatenate([piece[3] for piece in pieces], axis=0)
     return out, log_total(block_index, stat_near, stat_far)

time: 114 us -> 106 us (0.930)
  waiting for transfers between devices: 52.6 us -> 44.2 us
    ppermute x6, waiting for transfers between devices: 44.2 us -> 35.8 us  [from_behind(): return lax.ppermute(block, axis, route)]
  transfers between devices with their start and end apart: 8 -> 8, of which waited for: 5 -> 5; matrix products, arithmetic and copies ran while one was open for 3% -> 3% of each run, Pallas kernels for 15% -> 16%
where the time goes in v8:
time: 106 us; the launch traced here: 105 us
  waiting for transfers between devices  44.2 us (42%)
  starting transfers between devices  31.1 us (29%)
  Pallas kernels  19.4 us (18%)
  local copies, waits for them, and re-layouts  7.69 us (7%)
  other arithmetic  1.82 us (2%)
    ppermute x6, waiting for transfers between devices, from_behind(): return lax.ppermute(block, axis, route)  35.8 us
    ppermute x2, starting transfers between devices, from_ahead(): return lax.ppermute(block, axis, route)  16.7 us
    ppermute x6, starting transfers between devices, from_behind(): return lax.ppermute(block, axis, route)  14.4 us
    ppermute x2, waiting for transfers between devices, from_ahead(): return lax.ppermute(block, axis, route)  8.38 us
    pallas_call x2, Pallas kernels, near_attention(): pl.pallas_call(near_kernel, grid_spec=pltpu.PrefetchScalarGridSpec(num_sc...  7.04 us
    pallas_call x2, Pallas kernels, partial_attention(): pl.pallas_call(partial_kernel, grid=(steps,), in_specs=[block, key_block,...  6.79 us
    pallas_call x2, Pallas kernels, merged_output(): pl.pallas_call(merge_kernel, grid_spec=pltpu.PrefetchScalarGridSpec(num_s...  5.56 us
    unnamed x24, local copies, waits for them, and re-layouts  3.24 us
  transfers between devices with their start and end apart: 8, of which 5 were waited for; matrix products, arithmetic and copies ran while one was open for 3% of the time, Pallas kernels for 16%

profile of v8, /device:TPU:56, one launch (start us, length us, event | category | flops | bytes accessed | tf_op | source)
XLA Modules:
  0.0 105.0 jit_solution(4541588183480872701)
XLA Ops:
  0.6 3.2 %slice_bitcast_fusion.4 = (bf16[1,128,2048]{2,1,0:T(8,128)(2,1)S(1)}, bf16[1,128,2048]{2,1,0:T(8,128)(2,1)S(1)}, bf16[128,2048]{1,0:T(8,128)(2,1)}, bf16[128,204...) fusion(bf16[128,4096]{1,0:T(8,128)(2,1)} %param.5, ...), kind=kLoop, calls=%fused_computation.17 | loop fusion | bytes 6291456 | tf_op jit(solution)/shard_map/stack | solution.py:187
  3.8 0.1 pad_maximum_fusion.1
  3.9 3.4 %collective-permute-start.2 = (bf16[2,128,2048]{2,1,0:T(8,128)(2,1)S(1)}, bf16[2,128,2048]{2,1,0:T(8,128)(2,1)S(1)}, u32[]{:S(2)}, u32[]{:S(2)}) collective-permute-start(bf16[2,128,2048]{2,1,0:T(8,128)(2,1)S(1)} %pad_maximum_fusion.1), channel_id=1, source_target_pairs={{0,4},{4,8},{8,12},{12,16},{16,20},{20,24},{24,28},{28,32},{32,36}... | collective-permute-start | bytes 3145736 | tf_op jit(solution)/shard_map/ppermute | solution.py:20
  7.4 1.1 %pad_maximum_fusion = bf16[2,128,2048]{2,1,0:T(8,128)(2,1)} fusion(bf16[1,128,2048]{2,1,0:T(8,128)(2,1)S(1)} %get-tuple-element.23, bf16[1,128,2048]{2,1,0:T(8,128)(2,1)S(1)} %get-tuple-element.30), kind=kLoop, calls=%fused_computation | loop fusion | flops 524288 | bytes 2097152 | tf_op jit(solution)/shard_map/stack | solution.py:187
  8.4 3.4 %collective-permute-start = (bf16[2,128,2048]{2,1,0:T(8,128)(2,1)}, bf16[2,128,2048]{2,1,0:T(8,128)(2,1)S(1)}, u32[]{:S(2)}, u32[]{:S(2)}) collective-permute-start(bf16[2,128,2048]{2,1,0:T(8,128)(2,1)} %pad_maximum_fusion), channel_id=1, source_target_pairs={{0,4},{4,8},{8,12},{12,16},{16,20},{20,24},{24,28},{28,32},{32,36}... | collective-permute-start | bytes 3145736 | tf_op jit(solution)/shard_map/ppermute | solution.py:20
  11.8 0.1 fusion.8
  11.9 12.7 %collective-permute-start.3 = (bf16[128,2048]{1,0:T(8,128)(2,1)S(1)}, bf16[128,2048]{1,0:T(8,128)(2,1)S(1)}, u32[]{:S(2)}, u32[]{:S(2)}) collective-permute-start(bf16[128,2048]{1,0:T(8,128)(2,1)S(1)} %get-tuple-element.26.q_ref), channel_id=1, source_target_pairs={{4,0},{8,4},{12,8},{16,12},{20,16},{24,20},{28,24},{32,28},{36,32}... | collective-permute-start | bytes 1572872 | tf_op jit(solution)/shard_map/ppermute | solution.py:26
  24.7 3.9 %collective-permute-start.1 = (bf16[128,2048]{1,0:T(8,128)(2,1)S(1)}, bf16[128,2048]{1,0:T(8,128)(2,1)}, u32[]{:S(2)}, u32[]{:S(2)}) collective-permute-start(bf16[128,2048]{1,0:T(8,128)(2,1)S(1)} %get-tuple-element.27.q_ref), channel_id=1, source_target_pairs={{4,0},{8,4},{12,8},{16,12},{20,16},{24,20},{28,24},{32,28},{36,32}... | collective-permute-start | bytes 1572872 | tf_op jit(solution)/shard_map/ppermute | solution.py:26
  28.6 8.4 %collective-permute-done.3.q_ref = bf16[128,2048]{1,0:T(8,128)(2,1)S(1)} collective-permute-done((bf16[128,2048]{1,0:T(8,128)(2,1)S(1)}, bf16[128,2048]{1,0:T(8,128)(2,1)S(1)}, u32[]{:S(2)}, u32[]{:S(2)}) %collective-permute-start.3) | collective-permute-done | bytes 524320 | tf_op jit(solution)/shard_map/ppermute | solution.py:26
  37.0 0.8 copy-done.9
  37.8 5.8 %collective-permute-done.2.kp_ref.vp_ref.k_ref.v_ref = bf16[2,128,2048]{2,1,0:T(8,128)(2,1)S(1)} collective-permute-done((bf16[2,128,2048]{2,1,0:T(8,128)(2,1)S(1)}, bf16[2,128,2048]{2,1,0:T(8,128)(2,1)S(1)}, u32[]{:S(2)}, u32[]{:S(2)}) %collective-permute-start.2) | collective-permute-done | bytes 1048608 | tf_op jit(solution)/shard_map/ppermute | solution.py:20
  43.6 1.0 copy-done
  44.6 3.4 %shard_map.52 = (bf16[128,2048]{1,0:T(8,128)(2,1)}, f32[2,128,16]{2,1,0:T(8,128)}) custom-call(bf16[128,2048]{1,0:T(8,128)(2,1)} %copy-done.9, bf16[2,128,2048]{2,1,0:T(8,128)(2,1)} %copy-done, bf16[2,128,2048]{2,1,0:T(8,128)(2,1)} %copy-done), custom_call_target="tpu_custom_call" | custom-call | tf_op jit(solution)/shard_map/pallas_call | solution.py:80
  48.0 1.9 %collective-permute-start.4 = (f32[2,128,16]{2,1,0:T(8,128)}, f32[2,128,16]{2,1,0:T(8,128)S(1)}, u32[]{:S(2)}, u32[]{:S(2)}) collective-permute-start(f32[2,128,16]{2,1,0:T(8,128)} %get-tuple-element.13), channel_id=1, source_target_pairs={{0,4},{4,8},{8,12},{12,16},{16,20},{20,24},{24,28},{28,32},{32,36}... | collective-permute-start | bytes 49160 | tf_op jit(solution)/shard_map/ppermute | solution.py:20
  49.9 1.9 %collective-permute-start.7 = (bf16[128,2048]{1,0:T(8,128)(2,1)}, bf16[128,2048]{1,0:T(8,128)(2,1)}, u32[]{:S(2)}, u32[]{:S(2)}) collective-permute-start(bf16[128,2048]{1,0:T(8,128)(2,1)} %get-tuple-element.17), channel_id=1, source_target_pairs={{0,4},{4,8},{8,12},{12,16},{16,20},{20,24},{24,28},{28,32},{32,36}... | collective-permute-start | bytes 1572872 | tf_op jit(solution)/shard_map/ppermute | solution.py:20
  51.8 3.5 %shard_map.51 = (f32[128,2048]{1,0:T(8,128)}, f32[2,128,16]{2,1,0:T(8,128)}) custom-call(s32[1]{0:T(128)} %bitcast.block_ref, bf16[128,2048]{1,0:T(8,128)(2,1)} %copy-done.3, bf16[128,2048]{1,0:T(8,128)(2,1)} %get-tuple-element.29.k_ref, bf16[128,2048]{1,0:T(8,128)(2,1)} %get-tuple-element.24.v_ref, bf16[2,128,2048]{2,1,0:T(8,128)(2,1)} %copy-done, ...), custom_call_target="tpu_custom_call" | custom-call | tf_op jit(solution)/shard_map/pallas_call | solution.py:99
  55.4 10.7 %collective-permute-done.kp_ref.vp_ref.k_ref.v_ref = bf16[2,128,2048]{2,1,0:T(8,128)(2,1)S(1)} collective-permute-done((bf16[2,128,2048]{2,1,0:T(8,128)(2,1)}, bf16[2,128,2048]{2,1,0:T(8,128)(2,1)S(1)}, u32[]{:S(2)}, u32[]{:S(2)}) %collective-permute-start) | collective-permute-done | bytes 1048608 | tf_op jit(solution)/shard_map/ppermute | solution.py:20
  66.1 2.8 %collective-permute-done.4.rest_1_.far_ref = f32[2,128,16]{2,1,0:T(8,128)S(1)} collective-permute-done((f32[2,128,16]{2,1,0:T(8,128)}, f32[2,128,16]{2,1,0:T(8,128)S(1)}, u32[]{:S(2)}, u32[]{:S(2)}) %collective-permute-start.4) | collective-permute-done | bytes 16416 | tf_op jit(solution)/shard_map/ppermute | solution.py:20
  68.9 0.6 copy-done.4
  69.5 3.4 %shard_map.53 = (bf16[128,2048]{1,0:T(8,128)(2,1)}, f32[2,128,16]{2,1,0:T(8,128)}) custom-call(bf16[128,2048]{1,0:T(8,128)(2,1)} %collective-permute-done.1.q_ref, bf16[2,128,2048]{2,1,0:T(8,128)(2,1)} %copy-done.1, bf16[2,128,2048]{2,1,0:T(8,128)(2,1)} %copy-done.1, f32[2,128,16]{2,1,0:T(8,128)} %get-tuple-element.12.rest_0_.near_ref, f32[2,128,16]{2,1,0:T(8,128)} %copy-done.4), custom_call_target="tpu_custom_call" | custom-call | tf_op jit(solution)/shard_map/pallas_call | solution.py:80
  73.0 1.9 %collective-permute-start.5 = (bf16[128,2048]{1,0:T(8,128)(2,1)}, bf16[128,2048]{1,0:T(8,128)(2,1)S(1)}, u32[]{:S(2)}, u32[]{:S(2)}) collective-permute-start(bf16[128,2048]{1,0:T(8,128)(2,1)} %get-tuple-element.14), channel_id=1, source_target_pairs={{0,4},{4,8},{8,12},{12,16},{16,20},{20,24},{24,28},{28,32},{32,36}... | collective-permute-start | bytes 1572872 | tf_op jit(solution)/shard_map/ppermute | solution.py:20
  74.9 0.1 copy.12
  75.0 3.5 %shard_map.50 = (f32[128,2048]{1,0:T(8,128)}, f32[2,128,16]{2,1,0:T(8,128)}) custom-call(s32[1]{0:T(128)} %bitcast.block_ref, bf16[128,2048]{1,0:T(8,128)(2,1)} %copy-done.2, bf16[128,2048]{1,0:T(8,128)(2,1)} %get-tuple-element.28.k_ref, bf16[128,2048]{1,0:T(8,128)(2,1)} %get-tuple-element.25.v_ref, bf16[2,128,2048]{2,1,0:T(8,128)(2,1)} %copy-done.1, ...), custom_call_target="tpu_custom_call" | custom-call | tf_op jit(solution)/shard_map/pallas_call | solution.py:99
  78.5 1.0 copy.13
  79.5 1.9 %collective-permute-start.6 = (f32[2,128,16]{2,1,0:T(8,128)S(1)}, f32[2,128,16]{2,1,0:T(8,128)S(1)}, u32[]{:S(2)}, u32[]{:S(2)}) collective-permute-start(f32[2,128,16]{2,1,0:T(8,128)S(1)} %copy-done.11), channel_id=1, source_target_pairs={{0,4},{4,8},{8,12},{12,16},{16,20},{20,24},{24,28},{28,32},{32,36}... | collective-permute-start | bytes 49160 | tf_op jit(solution)/shard_map/ppermute | solution.py:20
  81.4 0.1 copy.14
  81.5 16.4 %collective-permute-done.6.far_ref = f32[2,128,16]{2,1,0:T(8,128)S(1)} collective-permute-done((f32[2,128,16]{2,1,0:T(8,128)S(1)}, f32[2,128,16]{2,1,0:T(8,128)S(1)}, u32[]{:S(2)}, u32[]{:S(2)}) %collective-permute-start.6) | collective-permute-done | bytes 16416 | tf_op jit(solution)/shard_map/ppermute | solution.py:20
  98.0 0.1 copy.15
  98.0 0.6 fusion.4
  98.7 2.8 %shard_map.54.rest_0_ = bf16[128,4096]{1,0:T(8,128)(2,1)} custom-call(s32[1]{0:T(128)} %bitcast.block_ref, f32[128,2048]{1,0:T(8,128)} %get-tuple-element.16.mixed_ref, f32[2,128,16]{2,1,0:T(8,128)} %get-tuple-element.12.rest_0_.near_ref, bf16[128,2048]{1,0:T(8,128)(2,1)} %collective-permute-done.7.o_ref, f32[2,128,16]{2,1,0:T(8,128)} %copy-done.4), custom_call_target="tpu_custom_call" | custom-call | tf_op jit(solution)/shard_map/pallas_call | solution.py:150
  101.5 0.8 copy-done.8
  102.3 2.8 %shard_map.55 = bf16[128,4096]{1,0:T(8,128)(2,1)} custom-call(s32[1]{0:T(128)} %bitcast.block_ref, f32[128,2048]{1,0:T(8,128)} %get-tuple-element.10.mixed_ref, f32[2,128,16]{2,1,0:T(8,128)} %get-tuple-element.11.near_ref, bf16[128,2048]{1,0:T(8,128)(2,1)} %copy-done.8, f32[2,128,16]{2,1,0:T(8,128)} %copy-done.10, ...), custom_call_target="tpu_custom_call", output_to_operand_aliasing={{}: (5, {})} | custom-call | tf_op jit(solution)/shard_map/pallas_call | solution.py:150
  (25 shorter events, 0.1 us)
Async XLA Ops:
  3.9 39.7 %collective-permute-start.2 = (bf16[2,128,2048]{2,1,0:T(8,128)(2,1)S(1)}, bf16[2,128,2048]{2,1,0:T(8,128)(2,1)S(1)}, u32[]{:S(2)}, u32[]{:S(2)}) collective-permute-start(bf16[2,128,2048]{2,1,0:T(8,128)(2,1)S(1)} %pad_maximum_fusion.1), channel_id=1, source_target_pairs={{0,4},{4,8},{8,12},{12,16},{16,20},{20,24},{24,28},{28,32},{32,36}... | collective-permute-start | bytes 3145736 | tf_op jit(solution)/shard_map/ppermute | solution.py:20
  7.3 4.5 %copy-start.7 = (bf16[128,4096]{1,0:T(8,128)(2,1)S(1)}, bf16[128,4096]{1,0:T(8,128)(2,1)}, u32[]{:S(2)}) copy-start(bf16[128,4096]{1,0:T(8,128)(2,1)} %param.3) | copy-start | bytes 3145732
  8.4 57.7 %collective-permute-start = (bf16[2,128,2048]{2,1,0:T(8,128)(2,1)}, bf16[2,128,2048]{2,1,0:T(8,128)(2,1)S(1)}, u32[]{:S(2)}, u32[]{:S(2)}) collective-permute-start(bf16[2,128,2048]{2,1,0:T(8,128)(2,1)} %pad_maximum_fusion), channel_id=1, source_target_pairs={{0,4},{4,8},{8,12},{12,16},{16,20},{20,24},{24,28},{28,32},{32,36}... | collective-permute-start | bytes 3145736 | tf_op jit(solution)/shard_map/ppermute | solution.py:20
  11.9 39.9 %copy-start.3 = (bf16[128,2048]{1,0:T(8,128)(2,1)}, bf16[128,2048]{1,0:T(8,128)(2,1)S(1)}, u32[]{:S(2)}) copy-start(bf16[128,2048]{1,0:T(8,128)(2,1)S(1)} %get-tuple-element.26.q_ref) | copy-start | bytes 1572868
  11.9 43.4 %copy-start.2 = (bf16[128,2048]{1,0:T(8,128)(2,1)}, bf16[128,2048]{1,0:T(8,128)(2,1)S(1)}, u32[]{:S(2)}) copy-start(bf16[128,2048]{1,0:T(8,128)(2,1)S(1)} %get-tuple-element.27.q_ref) | copy-start | bytes 1572868
  11.9 25.1 %collective-permute-start.3 = (bf16[128,2048]{1,0:T(8,128)(2,1)S(1)}, bf16[128,2048]{1,0:T(8,128)(2,1)S(1)}, u32[]{:S(2)}, u32[]{:S(2)}) collective-permute-start(bf16[128,2048]{1,0:T(8,128)(2,1)S(1)} %get-tuple-element.26.q_ref), channel_id=1, source_target_pairs={{4,0},{8,4},{12,8},{16,12},{20,16},{24,20},{28,24},{32,28},{36,32}... | collective-permute-start | bytes 1572872 | tf_op jit(solution)/shard_map/ppermute | solution.py:26
  24.7 30.7 %collective-permute-start.1 = (bf16[128,2048]{1,0:T(8,128)(2,1)S(1)}, bf16[128,2048]{1,0:T(8,128)(2,1)}, u32[]{:S(2)}, u32[]{:S(2)}) collective-permute-start(bf16[128,2048]{1,0:T(8,128)(2,1)S(1)} %get-tuple-element.27.q_ref), channel_id=1, source_target_pairs={{4,0},{8,4},{12,8},{16,12},{20,16},{24,20},{28,24},{32,28},{36,32}... | collective-permute-start | bytes 1572872 | tf_op jit(solution)/shard_map/ppermute | solution.py:26
  37.0 0.8 copy-start.9
  43.6 1.0 copy-start
  48.0 20.9 %collective-permute-start.4 = (f32[2,128,16]{2,1,0:T(8,128)}, f32[2,128,16]{2,1,0:T(8,128)S(1)}, u32[]{:S(2)}, u32[]{:S(2)}) collective-permute-start(f32[2,128,16]{2,1,0:T(8,128)} %get-tuple-element.13), channel_id=1, source_target_pairs={{0,4},{4,8},{8,12},{12,16},{16,20},{20,24},{24,28},{28,32},{32,36}... | collective-permute-start | bytes 49160 | tf_op jit(solution)/shard_map/ppermute | solution.py:20
  49.9 48.8 %collective-permute-start.7 = (bf16[128,2048]{1,0:T(8,128)(2,1)}, bf16[128,2048]{1,0:T(8,128)(2,1)}, u32[]{:S(2)}, u32[]{:S(2)}) collective-permute-start(bf16[128,2048]{1,0:T(8,128)(2,1)} %get-tuple-element.17), channel_id=1, source_target_pairs={{0,4},{4,8},{8,12},{12,16},{16,20},{20,24},{24,28},{28,32},{32,36}... | collective-permute-start | bytes 1572872 | tf_op jit(solution)/shard_map/ppermute | solution.py:20
  66.1 2.8 %copy-start.1 = (bf16[2,128,2048]{2,1,0:T(8,128)(2,1)}, bf16[2,128,2048]{2,1,0:T(8,128)(2,1)S(1)}, u32[]{:S(2)}) copy-start(bf16[2,128,2048]{2,1,0:T(8,128)(2,1)S(1)} %collective-permute-done.kp_ref.vp_ref.k_ref.v_ref) | copy-start | bytes 3145732
  68.9 0.6 copy-start.4
  69.5 5.3 %copy-start.6 = (f32[2,128,16]{2,1,0:T(8,128)S(1)}, f32[2,128,16]{2,1,0:T(8,128)}, u32[]{:S(2)}) copy-start(f32[2,128,16]{2,1,0:T(8,128)} %get-tuple-element.12.rest_0_.near_ref) | copy-start | bytes 49156
  73.0 28.5 %collective-permute-start.5 = (bf16[128,2048]{1,0:T(8,128)(2,1)}, bf16[128,2048]{1,0:T(8,128)(2,1)S(1)}, u32[]{:S(2)}, u32[]{:S(2)}) collective-permute-start(bf16[128,2048]{1,0:T(8,128)(2,1)} %get-tuple-element.14), channel_id=1, source_target_pairs={{0,4},{4,8},{8,12},{12,16},{16,20},{20,24},{24,28},{28,32},{32,36}... | collective-permute-start | bytes 1572872 | tf_op jit(solution)/shard_map/ppermute | solution.py:20
  74.9 4.5 %copy-start.11 = (f32[2,128,16]{2,1,0:T(8,128)S(1)}, f32[2,128,16]{2,1,0:T(8,128)}, u32[]{:S(2)}) copy-start(f32[2,128,16]{2,1,0:T(8,128)} %get-tuple-element.15) | copy-start | bytes 49156
  78.5 2.9 %copy-start.5 = (f32[2,128,16]{2,1,0:T(8,128)S(1)}, f32[2,128,16]{2,1,0:T(8,128)}, u32[]{:S(2)}) copy-start(f32[2,128,16]{2,1,0:T(8,128)} %copy-done.4) | copy-start | bytes 49156
  79.5 18.5 %collective-permute-start.6 = (f32[2,128,16]{2,1,0:T(8,128)S(1)}, f32[2,128,16]{2,1,0:T(8,128)S(1)}, u32[]{:S(2)}, u32[]{:S(2)}) collective-permute-start(f32[2,128,16]{2,1,0:T(8,128)S(1)} %copy-done.11), channel_id=1, source_target_pairs={{0,4},{4,8},{8,12},{12,16},{16,20},{20,24},{24,28},{28,32},{32,36}... | collective-permute-start | bytes 49160 | tf_op jit(solution)/shard_map/ppermute | solution.py:20
  98.0 0.7 copy-start.10
  101.5 0.8 copy-start.8

commit v9 on v8

--- a/solution.py
+++ b/solution.py
@@ -89,11 +89,13 @@
     )(q, kv, kv, *after)
 
 
-def near_attention(block_index, q, k, v, kv_prev):
+def near_attention(block_index, chunk, q, k, v, kv_prev):
     rows, width = q.shape
     step_width = HEADS_PER_STEP * HEAD_DIM
-    steps = width // step_width
-    block = pl.BlockSpec((rows, step_width), lambda g, b: (0, g))
+    steps = kv_prev.shape[2] // step_width
+    offset = chunk * steps
+    whole = pl.BlockSpec((rows, step_width), lambda g, b: (0, g + offset))
+    part = pl.BlockSpec((rows, step_width), lambda g, b: (0, g))
     key_block = pl.BlockSpec((None, rows, step_width), lambda g, b: (0, 0, g))
     value_block = pl.BlockSpec((None, rows, step_width), lambda g, b: (1, 0, g))
     return pl.pallas_call(
@@ -101,11 +103,11 @@
         grid_spec=pltpu.PrefetchScalarGridSpec(
             num_scalar_prefetch=1,
             grid=(steps,),
-            in_specs=[block] * 3 + [key_block, value_block],
-            out_specs=[block, stat_spec(rows)],
+            in_specs=[whole] * 3 + [key_block, value_block],
+            out_specs=[part, stat_spec(rows)],
         ),
         out_shape=[
-            jax.ShapeDtypeStruct((rows, width), jnp.float32),
+            jax.ShapeDtypeStruct((rows, kv_prev.shape[2]), jnp.float32),
             jax.ShapeDtypeStruct((steps, rows, 2 * HEADS_PER_STEP), jnp.float32),
         ],
     )(block_index, q, k, v, kv_prev, kv_prev)
@@ -183,12 +185,11 @@
     pieces = []
     for chunk in range(CHUNKS):
         cols = slice(chunk * chunk_width, (chunk + 1) * chunk_width)
-        q, k, v = att_query[:, cols], att_key[:, cols], att_value[:, cols]
-        kv_prev = from_behind(jnp.stack([k, v]), "ctx")
-        q_next = from_ahead(q, "ctx")
+        kv_prev = from_behind(jnp.stack([att_key[:, cols], att_value[:, cols]]), "ctx")
+        q_next = from_ahead(att_query[:, cols], "ctx")
         after = (pieces[-1][1], pieces[-1][3]) if pieces else ()
         o_far, stat_far = from_behind(partial_attention(q_next, kv_prev, after), "ctx")
-        mixed_near, stat_near = near_attention(index_ref, q, k, v, kv_prev)
+        mixed_near, stat_near = near_attention(index_ref, chunk, att_query, att_key, att_value, kv_prev)
         pieces.append((mixed_near, stat_near, o_far, stat_far))
     out = None
     for chunk in range(CHUNKS):

time: 106 us -> 105 us (level)
    another operation x1, local copies, waits for them, and re-layouts: 3.21 us -> 1.66 us  [shards(): jnp.stack([att_key[:, cols], att_value[:, cols]])]
  transfers between devices with their start and end apart: 8 -> 8, of which waited for: 5 -> 5; matrix products, arithmetic and copies ran while one was open for 3% -> 4% of each run, Pallas kernels for 16% -> 16%
where the time goes in v9:
time: 105 us; the launch traced here: 104 us
  waiting for transfers between devices  44.2 us (42%)
  starting transfers between devices  31.1 us (30%)
  Pallas kernels  19.5 us (19%)
  local copies, waits for them, and re-layouts  6.95 us (7%)
  other arithmetic  1.82 us (2%)
    ppermute x6, waiting for transfers between devices, from_behind(): return lax.ppermute(block, axis, route)  35.8 us
    ppermute x2, starting transfers between devices, from_ahead(): return lax.ppermute(block, axis, route)  16.7 us
    ppermute x6, starting transfers between devices, from_behind(): return lax.ppermute(block, axis, route)  14.4 us
    ppermute x2, waiting for transfers between devices, from_ahead(): return lax.ppermute(block, axis, route)  8.38 us
    pallas_call x2, Pallas kernels, near_attention(): pl.pallas_call(near_kernel, grid_spec=pltpu.PrefetchScalarGridSpec(num_sc...  7.06 us
    pallas_call x2, Pallas kernels, partial_attention(): pl.pallas_call(partial_kernel, grid=(steps,), in_specs=[block, key_block,...  6.84 us
    pallas_call x2, Pallas kernels, merged_output(): pl.pallas_call(merge_kernel, grid_spec=pltpu.PrefetchScalarGridSpec(num_s...  5.56 us
    unnamed x24, local copies, waits for them, and re-layouts  3.23 us
  transfers between devices with their start and end apart: 8, of which 5 were waited for; matrix products, arithmetic and copies ran while one was open for 4% of the time, Pallas kernels for 16%

profile of v9, /device:TPU:56, one launch (start us, length us, event | category | flops | bytes accessed | tf_op | source)
XLA Modules:
  0.0 104.3 jit_solution(14490396364505229846)
XLA Ops:
  0.6 1.7 %slice_bitcast_fusion = (bf16[1,128,2048]{2,1,0:T(8,128)(2,1)S(1)}, bf16[1,128,2048]{2,1,0:T(8,128)(2,1)S(1)}, bf16[1,128,2048]{2,1,0:T(8,128)(2,1)S(1)}, bf16[1,128,2048]{2,1,0:T(8,128)(2,1)S(1)}) fusion(bf16[128,4096]{1,0:T(8,128)(2,1)} %v_ref.3, bf16[128,4096]{1,0:T(8,128)(2,1)} %k_ref.3), kind=kLoop, calls=%fused_computation.2 | loop fusion | bytes 4194304 | tf_op jit(solution)/shard_map/stack | solution.py:188
  2.3 0.1 pad_maximum_fusion.1
  2.4 3.4 %collective-permute-start.2 = (bf16[2,128,2048]{2,1,0:T(8,128)(2,1)S(1)}, bf16[2,128,2048]{2,1,0:T(8,128)(2,1)S(1)}, u32[]{:S(2)}, u32[]{:S(2)}) collective-permute-start(bf16[2,128,2048]{2,1,0:T(8,128)(2,1)S(1)} %pad_maximum_fusion.1), channel_id=1, source_target_pairs={{0,4},{4,8},{8,12},{12,16},{16,20},{20,24},{24,28},{28,32},{32,36}... | collective-permute-start | bytes 3145736 | tf_op jit(solution)/shard_map/ppermute | solution.py:20
  5.8 1.1 %pad_maximum_fusion = bf16[2,128,2048]{2,1,0:T(8,128)(2,1)} fusion(bf16[1,128,2048]{2,1,0:T(8,128)(2,1)S(1)} %get-tuple-element.23, bf16[1,128,2048]{2,1,0:T(8,128)(2,1)S(1)} %get-tuple-element.24), kind=kLoop, calls=%fused_computation | loop fusion | flops 524288 | bytes 2097152 | tf_op jit(solution)/shard_map/stack | solution.py:188
  6.9 3.4 %collective-permute-start = (bf16[2,128,2048]{2,1,0:T(8,128)(2,1)}, bf16[2,128,2048]{2,1,0:T(8,128)(2,1)S(1)}, u32[]{:S(2)}, u32[]{:S(2)}) collective-permute-start(bf16[2,128,2048]{2,1,0:T(8,128)(2,1)} %pad_maximum_fusion), channel_id=1, source_target_pairs={{0,4},{4,8},{8,12},{12,16},{16,20},{20,24},{24,28},{28,32},{32,36}... | collective-permute-start | bytes 3145736 | tf_op jit(solution)/shard_map/ppermute | solution.py:20
  10.3 0.9 fusion.8
  11.2 12.7 %collective-permute-start.3 = (bf16[128,2048]{1,0:T(8,128)(2,1)S(1)}, bf16[128,2048]{1,0:T(8,128)(2,1)S(1)}, u32[]{:S(2)}, u32[]{:S(2)}) collective-permute-start(bf16[128,2048]{1,0:T(8,128)(2,1)S(1)} %get-tuple-element.18), channel_id=1, source_target_pairs={{4,0},{8,4},{12,8},{16,12},{20,16},{24,20},{28,24},{32,28},{36,32}... | collective-permute-start | bytes 1572872 | tf_op jit(solution)/shard_map/ppermute | solution.py:26
  23.9 3.9 %collective-permute-start.1 = (bf16[128,2048]{1,0:T(8,128)(2,1)}, bf16[128,2048]{1,0:T(8,128)(2,1)S(1)}, u32[]{:S(2)}, u32[]{:S(2)}) collective-permute-start(bf16[128,2048]{1,0:T(8,128)(2,1)} %get-tuple-element.19), channel_id=1, source_target_pairs={{4,0},{8,4},{12,8},{16,12},{20,16},{24,20},{28,24},{32,28},{36,32}... | collective-permute-start | bytes 1572872 | tf_op jit(solution)/shard_map/ppermute | solution.py:26
  27.8 8.4 %collective-permute-done.3.q_ref = bf16[128,2048]{1,0:T(8,128)(2,1)S(1)} collective-permute-done((bf16[128,2048]{1,0:T(8,128)(2,1)S(1)}, bf16[128,2048]{1,0:T(8,128)(2,1)S(1)}, u32[]{:S(2)}, u32[]{:S(2)}) %collective-permute-start.3) | collective-permute-done | bytes 524320 | tf_op jit(solution)/shard_map/ppermute | solution.py:26
  36.2 5.9 %collective-permute-done.2.kp_ref.vp_ref.k_ref.v_ref = bf16[2,128,2048]{2,1,0:T(8,128)(2,1)S(1)} collective-permute-done((bf16[2,128,2048]{2,1,0:T(8,128)(2,1)S(1)}, bf16[2,128,2048]{2,1,0:T(8,128)(2,1)S(1)}, u32[]{:S(2)}, u32[]{:S(2)}) %collective-permute-start.2) | collective-permute-done | bytes 1048608 | tf_op jit(solution)/shard_map/ppermute | solution.py:20
  42.1 1.0 copy-done
  43.1 3.4 %shard_map.52 = (bf16[128,2048]{1,0:T(8,128)(2,1)}, f32[2,128,16]{2,1,0:T(8,128)}) custom-call(bf16[128,2048]{1,0:T(8,128)(2,1)} %copy-done.7, bf16[2,128,2048]{2,1,0:T(8,128)(2,1)} %copy-done, bf16[2,128,2048]{2,1,0:T(8,128)(2,1)} %copy-done), custom_call_target="tpu_custom_call" | custom-call | tf_op jit(solution)/shard_map/pallas_call | solution.py:80
  46.5 1.9 %collective-permute-start.4 = (f32[2,128,16]{2,1,0:T(8,128)}, f32[2,128,16]{2,1,0:T(8,128)S(1)}, u32[]{:S(2)}, u32[]{:S(2)}) collective-permute-start(f32[2,128,16]{2,1,0:T(8,128)} %get-tuple-element.13), channel_id=1, source_target_pairs={{0,4},{4,8},{8,12},{12,16},{16,20},{20,24},{24,28},{28,32},{32,36}... | collective-permute-start | bytes 49160 | tf_op jit(solution)/shard_map/ppermute | solution.py:20
  48.4 1.9 %collective-permute-start.7 = (bf16[128,2048]{1,0:T(8,128)(2,1)}, bf16[128,2048]{1,0:T(8,128)(2,1)S(1)}, u32[]{:S(2)}, u32[]{:S(2)}) collective-permute-start(bf16[128,2048]{1,0:T(8,128)(2,1)} %get-tuple-element.17), channel_id=1, source_target_pairs={{0,4},{4,8},{8,12},{12,16},{16,20},{20,24},{24,28},{28,32},{32,36}... | collective-permute-start | bytes 1572872 | tf_op jit(solution)/shard_map/ppermute | solution.py:20
  50.3 3.5 %shard_map.51 = (f32[128,2048]{1,0:T(8,128)}, f32[2,128,16]{2,1,0:T(8,128)}) custom-call(s32[1]{0:T(128)} %bitcast.block_ref, bf16[128,4096]{1,0:T(8,128)(2,1)} %q_ref.3, bf16[128,4096]{1,0:T(8,128)(2,1)} %k_ref.3, bf16[128,4096]{1,0:T(8,128)(2,1)} %v_ref.3, bf16[2,128,2048]{2,1,0:T(8,128)(2,1)} %copy-done, bf16[2,128,2048]{2,1,0:T(8,128)(2,1)} %copy-done), custom_call_target="tpu_custom_call" | custom-call | tf_op jit(solution)/shard_map/pallas_call | solution.py:101
  53.8 10.7 %collective-permute-done.kp_ref.vp_ref.k_ref.v_ref = bf16[2,128,2048]{2,1,0:T(8,128)(2,1)S(1)} collective-permute-done((bf16[2,128,2048]{2,1,0:T(8,128)(2,1)}, bf16[2,128,2048]{2,1,0:T(8,128)(2,1)S(1)}, u32[]{:S(2)}, u32[]{:S(2)}) %collective-permute-start) | collective-permute-done | bytes 1048608 | tf_op jit(solution)/shard_map/ppermute | solution.py:20
  64.6 2.8 %collective-permute-done.4.rest_1_.far_ref = f32[2,128,16]{2,1,0:T(8,128)S(1)} collective-permute-done((f32[2,128,16]{2,1,0:T(8,128)}, f32[2,128,16]{2,1,0:T(8,128)S(1)}, u32[]{:S(2)}, u32[]{:S(2)}) %collective-permute-start.4) | collective-permute-done | bytes 16416 | tf_op jit(solution)/shard_map/ppermute | solution.py:20
  67.4 0.6 copy-done.3
  68.0 3.4 %shard_map.53 = (bf16[128,2048]{1,0:T(8,128)(2,1)}, f32[2,128,16]{2,1,0:T(8,128)}) custom-call(bf16[128,2048]{1,0:T(8,128)(2,1)} %copy-done.10, bf16[2,128,2048]{2,1,0:T(8,128)(2,1)} %copy-done.1, bf16[2,128,2048]{2,1,0:T(8,128)(2,1)} %copy-done.1, f32[2,128,16]{2,1,0:T(8,128)} %get-tuple-element.12.rest_0_.near_ref, f32[2,128,16]{2,1,0:T(8,128)} %copy-done.3), custom_call_target="tpu_custom_call" | custom-call | tf_op jit(solution)/shard_map/pallas_call | solution.py:80
  71.4 1.9 %collective-permute-start.5 = (bf16[128,2048]{1,0:T(8,128)(2,1)}, bf16[128,2048]{1,0:T(8,128)(2,1)S(1)}, u32[]{:S(2)}, u32[]{:S(2)}) collective-permute-start(bf16[128,2048]{1,0:T(8,128)(2,1)} %get-tuple-element.14), channel_id=1, source_target_pairs={{0,4},{4,8},{8,12},{12,16},{16,20},{20,24},{24,28},{28,32},{32,36}... | collective-permute-start | bytes 1572872 | tf_op jit(solution)/shard_map/ppermute | solution.py:20
  73.4 0.1 copy.12
  73.4 3.6 %shard_map.50 = (f32[128,2048]{1,0:T(8,128)}, f32[2,128,16]{2,1,0:T(8,128)}) custom-call(s32[1]{0:T(128)} %bitcast.block_ref, bf16[128,4096]{1,0:T(8,128)(2,1)} %q_ref.3, bf16[128,4096]{1,0:T(8,128)(2,1)} %k_ref.3, bf16[128,4096]{1,0:T(8,128)(2,1)} %v_ref.3, bf16[2,128,2048]{2,1,0:T(8,128)(2,1)} %copy-done.1, bf16[2,128,2048]{2,1,0:T(8,128)(2,1)} %copy-done.1), custom_call_target="tpu_custom_call" | custom-call | tf_op jit(solution)/shard_map/pallas_call | solution.py:101
  77.0 1.0 copy.13
  78.0 1.9 %collective-permute-start.6 = (f32[2,128,16]{2,1,0:T(8,128)S(1)}, f32[2,128,16]{2,1,0:T(8,128)S(1)}, u32[]{:S(2)}, u32[]{:S(2)}) collective-permute-start(f32[2,128,16]{2,1,0:T(8,128)S(1)} %copy-done.11), channel_id=1, source_target_pairs={{0,4},{4,8},{8,12},{12,16},{16,20},{20,24},{24,28},{28,32},{32,36}... | collective-permute-start | bytes 49160 | tf_op jit(solution)/shard_map/ppermute | solution.py:20
  80.0 0.1 copy.14
  80.0 16.4 %collective-permute-done.6.far_ref = f32[2,128,16]{2,1,0:T(8,128)S(1)} collective-permute-done((f32[2,128,16]{2,1,0:T(8,128)S(1)}, f32[2,128,16]{2,1,0:T(8,128)S(1)}, u32[]{:S(2)}, u32[]{:S(2)}) %collective-permute-start.6) | collective-permute-done | bytes 16416 | tf_op jit(solution)/shard_map/ppermute | solution.py:20
  96.5 0.1 copy.15
  96.5 0.6 fusion.4
  97.2 0.8 copy-done.9
  98.0 2.8 %shard_map.54.rest_0_ = bf16[128,4096]{1,0:T(8,128)(2,1)} custom-call(s32[1]{0:T(128)} %bitcast.block_ref, f32[128,2048]{1,0:T(8,128)} %get-tuple-element.16.mixed_ref, f32[2,128,16]{2,1,0:T(8,128)} %get-tuple-element.12.rest_0_.near_ref, bf16[128,2048]{1,0:T(8,128)(2,1)} %copy-done.9, f32[2,128,16]{2,1,0:T(8,128)} %copy-done.3), custom_call_target="tpu_custom_call" | custom-call | tf_op jit(solution)/shard_map/pallas_call | solution.py:152
  100.7 0.8 copy-done.6
  101.5 2.8 %shard_map.55 = bf16[128,4096]{1,0:T(8,128)(2,1)} custom-call(s32[1]{0:T(128)} %bitcast.block_ref, f32[128,2048]{1,0:T(8,128)} %get-tuple-element.10.mixed_ref, f32[2,128,16]{2,1,0:T(8,128)} %get-tuple-element.11.near_ref, bf16[128,2048]{1,0:T(8,128)(2,1)} %copy-done.6, f32[2,128,16]{2,1,0:T(8,128)} %copy-done.8, ...), custom_call_target="tpu_custom_call", output_to_operand_aliasing={{}: (5, {})} | custom-call | tf_op jit(solution)/shard_map/pallas_call | solution.py:152
  (25 shorter events, 0.1 us)
Async XLA Ops:
  2.4 39.7 %collective-permute-start.2 = (bf16[2,128,2048]{2,1,0:T(8,128)(2,1)S(1)}, bf16[2,128,2048]{2,1,0:T(8,128)(2,1)S(1)}, u32[]{:S(2)}, u32[]{:S(2)}) collective-permute-start(bf16[2,128,2048]{2,1,0:T(8,128)(2,1)S(1)} %pad_maximum_fusion.1), channel_id=1, source_target_pairs={{0,4},{4,8},{8,12},{12,16},{16,20},{20,24},{24,28},{28,32},{32,36}... | collective-permute-start | bytes 3145736 | tf_op jit(solution)/shard_map/ppermute | solution.py:20
  5.8 4.5 %copy-start.2 = (bf16[128,4096]{1,0:T(8,128)(2,1)S(1)}, bf16[128,4096]{1,0:T(8,128)(2,1)}, u32[]{:S(2)}) copy-start(bf16[128,4096]{1,0:T(8,128)(2,1)} %q_ref.3) | copy-start | bytes 3145732
  6.9 57.7 %collective-permute-start = (bf16[2,128,2048]{2,1,0:T(8,128)(2,1)}, bf16[2,128,2048]{2,1,0:T(8,128)(2,1)S(1)}, u32[]{:S(2)}, u32[]{:S(2)}) collective-permute-start(bf16[2,128,2048]{2,1,0:T(8,128)(2,1)} %pad_maximum_fusion), channel_id=1, source_target_pairs={{0,4},{4,8},{8,12},{12,16},{16,20},{20,24},{24,28},{28,32},{32,36}... | collective-permute-start | bytes 3145736 | tf_op jit(solution)/shard_map/ppermute | solution.py:20
  11.2 25.0 %collective-permute-start.3 = (bf16[128,2048]{1,0:T(8,128)(2,1)S(1)}, bf16[128,2048]{1,0:T(8,128)(2,1)S(1)}, u32[]{:S(2)}, u32[]{:S(2)}) collective-permute-start(bf16[128,2048]{1,0:T(8,128)(2,1)S(1)} %get-tuple-element.18), channel_id=1, source_target_pairs={{4,0},{8,4},{12,8},{16,12},{20,16},{24,20},{28,24},{32,28},{36,32}... | collective-permute-start | bytes 1572872 | tf_op jit(solution)/shard_map/ppermute | solution.py:26
  23.9 29.9 %collective-permute-start.1 = (bf16[128,2048]{1,0:T(8,128)(2,1)}, bf16[128,2048]{1,0:T(8,128)(2,1)S(1)}, u32[]{:S(2)}, u32[]{:S(2)}) collective-permute-start(bf16[128,2048]{1,0:T(8,128)(2,1)} %get-tuple-element.19), channel_id=1, source_target_pairs={{4,0},{8,4},{12,8},{16,12},{20,16},{24,20},{28,24},{32,28},{36,32}... | collective-permute-start | bytes 1572872 | tf_op jit(solution)/shard_map/ppermute | solution.py:26
  36.2 5.9 %copy-start.7 = (bf16[128,2048]{1,0:T(8,128)(2,1)}, bf16[128,2048]{1,0:T(8,128)(2,1)S(1)}, u32[]{:S(2)}) copy-start(bf16[128,2048]{1,0:T(8,128)(2,1)S(1)} %collective-permute-done.3.q_ref) | copy-start | bytes 1572868
  42.1 1.0 copy-start
  46.5 20.9 %collective-permute-start.4 = (f32[2,128,16]{2,1,0:T(8,128)}, f32[2,128,16]{2,1,0:T(8,128)S(1)}, u32[]{:S(2)}, u32[]{:S(2)}) collective-permute-start(f32[2,128,16]{2,1,0:T(8,128)} %get-tuple-element.13), channel_id=1, source_target_pairs={{0,4},{4,8},{8,12},{12,16},{16,20},{20,24},{24,28},{28,32},{32,36}... | collective-permute-start | bytes 49160 | tf_op jit(solution)/shard_map/ppermute | solution.py:20
  48.4 48.8 %collective-permute-start.7 = (bf16[128,2048]{1,0:T(8,128)(2,1)}, bf16[128,2048]{1,0:T(8,128)(2,1)S(1)}, u32[]{:S(2)}, u32[]{:S(2)}) collective-permute-start(bf16[128,2048]{1,0:T(8,128)(2,1)} %get-tuple-element.17), channel_id=1, source_target_pairs={{0,4},{4,8},{8,12},{12,16},{16,20},{20,24},{24,28},{28,32},{32,36}... | collective-permute-start | bytes 1572872 | tf_op jit(solution)/shard_map/ppermute | solution.py:20
  53.8 13.6 %copy-start.10 = (bf16[128,2048]{1,0:T(8,128)(2,1)}, bf16[128,2048]{1,0:T(8,128)(2,1)S(1)}, u32[]{:S(2)}) copy-start(bf16[128,2048]{1,0:T(8,128)(2,1)S(1)} %collective-permute-done.1.q_ref) | copy-start | bytes 1572868
  64.6 2.8 %copy-start.1 = (bf16[2,128,2048]{2,1,0:T(8,128)(2,1)}, bf16[2,128,2048]{2,1,0:T(8,128)(2,1)S(1)}, u32[]{:S(2)}) copy-start(bf16[2,128,2048]{2,1,0:T(8,128)(2,1)S(1)} %collective-permute-done.kp_ref.vp_ref.k_ref.v_ref) | copy-start | bytes 3145732
  67.4 0.6 copy-start.3
  68.0 5.4 %copy-start.5 = (f32[2,128,16]{2,1,0:T(8,128)S(1)}, f32[2,128,16]{2,1,0:T(8,128)}, u32[]{:S(2)}) copy-start(f32[2,128,16]{2,1,0:T(8,128)} %get-tuple-element.12.rest_0_.near_ref) | copy-start | bytes 49156
  71.4 29.3 %collective-permute-start.5 = (bf16[128,2048]{1,0:T(8,128)(2,1)}, bf16[128,2048]{1,0:T(8,128)(2,1)S(1)}, u32[]{:S(2)}, u32[]{:S(2)}) collective-permute-start(bf16[128,2048]{1,0:T(8,128)(2,1)} %get-tuple-element.14), channel_id=1, source_target_pairs={{0,4},{4,8},{8,12},{12,16},{16,20},{20,24},{24,28},{28,32},{32,36}... | collective-permute-start | bytes 1572872 | tf_op jit(solution)/shard_map/ppermute | solution.py:20
  73.4 4.6 %copy-start.11 = (f32[2,128,16]{2,1,0:T(8,128)S(1)}, f32[2,128,16]{2,1,0:T(8,128)}, u32[]{:S(2)}) copy-start(f32[2,128,16]{2,1,0:T(8,128)} %get-tuple-element.15) | copy-start | bytes 49156
  77.0 2.9 %copy-start.4 = (f32[2,128,16]{2,1,0:T(8,128)S(1)}, f32[2,128,16]{2,1,0:T(8,128)}, u32[]{:S(2)}) copy-start(f32[2,128,16]{2,1,0:T(8,128)} %copy-done.3) | copy-start | bytes 49156
  78.0 18.4 %collective-permute-start.6 = (f32[2,128,16]{2,1,0:T(8,128)S(1)}, f32[2,128,16]{2,1,0:T(8,128)S(1)}, u32[]{:S(2)}, u32[]{:S(2)}) collective-permute-start(f32[2,128,16]{2,1,0:T(8,128)S(1)} %copy-done.11), channel_id=1, source_target_pairs={{0,4},{4,8},{8,12},{12,16},{16,20},{20,24},{24,28},{28,32},{32,36}... | collective-permute-start | bytes 49160 | tf_op jit(solution)/shard_map/ppermute | solution.py:20
  96.4 0.7 copy-start.8
  97.2 0.8 copy-start.9
  100.7 0.8 copy-start.6

commit v10 on v9

--- a/solution.py
+++ b/solution.py
@@ -194,8 +194,9 @@
     out = None
     for chunk in range(CHUNKS):
         out = merged_output(index_ref, chunk, width, *pieces[chunk], out)
-    stat_near = jnp.concatenate([piece[1] for piece in pieces], axis=0)
-    stat_far = jnp.concatenate([piece[3] for piece in pieces], axis=0)
+    out, stats = lax.optimization_barrier((out, [(piece[1], piece[3]) for piece in pieces]))
+    stat_near = jnp.concatenate([piece[0] for piece in stats], axis=0)
+    stat_far = jnp.concatenate([piece[1] for piece in stats], axis=0)
     return out, log_total(block_index, stat_near, stat_far)
 
 

time: 105 us -> 103 us (0.981)
  waiting for transfers between devices: 44.2 us -> 41.7 us
    ppermute x6, waiting for transfers between devices: 35.8 us -> 33.4 us  [from_behind(): return lax.ppermute(block, axis, route)]
    pallas_call x2 -> x0, local copies, waits for them, and re-layouts: 1.06 us -> none  [near_attention(): pl.pallas_call(near_kernel, grid_spec=pltpu.PrefetchScalarGridSpec(num_sc...]
    unnamed x24 -> x26, local copies, waits for them, and re-layouts: 3.23 us -> 4.08 us
  transfers between devices with their start and end apart: 8 -> 8, of which waited for: 5 -> 5; matrix products, arithmetic and copies ran while one was open for 4% -> 2% of each run, Pallas kernels for 16% -> 16%
where the time goes in v10:
time: 103 us; the launch traced here: 102 us
  waiting for transfers between devices  41.7 us (40%)
  starting transfers between devices  31.1 us (30%)
  Pallas kernels  19.5 us (19%)
  local copies, waits for them, and re-layouts  6.88 us (7%)
  other arithmetic  1.81 us (2%)
    ppermute x6, waiting for transfers between devices, from_behind(): return lax.ppermute(block, axis, route)  33.4 us
    ppermute x2, starting transfers between devices, from_ahead(): return lax.ppermute(block, axis, route)  16.7 us
    ppermute x6, starting transfers between devices, from_behind(): return lax.ppermute(block, axis, route)  14.4 us
    ppermute x2, waiting for transfers between devices, from_ahead(): return lax.ppermute(block, axis, route)  8.38 us
    pallas_call x2, Pallas kernels, near_attention(): pl.pallas_call(near_kernel, grid_spec=pltpu.PrefetchScalarGridSpec(num_sc...  7.08 us
    pallas_call x2, Pallas kernels, partial_attention(): pl.pallas_call(partial_kernel, grid=(steps,), in_specs=[block, key_block,...  6.77 us
    pallas_call x2, Pallas kernels, merged_output(): pl.pallas_call(merge_kernel, grid_spec=pltpu.PrefetchScalarGridSpec(num_s...  5.6 us
    unnamed x26, local copies, waits for them, and re-layouts  4.08 us
  transfers between devices with their start and end apart: 8, of which 5 were waited for; matrix products, arithmetic and copies ran while one was open for 2% of the time, Pallas kernels for 16%

profile of v10, /device:TPU:56, one launch (start us, length us, event | category | flops | bytes accessed | tf_op | source)
XLA Modules:
  0.0 101.8 jit_solution(12073475757942585558)
XLA Ops:
  0.6 1.7 %slice_bitcast_fusion = (bf16[1,128,2048]{2,1,0:T(8,128)(2,1)S(1)}, bf16[1,128,2048]{2,1,0:T(8,128)(2,1)S(1)}, bf16[1,128,2048]{2,1,0:T(8,128)(2,1)S(1)}, bf16[1,128,2048]{2,1,0:T(8,128)(2,1)S(1)}) fusion(bf16[128,4096]{1,0:T(8,128)(2,1)} %v_ref.3, bf16[128,4096]{1,0:T(8,128)(2,1)} %k_ref.3), kind=kLoop, calls=%fused_computation.2 | loop fusion | bytes 4194304 | tf_op jit(solution)/shard_map/stack | solution.py:188
  2.3 0.1 pad_maximum_fusion.1
  2.4 3.4 %collective-permute-start.2 = (bf16[2,128,2048]{2,1,0:T(8,128)(2,1)S(1)}, bf16[2,128,2048]{2,1,0:T(8,128)(2,1)S(1)}, u32[]{:S(2)}, u32[]{:S(2)}) collective-permute-start(bf16[2,128,2048]{2,1,0:T(8,128)(2,1)S(1)} %pad_maximum_fusion.1), channel_id=1, source_target_pairs={{0,4},{4,8},{8,12},{12,16},{16,20},{20,24},{24,28},{28,32},{32,36}... | collective-permute-start | bytes 3145736 | tf_op jit(solution)/shard_map/ppermute | solution.py:20
  5.8 1.1 %pad_maximum_fusion = bf16[2,128,2048]{2,1,0:T(8,128)(2,1)} fusion(bf16[1,128,2048]{2,1,0:T(8,128)(2,1)S(1)} %get-tuple-element.33, bf16[1,128,2048]{2,1,0:T(8,128)(2,1)S(1)} %get-tuple-element.34), kind=kLoop, calls=%fused_computation | loop fusion | flops 524288 | bytes 2097152 | tf_op jit(solution)/shard_map/stack | solution.py:188
  6.9 3.4 %collective-permute-start = (bf16[2,128,2048]{2,1,0:T(8,128)(2,1)}, bf16[2,128,2048]{2,1,0:T(8,128)(2,1)S(1)}, u32[]{:S(2)}, u32[]{:S(2)}) collective-permute-start(bf16[2,128,2048]{2,1,0:T(8,128)(2,1)} %pad_maximum_fusion), channel_id=1, source_target_pairs={{0,4},{4,8},{8,12},{12,16},{16,20},{20,24},{24,28},{28,32},{32,36}... | collective-permute-start | bytes 3145736 | tf_op jit(solution)/shard_map/ppermute | solution.py:20
  10.3 0.9 fusion.8
  11.2 12.7 %collective-permute-start.3 = (bf16[128,2048]{1,0:T(8,128)(2,1)S(1)}, bf16[128,2048]{1,0:T(8,128)(2,1)S(1)}, u32[]{:S(2)}, u32[]{:S(2)}) collective-permute-start(bf16[128,2048]{1,0:T(8,128)(2,1)S(1)} %get-tuple-element.28), channel_id=1, source_target_pairs={{4,0},{8,4},{12,8},{16,12},{20,16},{24,20},{28,24},{32,28},{36,32}... | collective-permute-start | bytes 1572872 | tf_op jit(solution)/shard_map/ppermute | solution.py:26
  23.9 3.9 %collective-permute-start.1 = (bf16[128,2048]{1,0:T(8,128)(2,1)}, bf16[128,2048]{1,0:T(8,128)(2,1)S(1)}, u32[]{:S(2)}, u32[]{:S(2)}) collective-permute-start(bf16[128,2048]{1,0:T(8,128)(2,1)} %get-tuple-element.29), channel_id=1, source_target_pairs={{4,0},{8,4},{12,8},{16,12},{20,16},{24,20},{28,24},{32,28},{36,32}... | collective-permute-start | bytes 1572872 | tf_op jit(solution)/shard_map/ppermute | solution.py:26
  27.8 8.4 %collective-permute-done.3.q_ref = bf16[128,2048]{1,0:T(8,128)(2,1)S(1)} collective-permute-done((bf16[128,2048]{1,0:T(8,128)(2,1)S(1)}, bf16[128,2048]{1,0:T(8,128)(2,1)S(1)}, u32[]{:S(2)}, u32[]{:S(2)}) %collective-permute-start.3) | collective-permute-done | bytes 524320 | tf_op jit(solution)/shard_map/ppermute | solution.py:26
  36.2 5.9 %collective-permute-done.2.kp_ref.vp_ref.k_ref.v_ref = bf16[2,128,2048]{2,1,0:T(8,128)(2,1)S(1)} collective-permute-done((bf16[2,128,2048]{2,1,0:T(8,128)(2,1)S(1)}, bf16[2,128,2048]{2,1,0:T(8,128)(2,1)S(1)}, u32[]{:S(2)}, u32[]{:S(2)}) %collective-permute-start.2) | collective-permute-done | bytes 1048608 | tf_op jit(solution)/shard_map/ppermute | solution.py:20
  42.1 1.0 copy-done
  43.0 3.4 %shard_map.52 = (bf16[128,2048]{1,0:T(8,128)(2,1)}, f32[2,128,16]{2,1,0:T(8,128)}) custom-call(bf16[128,2048]{1,0:T(8,128)(2,1)} %copy-done.7, bf16[2,128,2048]{2,1,0:T(8,128)(2,1)} %copy-done, bf16[2,128,2048]{2,1,0:T(8,128)(2,1)} %copy-done), custom_call_target="tpu_custom_call" | custom-call | tf_op jit(solution)/shard_map/pallas_call | solution.py:80
  46.4 1.9 %collective-permute-start.4 = (f32[2,128,16]{2,1,0:T(8,128)}, f32[2,128,16]{2,1,0:T(8,128)S(1)}, u32[]{:S(2)}, u32[]{:S(2)}) collective-permute-start(f32[2,128,16]{2,1,0:T(8,128)} %get-tuple-element.18), channel_id=1, source_target_pairs={{0,4},{4,8},{8,12},{12,16},{16,20},{20,24},{24,28},{28,32},{32,36}... | collective-permute-start | bytes 49160 | tf_op jit(solution)/shard_map/ppermute | solution.py:20
  48.4 1.9 %collective-permute-start.7 = (bf16[128,2048]{1,0:T(8,128)(2,1)}, bf16[128,2048]{1,0:T(8,128)(2,1)S(1)}, u32[]{:S(2)}, u32[]{:S(2)}) collective-permute-start(bf16[128,2048]{1,0:T(8,128)(2,1)} %get-tuple-element.22), channel_id=1, source_target_pairs={{0,4},{4,8},{8,12},{12,16},{16,20},{20,24},{24,28},{28,32},{32,36}... | collective-permute-start | bytes 1572872 | tf_op jit(solution)/shard_map/ppermute | solution.py:20
  50.3 3.5 %shard_map.51 = (f32[128,2048]{1,0:T(8,128)}, f32[2,128,16]{2,1,0:T(8,128)}) custom-call(s32[1]{0:T(128)} %bitcast.block_ref, bf16[128,4096]{1,0:T(8,128)(2,1)} %q_ref.3, bf16[128,4096]{1,0:T(8,128)(2,1)} %k_ref.3, bf16[128,4096]{1,0:T(8,128)(2,1)} %v_ref.3, bf16[2,128,2048]{2,1,0:T(8,128)(2,1)} %copy-done, bf16[2,128,2048]{2,1,0:T(8,128)(2,1)} %copy-done), custom_call_target="tpu_custom_call" | custom-call | tf_op jit(solution)/shard_map/pallas_call | solution.py:101
  53.8 10.7 %collective-permute-done.kp_ref.vp_ref.k_ref.v_ref = bf16[2,128,2048]{2,1,0:T(8,128)(2,1)S(1)} collective-permute-done((bf16[2,128,2048]{2,1,0:T(8,128)(2,1)}, bf16[2,128,2048]{2,1,0:T(8,128)(2,1)S(1)}, u32[]{:S(2)}, u32[]{:S(2)}) %collective-permute-start) | collective-permute-done | bytes 1048608 | tf_op jit(solution)/shard_map/ppermute | solution.py:20
  64.6 2.8 %collective-permute-done.4.rest_1_.far_ref = f32[2,128,16]{2,1,0:T(8,128)S(1)} collective-permute-done((f32[2,128,16]{2,1,0:T(8,128)}, f32[2,128,16]{2,1,0:T(8,128)S(1)}, u32[]{:S(2)}, u32[]{:S(2)}) %collective-permute-start.4) | collective-permute-done | bytes 16416 | tf_op jit(solution)/shard_map/ppermute | solution.py:20
  67.4 0.6 copy-done.3
  68.0 3.4 %shard_map.53 = (bf16[128,2048]{1,0:T(8,128)(2,1)}, f32[2,128,16]{2,1,0:T(8,128)}) custom-call(bf16[128,2048]{1,0:T(8,128)(2,1)} %copy-done.11, bf16[2,128,2048]{2,1,0:T(8,128)(2,1)} %copy-done.1, bf16[2,128,2048]{2,1,0:T(8,128)(2,1)} %copy-done.1, f32[2,128,16]{2,1,0:T(8,128)} %get-tuple-element.24.rest_0_.near_ref, f32[2,128,16]{2,1,0:T(8,128)} %copy-done.3), custom_call_target="tpu_custom_call" | custom-call | tf_op jit(solution)/shard_map/pallas_call | solution.py:80
  71.4 1.9 %collective-permute-start.5 = (bf16[128,2048]{1,0:T(8,128)(2,1)}, bf16[128,2048]{1,0:T(8,128)(2,1)S(1)}, u32[]{:S(2)}, u32[]{:S(2)}) collective-permute-start(bf16[128,2048]{1,0:T(8,128)(2,1)} %get-tuple-element.19), channel_id=1, source_target_pairs={{0,4},{4,8},{8,12},{12,16},{16,20},{20,24},{24,28},{28,32},{32,36}... | collective-permute-start | bytes 1572872 | tf_op jit(solution)/shard_map/ppermute | solution.py:20
  73.3 1.9 %collective-permute-start.6 = (f32[2,128,16]{2,1,0:T(8,128)}, f32[2,128,16]{2,1,0:T(8,128)S(1)}, u32[]{:S(2)}, u32[]{:S(2)}) collective-permute-start(f32[2,128,16]{2,1,0:T(8,128)} %get-tuple-element.20), channel_id=1, source_target_pairs={{0,4},{4,8},{8,12},{12,16},{16,20},{20,24},{24,28},{28,32},{32,36}... | collective-permute-start | bytes 49160 | tf_op jit(solution)/shard_map/ppermute | solution.py:20
  75.2 3.6 %shard_map.50 = (f32[128,2048]{1,0:T(8,128)}, f32[2,128,16]{2,1,0:T(8,128)}) custom-call(s32[1]{0:T(128)} %bitcast.block_ref, bf16[128,4096]{1,0:T(8,128)(2,1)} %q_ref.3, bf16[128,4096]{1,0:T(8,128)(2,1)} %k_ref.3, bf16[128,4096]{1,0:T(8,128)(2,1)} %v_ref.3, bf16[2,128,2048]{2,1,0:T(8,128)(2,1)} %copy-done.1, bf16[2,128,2048]{2,1,0:T(8,128)(2,1)} %copy-done.1), custom_call_target="tpu_custom_call" | custom-call | tf_op jit(solution)/shard_map/pallas_call | solution.py:101
  78.8 0.8 copy-done.12
  79.6 2.8 %shard_map.54.rest_0_ = bf16[128,4096]{1,0:T(8,128)(2,1)} custom-call(s32[1]{0:T(128)} %bitcast.block_ref, f32[128,2048]{1,0:T(8,128)} %get-tuple-element.21.mixed_ref, f32[2,128,16]{2,1,0:T(8,128)} %get-tuple-element.24.rest_0_.near_ref, bf16[128,2048]{1,0:T(8,128)(2,1)} %copy-done.12, f32[2,128,16]{2,1,0:T(8,128)} %copy-done.3), custom_call_target="tpu_custom_call" | custom-call | tf_op jit(solution)/shard_map/pallas_call | solution.py:152
  82.4 14.0 %collective-permute-done.6.far_ref = f32[2,128,16]{2,1,0:T(8,128)S(1)} collective-permute-done((f32[2,128,16]{2,1,0:T(8,128)}, f32[2,128,16]{2,1,0:T(8,128)S(1)}, u32[]{:S(2)}, u32[]{:S(2)}) %collective-permute-start.6) | collective-permute-done | bytes 16416 | tf_op jit(solution)/shard_map/ppermute | solution.py:20
  96.4 0.7 copy-done.8
  97.0 0.2 copy-done.6
  97.2 2.8 %shard_map.55 = bf16[128,4096]{1,0:T(8,128)(2,1)} custom-call(s32[1]{0:T(128)} %bitcast.block_ref, f32[128,2048]{1,0:T(8,128)} %get-tuple-element.15.mixed_ref, f32[2,128,16]{2,1,0:T(8,128)} %get-tuple-element.25.near_ref, bf16[128,2048]{1,0:T(8,128)(2,1)} %copy-done.6, f32[2,128,16]{2,1,0:T(8,128)} %copy-done.8, ...), custom_call_target="tpu_custom_call", output_to_operand_aliasing={{}: (5, {})} | custom-call | tf_op jit(solution)/shard_map/pallas_call | solution.py:152
  100.1 0.1 copy.12
  100.1 0.1 copy.13
  100.2 0.8 copy-done.4
  101.1 0.6 fusion.4
  (27 shorter events, 0.2 us)
Async XLA Ops:
  2.4 39.7 %collective-permute-start.2 = (bf16[2,128,2048]{2,1,0:T(8,128)(2,1)S(1)}, bf16[2,128,2048]{2,1,0:T(8,128)(2,1)S(1)}, u32[]{:S(2)}, u32[]{:S(2)}) collective-permute-start(bf16[2,128,2048]{2,1,0:T(8,128)(2,1)S(1)} %pad_maximum_fusion.1), channel_id=1, source_target_pairs={{0,4},{4,8},{8,12},{12,16},{16,20},{20,24},{24,28},{28,32},{32,36}... | collective-permute-start | bytes 3145736 | tf_op jit(solution)/shard_map/ppermute | solution.py:20
  5.8 4.5 %copy-start.2 = (bf16[128,4096]{1,0:T(8,128)(2,1)S(1)}, bf16[128,4096]{1,0:T(8,128)(2,1)}, u32[]{:S(2)}) copy-start(bf16[128,4096]{1,0:T(8,128)(2,1)} %q_ref.3) | copy-start | bytes 3145732
  6.9 57.7 %collective-permute-start = (bf16[2,128,2048]{2,1,0:T(8,128)(2,1)}, bf16[2,128,2048]{2,1,0:T(8,128)(2,1)S(1)}, u32[]{:S(2)}, u32[]{:S(2)}) collective-permute-start(bf16[2,128,2048]{2,1,0:T(8,128)(2,1)} %pad_maximum_fusion), channel_id=1, source_target_pairs={{0,4},{4,8},{8,12},{12,16},{16,20},{20,24},{24,28},{28,32},{32,36}... | collective-permute-start | bytes 3145736 | tf_op jit(solution)/shard_map/ppermute | solution.py:20
  11.2 25.0 %collective-permute-start.3 = (bf16[128,2048]{1,0:T(8,128)(2,1)S(1)}, bf16[128,2048]{1,0:T(8,128)(2,1)S(1)}, u32[]{:S(2)}, u32[]{:S(2)}) collective-permute-start(bf16[128,2048]{1,0:T(8,128)(2,1)S(1)} %get-tuple-element.28), channel_id=1, source_target_pairs={{4,0},{8,4},{12,8},{16,12},{20,16},{24,20},{28,24},{32,28},{36,32}... | collective-permute-start | bytes 1572872 | tf_op jit(solution)/shard_map/ppermute | solution.py:26
  23.9 29.9 %collective-permute-start.1 = (bf16[128,2048]{1,0:T(8,128)(2,1)}, bf16[128,2048]{1,0:T(8,128)(2,1)S(1)}, u32[]{:S(2)}, u32[]{:S(2)}) collective-permute-start(bf16[128,2048]{1,0:T(8,128)(2,1)} %get-tuple-element.29), channel_id=1, source_target_pairs={{4,0},{8,4},{12,8},{16,12},{20,16},{24,20},{28,24},{32,28},{36,32}... | collective-permute-start | bytes 1572872 | tf_op jit(solution)/shard_map/ppermute | solution.py:26
  36.2 5.9 %copy-start.7 = (bf16[128,2048]{1,0:T(8,128)(2,1)}, bf16[128,2048]{1,0:T(8,128)(2,1)S(1)}, u32[]{:S(2)}) copy-start(bf16[128,2048]{1,0:T(8,128)(2,1)S(1)} %collective-permute-done.3.q_ref) | copy-start | bytes 1572868
  42.1 1.0 copy-start
  46.4 20.9 %collective-permute-start.4 = (f32[2,128,16]{2,1,0:T(8,128)}, f32[2,128,16]{2,1,0:T(8,128)S(1)}, u32[]{:S(2)}, u32[]{:S(2)}) collective-permute-start(f32[2,128,16]{2,1,0:T(8,128)} %get-tuple-element.18), channel_id=1, source_target_pairs={{0,4},{4,8},{8,12},{12,16},{16,20},{20,24},{24,28},{28,32},{32,36}... | collective-permute-start | bytes 49160 | tf_op jit(solution)/shard_map/ppermute | solution.py:20
  48.4 30.4 %collective-permute-start.7 = (bf16[128,2048]{1,0:T(8,128)(2,1)}, bf16[128,2048]{1,0:T(8,128)(2,1)S(1)}, u32[]{:S(2)}, u32[]{:S(2)}) collective-permute-start(bf16[128,2048]{1,0:T(8,128)(2,1)} %get-tuple-element.22), channel_id=1, source_target_pairs={{0,4},{4,8},{8,12},{12,16},{16,20},{20,24},{24,28},{28,32},{32,36}... | collective-permute-start | bytes 1572872 | tf_op jit(solution)/shard_map/ppermute | solution.py:20
  53.8 13.5 %copy-start.11 = (bf16[128,2048]{1,0:T(8,128)(2,1)}, bf16[128,2048]{1,0:T(8,128)(2,1)S(1)}, u32[]{:S(2)}) copy-start(bf16[128,2048]{1,0:T(8,128)(2,1)S(1)} %collective-permute-done.1.q_ref) | copy-start | bytes 1572868
  64.6 2.8 %copy-start.1 = (bf16[2,128,2048]{2,1,0:T(8,128)(2,1)}, bf16[2,128,2048]{2,1,0:T(8,128)(2,1)S(1)}, u32[]{:S(2)}) copy-start(bf16[2,128,2048]{2,1,0:T(8,128)(2,1)S(1)} %collective-permute-done.kp_ref.vp_ref.k_ref.v_ref) | copy-start | bytes 3145732
  67.4 0.7 copy-start.3
  71.4 25.0 %collective-permute-start.5 = (bf16[128,2048]{1,0:T(8,128)(2,1)}, bf16[128,2048]{1,0:T(8,128)(2,1)S(1)}, u32[]{:S(2)}, u32[]{:S(2)}) collective-permute-start(bf16[128,2048]{1,0:T(8,128)(2,1)} %get-tuple-element.19), channel_id=1, source_target_pairs={{0,4},{4,8},{8,12},{12,16},{16,20},{20,24},{24,28},{28,32},{32,36}... | collective-permute-start | bytes 1572872 | tf_op jit(solution)/shard_map/ppermute | solution.py:20
  73.3 23.1 %collective-permute-start.6 = (f32[2,128,16]{2,1,0:T(8,128)}, f32[2,128,16]{2,1,0:T(8,128)S(1)}, u32[]{:S(2)}, u32[]{:S(2)}) collective-permute-start(f32[2,128,16]{2,1,0:T(8,128)} %get-tuple-element.20), channel_id=1, source_target_pairs={{0,4},{4,8},{8,12},{12,16},{16,20},{20,24},{24,28},{28,32},{32,36}... | collective-permute-start | bytes 49160 | tf_op jit(solution)/shard_map/ppermute | solution.py:20
  78.8 0.8 copy-start.12
  96.4 0.7 copy-start.8
  96.4 0.8 copy-start.6
  97.2 2.8 %copy-start.5 = (f32[2,128,16]{2,1,0:T(8,128)S(1)}, f32[2,128,16]{2,1,0:T(8,128)}, u32[]{:S(2)}) copy-start(f32[2,128,16]{2,1,0:T(8,128)} %get-tuple-element.24.rest_0_.near_ref) | copy-start | bytes 49156
  97.2 2.9 %copy-start.10 = (f32[2,128,16]{2,1,0:T(8,128)S(1)}, f32[2,128,16]{2,1,0:T(8,128)}, u32[]{:S(2)}) copy-start(f32[2,128,16]{2,1,0:T(8,128)} %get-tuple-element.25.near_ref) | copy-start | bytes 49156
  100.1 0.9 copy-start.4
  100.1 0.9 copy-start.9

commit v11 on v10

--- a/solution.py
+++ b/solution.py
@@ -8,7 +8,7 @@
 from jax.sharding import PartitionSpec as P
 
 HEAD_DIM = 128
-HEADS_PER_STEP = 8
+HEADS_PER_STEP = 16
 CHUNKS = 2
 SCALE = 1.0 / math.sqrt(HEAD_DIM)
 NT_DIMS = (((1,), (1,)), ((), ()))

time: 103 us -> 101 us (0.981)
  waiting for transfers between devices: 41.7 us -> 36.9 us
  Pallas kernels: 19.5 us -> 21.6 us
    ppermute x6, waiting for transfers between devices: 33.4 us -> 28.5 us  [from_behind(): return lax.ppermute(block, axis, route)]
    pallas_call x2, Pallas kernels: 7.08 us -> 9 us  [near_attention(): pl.pallas_call(near_kernel, grid_spec=pltpu.PrefetchScalarGridSpec(num_sc...]
  transfers between devices with their start and end apart: 8 -> 8, of which waited for: 5 -> 5; matrix products, arithmetic and copies ran while one was open for 2% -> 2% of each run, Pallas kernels for 16% -> 19%
where the time goes in v11:
time: 101 us; the launch traced here: 99.9 us
  waiting for transfers between devices  36.9 us (37%)
  starting transfers between devices  31.1 us (31%)
  Pallas kernels  21.6 us (21%)
  local copies, waits for them, and re-layouts  7.67 us (8%)
  other arithmetic  1.82 us (2%)
    ppermute x6, waiting for transfers between devices, from_behind(): return lax.ppermute(block, axis, route)  28.5 us
    ppermute x2, starting transfers between devices, from_ahead(): return lax.ppermute(block, axis, route)  16.7 us
    ppermute x6, starting transfers between devices, from_behind(): return lax.ppermute(block, axis, route)  14.4 us
    pallas_call x2, Pallas kernels, near_attention(): pl.pallas_call(near_kernel, grid_spec=pltpu.PrefetchScalarGridSpec(num_sc...  9 us
    ppermute x2, waiting for transfers between devices, from_ahead(): return lax.ppermute(block, axis, route)  8.38 us
    pallas_call x2, Pallas kernels, partial_attention(): pl.pallas_call(partial_kernel, grid=(steps,), in_specs=[block, key_block,...  6.73 us
    pallas_call x2, Pallas kernels, merged_output(): pl.pallas_call(merge_kernel, grid_spec=pltpu.PrefetchScalarGridSpec(num_s...  5.87 us
    unnamed x26, local copies, waits for them, and re-layouts  4.85 us
  transfers between devices with their start and end apart: 8, of which 5 were waited for; matrix products, arithmetic and copies ran while one was open for 2% of the time, Pallas kernels for 19%

profile of v11, /device:TPU:56, one launch (start us, length us, event | category | flops | bytes accessed | tf_op | source)
XLA Modules:
  0.0 99.9 jit_solution(7351839371414993834)
XLA Ops:
  0.6 1.7 %slice_bitcast_fusion = (bf16[1,128,2048]{2,1,0:T(8,128)(2,1)S(1)}, bf16[1,128,2048]{2,1,0:T(8,128)(2,1)S(1)}, bf16[1,128,2048]{2,1,0:T(8,128)(2,1)S(1)}, bf16[1,128,2048]{2,1,0:T(8,128)(2,1)S(1)}) fusion(bf16[128,4096]{1,0:T(8,128)(2,1)} %v_ref.3, bf16[128,4096]{1,0:T(8,128)(2,1)} %k_ref.3), kind=kLoop, calls=%fused_computation.2 | loop fusion | bytes 4194304 | tf_op jit(solution)/shard_map/stack | solution.py:188
  2.3 0.1 pad_maximum_fusion.1
  2.4 3.4 %collective-permute-start.2 = (bf16[2,128,2048]{2,1,0:T(8,128)(2,1)S(1)}, bf16[2,128,2048]{2,1,0:T(8,128)(2,1)S(1)}, u32[]{:S(2)}, u32[]{:S(2)}) collective-permute-start(bf16[2,128,2048]{2,1,0:T(8,128)(2,1)S(1)} %pad_maximum_fusion.1), channel_id=1, source_target_pairs={{0,4},{4,8},{8,12},{12,16},{16,20},{20,24},{24,28},{28,32},{32,36}... | collective-permute-start | bytes 3145736 | tf_op jit(solution)/shard_map/ppermute | solution.py:20
  5.8 1.1 %pad_maximum_fusion = bf16[2,128,2048]{2,1,0:T(8,128)(2,1)} fusion(bf16[1,128,2048]{2,1,0:T(8,128)(2,1)S(1)} %get-tuple-element.33, bf16[1,128,2048]{2,1,0:T(8,128)(2,1)S(1)} %get-tuple-element.38), kind=kLoop, calls=%fused_computation | loop fusion | flops 524288 | bytes 2097152 | tf_op jit(solution)/shard_map/stack | solution.py:188
  6.9 3.4 %collective-permute-start = (bf16[2,128,2048]{2,1,0:T(8,128)(2,1)}, bf16[2,128,2048]{2,1,0:T(8,128)(2,1)S(1)}, u32[]{:S(2)}, u32[]{:S(2)}) collective-permute-start(bf16[2,128,2048]{2,1,0:T(8,128)(2,1)} %pad_maximum_fusion), channel_id=1, source_target_pairs={{0,4},{4,8},{8,12},{12,16},{16,20},{20,24},{24,28},{28,32},{32,36}... | collective-permute-start | bytes 3145736 | tf_op jit(solution)/shard_map/ppermute | solution.py:20
  10.3 0.9 fusion.7
  11.2 12.7 %collective-permute-start.3 = (bf16[128,2048]{1,0:T(8,128)(2,1)S(1)}, bf16[128,2048]{1,0:T(8,128)(2,1)S(1)}, u32[]{:S(2)}, u32[]{:S(2)}) collective-permute-start(bf16[128,2048]{1,0:T(8,128)(2,1)S(1)} %get-tuple-element.28), channel_id=1, source_target_pairs={{4,0},{8,4},{12,8},{16,12},{20,16},{24,20},{28,24},{32,28},{36,32}... | collective-permute-start | bytes 1572872 | tf_op jit(solution)/shard_map/ppermute | solution.py:26
  23.9 3.9 %collective-permute-start.1 = (bf16[128,2048]{1,0:T(8,128)(2,1)}, bf16[128,2048]{1,0:T(8,128)(2,1)S(1)}, u32[]{:S(2)}, u32[]{:S(2)}) collective-permute-start(bf16[128,2048]{1,0:T(8,128)(2,1)} %get-tuple-element.29), channel_id=1, source_target_pairs={{4,0},{8,4},{12,8},{16,12},{20,16},{24,20},{28,24},{32,28},{36,32}... | collective-permute-start | bytes 1572872 | tf_op jit(solution)/shard_map/ppermute | solution.py:26
  27.9 8.4 %collective-permute-done.3.q_ref = bf16[128,2048]{1,0:T(8,128)(2,1)S(1)} collective-permute-done((bf16[128,2048]{1,0:T(8,128)(2,1)S(1)}, bf16[128,2048]{1,0:T(8,128)(2,1)S(1)}, u32[]{:S(2)}, u32[]{:S(2)}) %collective-permute-start.3) | collective-permute-done | bytes 524320 | tf_op jit(solution)/shard_map/ppermute | solution.py:26
  36.2 5.8 %collective-permute-done.2.kp_ref.vp_ref.k_ref.v_ref = bf16[2,128,2048]{2,1,0:T(8,128)(2,1)S(1)} collective-permute-done((bf16[2,128,2048]{2,1,0:T(8,128)(2,1)S(1)}, bf16[2,128,2048]{2,1,0:T(8,128)(2,1)S(1)}, u32[]{:S(2)}, u32[]{:S(2)}) %collective-permute-start.2) | collective-permute-done | bytes 1048608 | tf_op jit(solution)/shard_map/ppermute | solution.py:20
  42.1 1.0 copy-done.1
  43.0 3.4 %shard_map.52 = (bf16[128,2048]{1,0:T(8,128)(2,1)}, f32[1,128,32]{2,1,0:T(8,128)}) custom-call(bf16[128,2048]{1,0:T(8,128)(2,1)} %copy-done.6, bf16[2,128,2048]{2,1,0:T(8,128)(2,1)} %copy-done.1, bf16[2,128,2048]{2,1,0:T(8,128)(2,1)} %copy-done.1), custom_call_target="tpu_custom_call" | custom-call | tf_op jit(solution)/shard_map/pallas_call | solution.py:80
  46.4 1.9 %collective-permute-start.4 = (f32[1,128,32]{2,1,0:T(8,128)}, f32[1,128,32]{2,1,0:T(8,128)S(1)}, u32[]{:S(2)}, u32[]{:S(2)}) collective-permute-start(f32[1,128,32]{2,1,0:T(8,128)} %get-tuple-element.18), channel_id=1, source_target_pairs={{0,4},{4,8},{8,12},{12,16},{16,20},{20,24},{24,28},{28,32},{32,36}... | collective-permute-start | bytes 49160 | tf_op jit(solution)/shard_map/ppermute | solution.py:20
  48.3 1.9 %collective-permute-start.7 = (bf16[128,2048]{1,0:T(8,128)(2,1)}, bf16[128,2048]{1,0:T(8,128)(2,1)S(1)}, u32[]{:S(2)}, u32[]{:S(2)}) collective-permute-start(bf16[128,2048]{1,0:T(8,128)(2,1)} %get-tuple-element.22), channel_id=1, source_target_pairs={{0,4},{4,8},{8,12},{12,16},{16,20},{20,24},{24,28},{28,32},{32,36}... | collective-permute-start | bytes 1572872 | tf_op jit(solution)/shard_map/ppermute | solution.py:20
  50.3 4.5 %shard_map.51 = (f32[128,2048]{1,0:T(8,128)}, f32[1,128,32]{2,1,0:T(8,128)}) custom-call(s32[1]{0:T(128)} %bitcast.block_ref, bf16[128,4096]{1,0:T(8,128)(2,1)} %q_ref.3, bf16[128,4096]{1,0:T(8,128)(2,1)} %k_ref.3, bf16[128,4096]{1,0:T(8,128)(2,1)} %v_ref.3, bf16[2,128,2048]{2,1,0:T(8,128)(2,1)} %copy-done.1, bf16[2,128,2048]{2,1,0:T(8,128)(2,1)} %copy-done.1), custom_call_target="tpu_custom_call" | custom-call | tf_op jit(solution)/shard_map/pallas_call | solution.py:101
  54.8 9.8 %collective-permute-done.kp_ref.vp_ref.k_ref.v_ref = bf16[2,128,2048]{2,1,0:T(8,128)(2,1)S(1)} collective-permute-done((bf16[2,128,2048]{2,1,0:T(8,128)(2,1)}, bf16[2,128,2048]{2,1,0:T(8,128)(2,1)S(1)}, u32[]{:S(2)}, u32[]{:S(2)}) %collective-permute-start) | collective-permute-done | bytes 1048608 | tf_op jit(solution)/shard_map/ppermute | solution.py:20
  64.6 1.4 %collective-permute-done.4.rest_1_.far_ref = f32[1,128,32]{2,1,0:T(8,128)S(1)} collective-permute-done((f32[1,128,32]{2,1,0:T(8,128)}, f32[1,128,32]{2,1,0:T(8,128)S(1)}, u32[]{:S(2)}, u32[]{:S(2)}) %collective-permute-start.4) | collective-permute-done | bytes 16416 | tf_op jit(solution)/shard_map/ppermute | solution.py:20
  66.0 0.6 copy-done.3
  66.6 3.4 %shard_map.53 = (bf16[128,2048]{1,0:T(8,128)(2,1)}, f32[1,128,32]{2,1,0:T(8,128)}) custom-call(bf16[128,2048]{1,0:T(8,128)(2,1)} %copy-done.7, bf16[2,128,2048]{2,1,0:T(8,128)(2,1)} %copy-done, bf16[2,128,2048]{2,1,0:T(8,128)(2,1)} %copy-done, f32[1,128,32]{2,1,0:T(8,128)} %get-tuple-element.24.rest_0_.near_ref, f32[1,128,32]{2,1,0:T(8,128)} %copy-done.3), custom_call_target="tpu_custom_call" | custom-call | tf_op jit(solution)/shard_map/pallas_call | solution.py:80
  70.0 1.9 %collective-permute-start.5 = (bf16[128,2048]{1,0:T(8,128)(2,1)}, bf16[128,2048]{1,0:T(8,128)(2,1)S(1)}, u32[]{:S(2)}, u32[]{:S(2)}) collective-permute-start(bf16[128,2048]{1,0:T(8,128)(2,1)} %get-tuple-element.19), channel_id=1, source_target_pairs={{0,4},{4,8},{8,12},{12,16},{16,20},{20,24},{24,28},{28,32},{32,36}... | collective-permute-start | bytes 1572872 | tf_op jit(solution)/shard_map/ppermute | solution.py:20
  71.9 1.9 %collective-permute-start.6 = (f32[1,128,32]{2,1,0:T(8,128)}, f32[1,128,32]{2,1,0:T(8,128)S(1)}, u32[]{:S(2)}, u32[]{:S(2)}) collective-permute-start(f32[1,128,32]{2,1,0:T(8,128)} %get-tuple-element.20), channel_id=1, source_target_pairs={{0,4},{4,8},{8,12},{12,16},{16,20},{20,24},{24,28},{28,32},{32,36}... | collective-permute-start | bytes 49160 | tf_op jit(solution)/shard_map/ppermute | solution.py:20
  73.8 4.5 %shard_map.50 = (f32[128,2048]{1,0:T(8,128)}, f32[1,128,32]{2,1,0:T(8,128)}) custom-call(s32[1]{0:T(128)} %bitcast.block_ref, bf16[128,4096]{1,0:T(8,128)(2,1)} %q_ref.3, bf16[128,4096]{1,0:T(8,128)(2,1)} %k_ref.3, bf16[128,4096]{1,0:T(8,128)(2,1)} %v_ref.3, bf16[2,128,2048]{2,1,0:T(8,128)(2,1)} %copy-done, bf16[2,128,2048]{2,1,0:T(8,128)(2,1)} %copy-done), custom_call_target="tpu_custom_call" | custom-call | tf_op jit(solution)/shard_map/pallas_call | solution.py:101
  78.3 0.8 copy-done.8
  79.1 2.9 %shard_map.54.rest_0_ = bf16[128,4096]{1,0:T(8,128)(2,1)} custom-call(s32[1]{0:T(128)} %bitcast.block_ref, f32[128,2048]{1,0:T(8,128)} %get-tuple-element.21.mixed_ref, f32[1,128,32]{2,1,0:T(8,128)} %get-tuple-element.24.rest_0_.near_ref, bf16[128,2048]{1,0:T(8,128)(2,1)} %copy-done.8, f32[1,128,32]{2,1,0:T(8,128)} %copy-done.3), custom_call_target="tpu_custom_call" | custom-call | tf_op jit(solution)/shard_map/pallas_call | solution.py:152
  82.0 11.5 %collective-permute-done.6.far_ref = f32[1,128,32]{2,1,0:T(8,128)S(1)} collective-permute-done((f32[1,128,32]{2,1,0:T(8,128)}, f32[1,128,32]{2,1,0:T(8,128)S(1)}, u32[]{:S(2)}, u32[]{:S(2)}) %collective-permute-start.6) | collective-permute-done | bytes 16416 | tf_op jit(solution)/shard_map/ppermute | solution.py:20
  93.6 0.6 copy-done.10
  94.2 0.2 copy-done.9
  94.4 3.0 %shard_map.55 = bf16[128,4096]{1,0:T(8,128)(2,1)} custom-call(s32[1]{0:T(128)} %bitcast.block_ref, f32[128,2048]{1,0:T(8,128)} %get-tuple-element.15.mixed_ref, f32[1,128,32]{2,1,0:T(8,128)} %get-tuple-element.25.near_ref, bf16[128,2048]{1,0:T(8,128)(2,1)} %copy-done.9, f32[1,128,32]{2,1,0:T(8,128)} %copy-done.10, ...), custom_call_target="tpu_custom_call", output_to_operand_aliasing={{}: (5, {})} | custom-call | tf_op jit(solution)/shard_map/pallas_call | solution.py:152
  97.4 0.8 copy-done.12
  98.3 0.8 copy-done.4
  99.2 0.1 copy.15
  99.3 0.6 fusion.2
  (29 shorter events, 0.3 us)
Async XLA Ops:
  2.4 39.7 %collective-permute-start.2 = (bf16[2,128,2048]{2,1,0:T(8,128)(2,1)S(1)}, bf16[2,128,2048]{2,1,0:T(8,128)(2,1)S(1)}, u32[]{:S(2)}, u32[]{:S(2)}) collective-permute-start(bf16[2,128,2048]{2,1,0:T(8,128)(2,1)S(1)} %pad_maximum_fusion.1), channel_id=1, source_target_pairs={{0,4},{4,8},{8,12},{12,16},{16,20},{20,24},{24,28},{28,32},{32,36}... | collective-permute-start | bytes 3145736 | tf_op jit(solution)/shard_map/ppermute | solution.py:20
  5.8 4.5 %copy-start.2 = (bf16[128,4096]{1,0:T(8,128)(2,1)S(1)}, bf16[128,4096]{1,0:T(8,128)(2,1)}, u32[]{:S(2)}) copy-start(bf16[128,4096]{1,0:T(8,128)(2,1)} %q_ref.3) | copy-start | bytes 3145732
  6.9 57.7 %collective-permute-start = (bf16[2,128,2048]{2,1,0:T(8,128)(2,1)}, bf16[2,128,2048]{2,1,0:T(8,128)(2,1)S(1)}, u32[]{:S(2)}, u32[]{:S(2)}) collective-permute-start(bf16[2,128,2048]{2,1,0:T(8,128)(2,1)} %pad_maximum_fusion), channel_id=1, source_target_pairs={{0,4},{4,8},{8,12},{12,16},{16,20},{20,24},{24,28},{28,32},{32,36}... | collective-permute-start | bytes 3145736 | tf_op jit(solution)/shard_map/ppermute | solution.py:20
  11.2 25.0 %collective-permute-start.3 = (bf16[128,2048]{1,0:T(8,128)(2,1)S(1)}, bf16[128,2048]{1,0:T(8,128)(2,1)S(1)}, u32[]{:S(2)}, u32[]{:S(2)}) collective-permute-start(bf16[128,2048]{1,0:T(8,128)(2,1)S(1)} %get-tuple-element.28), channel_id=1, source_target_pairs={{4,0},{8,4},{12,8},{16,12},{20,16},{24,20},{28,24},{32,28},{36,32}... | collective-permute-start | bytes 1572872 | tf_op jit(solution)/shard_map/ppermute | solution.py:26
  23.9 30.9 %collective-permute-start.1 = (bf16[128,2048]{1,0:T(8,128)(2,1)}, bf16[128,2048]{1,0:T(8,128)(2,1)S(1)}, u32[]{:S(2)}, u32[]{:S(2)}) collective-permute-start(bf16[128,2048]{1,0:T(8,128)(2,1)} %get-tuple-element.29), channel_id=1, source_target_pairs={{4,0},{8,4},{12,8},{16,12},{20,16},{24,20},{28,24},{32,28},{36,32}... | collective-permute-start | bytes 1572872 | tf_op jit(solution)/shard_map/ppermute | solution.py:26
  36.2 5.8 %copy-start.6 = (bf16[128,2048]{1,0:T(8,128)(2,1)}, bf16[128,2048]{1,0:T(8,128)(2,1)S(1)}, u32[]{:S(2)}) copy-start(bf16[128,2048]{1,0:T(8,128)(2,1)S(1)} %collective-permute-done.3.q_ref) | copy-start | bytes 1572868
  42.1 1.0 copy-start.1
  46.4 19.5 %collective-permute-start.4 = (f32[1,128,32]{2,1,0:T(8,128)}, f32[1,128,32]{2,1,0:T(8,128)S(1)}, u32[]{:S(2)}, u32[]{:S(2)}) collective-permute-start(f32[1,128,32]{2,1,0:T(8,128)} %get-tuple-element.18), channel_id=1, source_target_pairs={{0,4},{4,8},{8,12},{12,16},{16,20},{20,24},{24,28},{28,32},{32,36}... | collective-permute-start | bytes 49160 | tf_op jit(solution)/shard_map/ppermute | solution.py:20
  48.3 29.9 %collective-permute-start.7 = (bf16[128,2048]{1,0:T(8,128)(2,1)}, bf16[128,2048]{1,0:T(8,128)(2,1)S(1)}, u32[]{:S(2)}, u32[]{:S(2)}) collective-permute-start(bf16[128,2048]{1,0:T(8,128)(2,1)} %get-tuple-element.22), channel_id=1, source_target_pairs={{0,4},{4,8},{8,12},{12,16},{16,20},{20,24},{24,28},{28,32},{32,36}... | collective-permute-start | bytes 1572872 | tf_op jit(solution)/shard_map/ppermute | solution.py:20
  54.8 11.2 %copy-start.7 = (bf16[128,2048]{1,0:T(8,128)(2,1)}, bf16[128,2048]{1,0:T(8,128)(2,1)S(1)}, u32[]{:S(2)}) copy-start(bf16[128,2048]{1,0:T(8,128)(2,1)S(1)} %collective-permute-done.1.q_ref) | copy-start | bytes 1572868
  64.6 1.4 %copy-start = (bf16[2,128,2048]{2,1,0:T(8,128)(2,1)}, bf16[2,128,2048]{2,1,0:T(8,128)(2,1)S(1)}, u32[]{:S(2)}) copy-start(bf16[2,128,2048]{2,1,0:T(8,128)(2,1)S(1)} %collective-permute-done.kp_ref.vp_ref.k_ref.v_ref) | copy-start | bytes 3145732
  66.0 0.6 copy-start.3
  70.0 23.6 %collective-permute-start.5 = (bf16[128,2048]{1,0:T(8,128)(2,1)}, bf16[128,2048]{1,0:T(8,128)(2,1)S(1)}, u32[]{:S(2)}, u32[]{:S(2)}) collective-permute-start(bf16[128,2048]{1,0:T(8,128)(2,1)} %get-tuple-element.19), channel_id=1, source_target_pairs={{0,4},{4,8},{8,12},{12,16},{16,20},{20,24},{24,28},{28,32},{32,36}... | collective-permute-start | bytes 1572872 | tf_op jit(solution)/shard_map/ppermute | solution.py:20
  71.9 21.7 %collective-permute-start.6 = (f32[1,128,32]{2,1,0:T(8,128)}, f32[1,128,32]{2,1,0:T(8,128)S(1)}, u32[]{:S(2)}, u32[]{:S(2)}) collective-permute-start(f32[1,128,32]{2,1,0:T(8,128)} %get-tuple-element.20), channel_id=1, source_target_pairs={{0,4},{4,8},{8,12},{12,16},{16,20},{20,24},{24,28},{28,32},{32,36}... | collective-permute-start | bytes 49160 | tf_op jit(solution)/shard_map/ppermute | solution.py:20
  78.3 0.8 copy-start.8
  93.5 0.6 copy-start.10
  93.6 0.8 copy-start.9
  94.4 3.0 %copy-start.5 = (f32[1,128,32]{2,1,0:T(8,128)S(1)}, f32[1,128,32]{2,1,0:T(8,128)}, u32[]{:S(2)}) copy-start(f32[1,128,32]{2,1,0:T(8,128)} %get-tuple-element.24.rest_0_.near_ref) | copy-start | bytes 49156
  97.3 0.8 copy-start.12
  98.2 0.9 copy-start.4
  98.3 0.9 copy-start.11

commit v12 on v11

--- a/solution.py
+++ b/solution.py
@@ -114,7 +114,8 @@
 
 
 def merge_kernel(block_ref, mixed_ref, near_ref, o_ref, far_ref, *rest):
-    out_ref = rest[-1]
+    out_ref, lse_ref = rest[-2:]
+    rows = mixed_ref.shape[0]
     has_far = block_ref[0] >= 2
     n = HEADS_PER_STEP
     near = near_ref[...]
@@ -124,15 +125,19 @@
     m = jnp.where(has_far, jnp.maximum(m_near, m_far), m_near)
     near_scale = jnp.exp(m_near - m)
     far_scale = jnp.where(has_far, jnp.exp(m_far - m), 0.0)
-    inverse = 1.0 / (near_scale * l_near + far_scale * l_far)
+    total = near_scale * l_near + far_scale * l_far
+    lse = m + jnp.log(total)
+    inverse = 1.0 / total
     near_scale = near_scale * inverse
     far_scale = far_scale * inverse
+    diagonal = lax.broadcasted_iota(jnp.int32, (rows, rows), 0) == lax.broadcasted_iota(jnp.int32, (rows, rows), 1)
     for h in range(n):
         cols = slice(h * HEAD_DIM, (h + 1) * HEAD_DIM)
         mixed = near_scale[:, h : h + 1] * mixed_ref[:, cols] + far_scale[:, h : h + 1] * o_ref[:, cols].astype(
             jnp.float32
         )
         out_ref[:, cols] = mixed.astype(out_ref.dtype)
+        lse_ref[h : h + 1, :] = jnp.sum(jnp.where(diagonal, lse[:, h : h + 1], 0.0), axis=0, keepdims=True)
 
 
 def merged_output(block_index, chunk, width, mixed_near, stat_near, o_far, stat_far, previous):
@@ -142,46 +147,34 @@
     offset = chunk * steps
     part = pl.BlockSpec((rows, step_width), lambda g, b: (0, g))
     whole = pl.BlockSpec((rows, step_width), lambda g, b: (0, g + offset))
+    lse_block = pl.BlockSpec((HEADS_PER_STEP, rows), lambda g, b: (g + offset, 0))
     operands = [block_index, mixed_near, stat_near, o_far, stat_far]
     in_specs = [part, stat_spec(rows), part, stat_spec(rows)]
     aliases = {}
     if previous is not None:
-        in_specs = in_specs + [pl.BlockSpec(memory_space=pl.ANY)]
-        aliases = {len(operands): 0}
-        operands = operands + [previous]
+        in_specs = in_specs + [pl.BlockSpec(memory_space=pl.ANY)] * 2
+        aliases = {len(operands): 0, len(operands) + 1: 1}
+        operands = operands + list(previous)
     return pl.pallas_call(
         merge_kernel,
         grid_spec=pltpu.PrefetchScalarGridSpec(
             num_scalar_prefetch=1,
             grid=(steps,),
             in_specs=in_specs,
-            out_specs=whole,
+            out_specs=[whole, lse_block],
         ),
-        out_shape=jax.ShapeDtypeStruct((rows, width), jnp.bfloat16),
+        out_shape=[
+            jax.ShapeDtypeStruct((rows, width), jnp.bfloat16),
+            jax.ShapeDtypeStruct((width // HEAD_DIM, rows), jnp.float32),
+        ],
         input_output_aliases=aliases,
     )(*operands)
-
-
-def per_head(stat):
-    steps, rows, _ = stat.shape
-    stat = jnp.transpose(stat.reshape(steps, rows, 2, HEADS_PER_STEP), (2, 1, 0, 3))
-    return stat[0].reshape(rows, steps * HEADS_PER_STEP), stat[1].reshape(rows, steps * HEADS_PER_STEP)
-
-
-def log_total(block_index, stat_near, stat_far):
-    m_near, l_near = per_head(stat_near)
-    m_far, l_far = per_head(stat_far)
-    has_far = block_index >= 2
-    m = jnp.where(has_far, jnp.maximum(m_near, m_far), m_near)
-    total = jnp.exp(m_near - m) * l_near + jnp.where(has_far, jnp.exp(m_far - m), 0.0) * l_far
-    return jnp.transpose(m + jnp.log(total))
 
 
 def shards(att_query, att_key, att_value):
     width = att_query.shape[1]
     chunk_width = width // CHUNKS
-    block_index = lax.axis_index("ctx").astype(jnp.int32)
-    index_ref = block_index.reshape(1)
+    index_ref = lax.axis_index("ctx").astype(jnp.int32).reshape(1)
     pieces = []
     for chunk in range(CHUNKS):
         cols = slice(chunk * chunk_width, (chunk + 1) * chunk_width)
@@ -194,10 +187,7 @@
     out = None
     for chunk in range(CHUNKS):
         out = merged_output(index_ref, chunk, width, *pieces[chunk], out)
-    out, stats = lax.optimization_barrier((out, [(piece[1], piece[3]) for piece in pieces]))
-    stat_near = jnp.concatenate([piece[0] for piece in stats], axis=0)
-    stat_far = jnp.concatenate([piece[1] for piece in stats], axis=0)
-    return out, log_total(block_index, stat_near, stat_far)
+    return tuple(out)
 
 
 def solution(mesh):

time: 101 us -> 98.3 us (0.973)
  local copies, waits for them, and re-layouts: 7.67 us -> 5.72 us
    unnamed x26 -> x18, local copies, waits for them, and re-layouts: 4.85 us -> 3.19 us
where the time goes in v12:
time: 98.3 us; the launch traced here: 97.5 us
  waiting for transfers between devices  36.7 us (37%)
  starting transfers between devices  31.1 us (32%)
  Pallas kernels  22.1 us (22%)
  local copies, waits for them, and re-layouts  5.72 us (6%)
  other arithmetic  1.16 us (1%)
    ppermute x6, waiting for transfers between devices, from_behind(): return lax.ppermute(block, axis, route)  28.3 us
    ppermute x2, starting transfers between devices, from_ahead(): return lax.ppermute(block, axis, route)  16.7 us
    ppermute x6, starting transfers between devices, from_behind(): return lax.ppermute(block, axis, route)  14.4 us
    pallas_call x2, Pallas kernels, near_attention(): pl.pallas_call(near_kernel, grid_spec=pltpu.PrefetchScalarGridSpec(num_sc...  9.02 us
    ppermute x2, waiting for transfers between devices, from_ahead(): return lax.ppermute(block, axis, route)  8.38 us
    pallas_call x2, Pallas kernels, partial_attention(): pl.pallas_call(partial_kernel, grid=(steps,), in_specs=[block, key_block,...  6.7 us
    pallas_call x2, Pallas kernels, merged_output(): pl.pallas_call(merge_kernel, grid_spec=pltpu.PrefetchScalarGridSpec(num_s...  6.38 us
    unnamed x18, local copies, waits for them, and re-layouts  3.19 us
  transfers between devices with their start and end apart: 8, of which 5 were waited for; matrix products, arithmetic and copies ran while one was open for 2% of the time, Pallas kernels for 19%

profile of v12, /device:TPU:56, one launch (start us, length us, event | category | flops | bytes accessed | tf_op | source)
XLA Modules:
  0.0 97.5 jit_solution(406270413123198888)
XLA Ops:
  0.6 1.7 %slice_bitcast_fusion = (bf16[1,128,2048]{2,1,0:T(8,128)(2,1)S(1)}, bf16[1,128,2048]{2,1,0:T(8,128)(2,1)S(1)}, bf16[1,128,2048]{2,1,0:T(8,128)(2,1)S(1)}, bf16[1,128,2048]{2,1,0:T(8,128)(2,1)S(1)}) fusion(bf16[128,4096]{1,0:T(8,128)(2,1)} %v_ref.3, bf16[128,4096]{1,0:T(8,128)(2,1)} %k_ref.3), kind=kLoop, calls=%fused_computation.2 | loop fusion | bytes 4194304 | tf_op jit(solution)/shard_map/stack | solution.py:181
  2.3 0.1 pad_maximum_fusion.1
  2.4 3.4 %collective-permute-start.2 = (bf16[2,128,2048]{2,1,0:T(8,128)(2,1)S(1)}, bf16[2,128,2048]{2,1,0:T(8,128)(2,1)S(1)}, u32[]{:S(2)}, u32[]{:S(2)}) collective-permute-start(bf16[2,128,2048]{2,1,0:T(8,128)(2,1)S(1)} %pad_maximum_fusion.1), channel_id=1, source_target_pairs={{0,4},{4,8},{8,12},{12,16},{16,20},{20,24},{24,28},{28,32},{32,36}... | collective-permute-start | bytes 3145736 | tf_op jit(solution)/shard_map/ppermute | solution.py:20
  5.8 0.0 copy-start.2
  5.8 1.1 %pad_maximum_fusion = bf16[2,128,2048]{2,1,0:T(8,128)(2,1)} fusion(bf16[1,128,2048]{2,1,0:T(8,128)(2,1)S(1)} %get-tuple-element.27, bf16[1,128,2048]{2,1,0:T(8,128)(2,1)S(1)} %get-tuple-element.28), kind=kLoop, calls=%fused_computation | loop fusion | flops 524288 | bytes 2097152 | tf_op jit(solution)/shard_map/stack | solution.py:181
  6.9 3.4 %collective-permute-start = (bf16[2,128,2048]{2,1,0:T(8,128)(2,1)}, bf16[2,128,2048]{2,1,0:T(8,128)(2,1)S(1)}, u32[]{:S(2)}, u32[]{:S(2)}) collective-permute-start(bf16[2,128,2048]{2,1,0:T(8,128)(2,1)} %pad_maximum_fusion), channel_id=1, source_target_pairs={{0,4},{4,8},{8,12},{12,16},{16,20},{20,24},{24,28},{28,32},{32,36}... | collective-permute-start | bytes 3145736 | tf_op jit(solution)/shard_map/ppermute | solution.py:20
  10.3 0.9 fusion
  11.2 12.7 %collective-permute-start.3 = (bf16[128,2048]{1,0:T(8,128)(2,1)S(1)}, bf16[128,2048]{1,0:T(8,128)(2,1)S(1)}, u32[]{:S(2)}, u32[]{:S(2)}) collective-permute-start(bf16[128,2048]{1,0:T(8,128)(2,1)S(1)} %get-tuple-element.22), channel_id=1, source_target_pairs={{4,0},{8,4},{12,8},{16,12},{20,16},{24,20},{28,24},{32,28},{36,32}... | collective-permute-start | bytes 1572872 | tf_op jit(solution)/shard_map/ppermute | solution.py:26
  23.9 3.9 %collective-permute-start.1 = (bf16[128,2048]{1,0:T(8,128)(2,1)}, bf16[128,2048]{1,0:T(8,128)(2,1)S(1)}, u32[]{:S(2)}, u32[]{:S(2)}) collective-permute-start(bf16[128,2048]{1,0:T(8,128)(2,1)} %get-tuple-element.23), channel_id=1, source_target_pairs={{4,0},{8,4},{12,8},{16,12},{20,16},{24,20},{28,24},{32,28},{36,32}... | collective-permute-start | bytes 1572872 | tf_op jit(solution)/shard_map/ppermute | solution.py:26
  27.8 8.4 %collective-permute-done.3.q_ref = bf16[128,2048]{1,0:T(8,128)(2,1)S(1)} collective-permute-done((bf16[128,2048]{1,0:T(8,128)(2,1)S(1)}, bf16[128,2048]{1,0:T(8,128)(2,1)S(1)}, u32[]{:S(2)}, u32[]{:S(2)}) %collective-permute-start.3) | collective-permute-done | bytes 524320 | tf_op jit(solution)/shard_map/ppermute | solution.py:26
  36.2 5.9 %collective-permute-done.2.kp_ref.vp_ref.k_ref.v_ref = bf16[2,128,2048]{2,1,0:T(8,128)(2,1)S(1)} collective-permute-done((bf16[2,128,2048]{2,1,0:T(8,128)(2,1)S(1)}, bf16[2,128,2048]{2,1,0:T(8,128)(2,1)S(1)}, u32[]{:S(2)}, u32[]{:S(2)}) %collective-permute-start.2) | collective-permute-done | bytes 1048608 | tf_op jit(solution)/shard_map/ppermute | solution.py:20
  42.1 1.0 copy-done.1
  43.0 3.3 %shard_map.52 = (bf16[128,2048]{1,0:T(8,128)(2,1)}, f32[1,128,32]{2,1,0:T(8,128)}) custom-call(bf16[128,2048]{1,0:T(8,128)(2,1)} %copy-done.3, bf16[2,128,2048]{2,1,0:T(8,128)(2,1)} %copy-done.1, bf16[2,128,2048]{2,1,0:T(8,128)(2,1)} %copy-done.1), custom_call_target="tpu_custom_call" | custom-call | tf_op jit(solution)/shard_map/pallas_call | solution.py:80
  46.4 1.9 %collective-permute-start.4 = (f32[1,128,32]{2,1,0:T(8,128)}, f32[1,128,32]{2,1,0:T(8,128)S(1)}, u32[]{:S(2)}, u32[]{:S(2)}) collective-permute-start(f32[1,128,32]{2,1,0:T(8,128)} %get-tuple-element.15), channel_id=1, source_target_pairs={{0,4},{4,8},{8,12},{12,16},{16,20},{20,24},{24,28},{28,32},{32,36}... | collective-permute-start | bytes 49160 | tf_op jit(solution)/shard_map/ppermute | solution.py:20
  48.3 1.9 %collective-permute-start.7 = (bf16[128,2048]{1,0:T(8,128)(2,1)}, bf16[128,2048]{1,0:T(8,128)(2,1)S(1)}, u32[]{:S(2)}, u32[]{:S(2)}) collective-permute-start(bf16[128,2048]{1,0:T(8,128)(2,1)} %get-tuple-element.19), channel_id=1, source_target_pairs={{0,4},{4,8},{8,12},{12,16},{16,20},{20,24},{24,28},{28,32},{32,36}... | collective-permute-start | bytes 1572872 | tf_op jit(solution)/shard_map/ppermute | solution.py:20
  50.2 4.5 %shard_map.51 = (f32[128,2048]{1,0:T(8,128)}, f32[1,128,32]{2,1,0:T(8,128)}) custom-call(s32[1]{0:T(128)} %bitcast.block_ref, bf16[128,4096]{1,0:T(8,128)(2,1)} %q_ref.3, bf16[128,4096]{1,0:T(8,128)(2,1)} %k_ref.3, bf16[128,4096]{1,0:T(8,128)(2,1)} %v_ref.3, bf16[2,128,2048]{2,1,0:T(8,128)(2,1)} %copy-done.1, bf16[2,128,2048]{2,1,0:T(8,128)(2,1)} %copy-done.1), custom_call_target="tpu_custom_call" | custom-call | tf_op jit(solution)/shard_map/pallas_call | solution.py:101
  54.8 0.0 collective-permute-done.1.q_ref
  54.8 9.8 %collective-permute-done.kp_ref.vp_ref.k_ref.v_ref = bf16[2,128,2048]{2,1,0:T(8,128)(2,1)S(1)} collective-permute-done((bf16[2,128,2048]{2,1,0:T(8,128)(2,1)}, bf16[2,128,2048]{2,1,0:T(8,128)(2,1)S(1)}, u32[]{:S(2)}, u32[]{:S(2)}) %collective-permute-start) | collective-permute-done | bytes 1048608 | tf_op jit(solution)/shard_map/ppermute | solution.py:20
  64.6 1.4 %collective-permute-done.4.rest_1_.far_ref = f32[1,128,32]{2,1,0:T(8,128)S(1)} collective-permute-done((f32[1,128,32]{2,1,0:T(8,128)}, f32[1,128,32]{2,1,0:T(8,128)S(1)}, u32[]{:S(2)}, u32[]{:S(2)}) %collective-permute-start.4) | collective-permute-done | bytes 16416 | tf_op jit(solution)/shard_map/ppermute | solution.py:20
  66.0 0.6 copy-done.7
  66.6 3.4 %shard_map.53 = (bf16[128,2048]{1,0:T(8,128)(2,1)}, f32[1,128,32]{2,1,0:T(8,128)}) custom-call(bf16[128,2048]{1,0:T(8,128)(2,1)} %copy-done.5, bf16[2,128,2048]{2,1,0:T(8,128)(2,1)} %copy-done, bf16[2,128,2048]{2,1,0:T(8,128)(2,1)} %copy-done, f32[1,128,32]{2,1,0:T(8,128)} %get-tuple-element.14.rest_0_.near_ref, f32[1,128,32]{2,1,0:T(8,128)} %copy-done.7), custom_call_target="tpu_custom_call" | custom-call | tf_op jit(solution)/shard_map/pallas_call | solution.py:80
  69.9 1.9 %collective-permute-start.5 = (bf16[128,2048]{1,0:T(8,128)(2,1)}, bf16[128,2048]{1,0:T(8,128)(2,1)S(1)}, u32[]{:S(2)}, u32[]{:S(2)}) collective-permute-start(bf16[128,2048]{1,0:T(8,128)(2,1)} %get-tuple-element.16), channel_id=1, source_target_pairs={{0,4},{4,8},{8,12},{12,16},{16,20},{20,24},{24,28},{28,32},{32,36}... | collective-permute-start | bytes 1572872 | tf_op jit(solution)/shard_map/ppermute | solution.py:20
  71.8 1.9 %collective-permute-start.6 = (f32[1,128,32]{2,1,0:T(8,128)}, f32[1,128,32]{2,1,0:T(8,128)S(1)}, u32[]{:S(2)}, u32[]{:S(2)}) collective-permute-start(f32[1,128,32]{2,1,0:T(8,128)} %get-tuple-element.17), channel_id=1, source_target_pairs={{0,4},{4,8},{8,12},{12,16},{16,20},{20,24},{24,28},{28,32},{32,36}... | collective-permute-start | bytes 49160 | tf_op jit(solution)/shard_map/ppermute | solution.py:20
  73.8 4.5 %shard_map.50 = (f32[128,2048]{1,0:T(8,128)}, f32[1,128,32]{2,1,0:T(8,128)}) custom-call(s32[1]{0:T(128)} %bitcast.block_ref, bf16[128,4096]{1,0:T(8,128)(2,1)} %q_ref.3, bf16[128,4096]{1,0:T(8,128)(2,1)} %k_ref.3, bf16[128,4096]{1,0:T(8,128)(2,1)} %v_ref.3, bf16[2,128,2048]{2,1,0:T(8,128)(2,1)} %copy-done, bf16[2,128,2048]{2,1,0:T(8,128)(2,1)} %copy-done), custom_call_target="tpu_custom_call" | custom-call | tf_op jit(solution)/shard_map/pallas_call | solution.py:101
  78.3 0.0 collective-permute-done.7.o_ref
  78.3 0.8 copy-done.4
  79.1 3.2 %shard_map.54 = (bf16[128,4096]{1,0:T(8,128)(2,1)}, f32[32,128]{1,0:T(8,128)}) custom-call(s32[1]{0:T(128)} %bitcast.block_ref, f32[128,2048]{1,0:T(8,128)} %get-tuple-element.18.mixed_ref, f32[1,128,32]{2,1,0:T(8,128)} %get-tuple-element.14.rest_0_.near_ref, bf16[128,2048]{1,0:T(8,128)(2,1)} %copy-done.4, f32[1,128,32]{2,1,0:T(8,128)} %copy-done.7), custom_call_target="tpu_custom_call" | custom-call | tf_op jit(solution)/shard_map/pallas_call | solution.py:158
  82.2 11.3 %collective-permute-done.6.far_ref = f32[1,128,32]{2,1,0:T(8,128)S(1)} collective-permute-done((f32[1,128,32]{2,1,0:T(8,128)}, f32[1,128,32]{2,1,0:T(8,128)S(1)}, u32[]{:S(2)}, u32[]{:S(2)}) %collective-permute-start.6) | collective-permute-done | bytes 16416 | tf_op jit(solution)/shard_map/ppermute | solution.py:20
  93.5 0.0 collective-permute-done.5.o_ref
  93.5 0.6 copy-done.8
  94.1 0.2 copy-done.6
  94.3 3.2 %shard_map.55 = (bf16[128,4096]{1,0:T(8,128)(2,1)}, f32[32,128]{1,0:T(8,128)}) custom-call(s32[1]{0:T(128)} %bitcast.block_ref, f32[128,2048]{1,0:T(8,128)} %get-tuple-element.12.mixed_ref, f32[1,128,32]{2,1,0:T(8,128)} %get-tuple-element.13.near_ref, bf16[128,2048]{1,0:T(8,128)(2,1)} %copy-done.6, ...), custom_call_target="tpu_custom_call", output_to_operand_aliasing={{0}: (5, {}), {1}: (6, {})} | custom-call | tf_op jit(solution)/shard_map/pallas_call | solution.py:158
  (12 shorter events, 0.0 us)
Async XLA Ops:
  2.4 39.7 %collective-permute-start.2 = (bf16[2,128,2048]{2,1,0:T(8,128)(2,1)S(1)}, bf16[2,128,2048]{2,1,0:T(8,128)(2,1)S(1)}, u32[]{:S(2)}, u32[]{:S(2)}) collective-permute-start(bf16[2,128,2048]{2,1,0:T(8,128)(2,1)S(1)} %pad_maximum_fusion.1), channel_id=1, source_target_pairs={{0,4},{4,8},{8,12},{12,16},{16,20},{20,24},{24,28},{28,32},{32,36}... | collective-permute-start | bytes 3145736 | tf_op jit(solution)/shard_map/ppermute | solution.py:20
  5.8 4.5 %copy-start.2 = (bf16[128,4096]{1,0:T(8,128)(2,1)S(1)}, bf16[128,4096]{1,0:T(8,128)(2,1)}, u32[]{:S(2)}) copy-start(bf16[128,4096]{1,0:T(8,128)(2,1)} %q_ref.3) | copy-start | bytes 3145732
  6.9 57.7 %collective-permute-start = (bf16[2,128,2048]{2,1,0:T(8,128)(2,1)}, bf16[2,128,2048]{2,1,0:T(8,128)(2,1)S(1)}, u32[]{:S(2)}, u32[]{:S(2)}) collective-permute-start(bf16[2,128,2048]{2,1,0:T(8,128)(2,1)} %pad_maximum_fusion), channel_id=1, source_target_pairs={{0,4},{4,8},{8,12},{12,16},{16,20},{20,24},{24,28},{28,32},{32,36}... | collective-permute-start | bytes 3145736 | tf_op jit(solution)/shard_map/ppermute | solution.py:20
  11.2 25.0 %collective-permute-start.3 = (bf16[128,2048]{1,0:T(8,128)(2,1)S(1)}, bf16[128,2048]{1,0:T(8,128)(2,1)S(1)}, u32[]{:S(2)}, u32[]{:S(2)}) collective-permute-start(bf16[128,2048]{1,0:T(8,128)(2,1)S(1)} %get-tuple-element.22), channel_id=1, source_target_pairs={{4,0},{8,4},{12,8},{16,12},{20,16},{24,20},{28,24},{32,28},{36,32}... | collective-permute-start | bytes 1572872 | tf_op jit(solution)/shard_map/ppermute | solution.py:26
  23.9 30.9 %collective-permute-start.1 = (bf16[128,2048]{1,0:T(8,128)(2,1)}, bf16[128,2048]{1,0:T(8,128)(2,1)S(1)}, u32[]{:S(2)}, u32[]{:S(2)}) collective-permute-start(bf16[128,2048]{1,0:T(8,128)(2,1)} %get-tuple-element.23), channel_id=1, source_target_pairs={{4,0},{8,4},{12,8},{16,12},{20,16},{24,20},{28,24},{32,28},{36,32}... | collective-permute-start | bytes 1572872 | tf_op jit(solution)/shard_map/ppermute | solution.py:26
  36.2 5.9 %copy-start.3 = (bf16[128,2048]{1,0:T(8,128)(2,1)}, bf16[128,2048]{1,0:T(8,128)(2,1)S(1)}, u32[]{:S(2)}) copy-start(bf16[128,2048]{1,0:T(8,128)(2,1)S(1)} %collective-permute-done.3.q_ref) | copy-start | bytes 1572868
  42.1 1.0 copy-start.1
  46.4 19.6 %collective-permute-start.4 = (f32[1,128,32]{2,1,0:T(8,128)}, f32[1,128,32]{2,1,0:T(8,128)S(1)}, u32[]{:S(2)}, u32[]{:S(2)}) collective-permute-start(f32[1,128,32]{2,1,0:T(8,128)} %get-tuple-element.15), channel_id=1, source_target_pairs={{0,4},{4,8},{8,12},{12,16},{16,20},{20,24},{24,28},{28,32},{32,36}... | collective-permute-start | bytes 49160 | tf_op jit(solution)/shard_map/ppermute | solution.py:20
  48.3 30.0 %collective-permute-start.7 = (bf16[128,2048]{1,0:T(8,128)(2,1)}, bf16[128,2048]{1,0:T(8,128)(2,1)S(1)}, u32[]{:S(2)}, u32[]{:S(2)}) collective-permute-start(bf16[128,2048]{1,0:T(8,128)(2,1)} %get-tuple-element.19), channel_id=1, source_target_pairs={{0,4},{4,8},{8,12},{12,16},{16,20},{20,24},{24,28},{28,32},{32,36}... | collective-permute-start | bytes 1572872 | tf_op jit(solution)/shard_map/ppermute | solution.py:20
  54.8 11.2 %copy-start.5 = (bf16[128,2048]{1,0:T(8,128)(2,1)}, bf16[128,2048]{1,0:T(8,128)(2,1)S(1)}, u32[]{:S(2)}) copy-start(bf16[128,2048]{1,0:T(8,128)(2,1)S(1)} %collective-permute-done.1.q_ref) | copy-start | bytes 1572868
  64.6 1.4 %copy-start = (bf16[2,128,2048]{2,1,0:T(8,128)(2,1)}, bf16[2,128,2048]{2,1,0:T(8,128)(2,1)S(1)}, u32[]{:S(2)}) copy-start(bf16[2,128,2048]{2,1,0:T(8,128)(2,1)S(1)} %collective-permute-done.kp_ref.vp_ref.k_ref.v_ref) | copy-start | bytes 3145732
  66.0 0.6 copy-start.7
  69.9 23.6 %collective-permute-start.5 = (bf16[128,2048]{1,0:T(8,128)(2,1)}, bf16[128,2048]{1,0:T(8,128)(2,1)S(1)}, u32[]{:S(2)}, u32[]{:S(2)}) collective-permute-start(bf16[128,2048]{1,0:T(8,128)(2,1)} %get-tuple-element.16), channel_id=1, source_target_pairs={{0,4},{4,8},{8,12},{12,16},{16,20},{20,24},{24,28},{28,32},{32,36}... | collective-permute-start | bytes 1572872 | tf_op jit(solution)/shard_map/ppermute | solution.py:20
  71.8 21.7 %collective-permute-start.6 = (f32[1,128,32]{2,1,0:T(8,128)}, f32[1,128,32]{2,1,0:T(8,128)S(1)}, u32[]{:S(2)}, u32[]{:S(2)}) collective-permute-start(f32[1,128,32]{2,1,0:T(8,128)} %get-tuple-element.17), channel_id=1, source_target_pairs={{0,4},{4,8},{8,12},{12,16},{16,20},{20,24},{24,28},{28,32},{32,36}... | collective-permute-start | bytes 49160 | tf_op jit(solution)/shard_map/ppermute | solution.py:20
  78.3 0.8 copy-start.4
  93.5 0.6 copy-start.8
  93.5 0.8 copy-start.6

commit v13 on v12

--- a/solution.py
+++ b/solution.py
@@ -171,6 +171,26 @@
     )(*operands)
 
 
+def stacked_chunk(k, v, start, size):
+    def kernel(k_hbm, v_hbm, o_hbm, sem):
+        copies = [
+            pltpu.make_async_copy(k_hbm.at[:, pl.ds(start, size)], o_hbm.at[0], sem.at[0]),
+            pltpu.make_async_copy(v_hbm.at[:, pl.ds(start, size)], o_hbm.at[1], sem.at[1]),
+        ]
+        for copy in copies:
+            copy.start()
+        for copy in copies:
+            copy.wait()
+
+    return pl.pallas_call(
+        kernel,
+        in_specs=[pl.BlockSpec(memory_space=pl.ANY)] * 2,
+        out_specs=pl.BlockSpec(memory_space=pl.ANY),
+        out_shape=jax.ShapeDtypeStruct((2, k.shape[0], size), k.dtype),
+        scratch_shapes=[pltpu.SemaphoreType.DMA((2,))],
+    )(k, v)
+
+
 def shards(att_query, att_key, att_value):
     width = att_query.shape[1]
     chunk_width = width // CHUNKS
@@ -178,7 +198,7 @@
     pieces = []
     for chunk in range(CHUNKS):
         cols = slice(chunk * chunk_width, (chunk + 1) * chunk_width)
-        kv_prev = from_behind(jnp.stack([att_key[:, cols], att_value[:, cols]]), "ctx")
+        kv_prev = from_behind(stacked_chunk(att_key, att_value, chunk * chunk_width, chunk_width), "ctx")
         q_next = from_ahead(att_query[:, cols], "ctx")
         after = (pieces[-1][1], pieces[-1][3]) if pieces else ()
         o_far, stat_far = from_behind(partial_attention(q_next, kv_prev, after), "ctx")

time: 98.3 us -> 151 us (1.54)
  Pallas kernels: 22.1 us -> 87.9 us
  waiting for transfers between devices: 36.7 us -> 24.3 us
    pallas_call x0 -> x2, Pallas kernels: none -> 65.8 us  [stacked_chunk(): pl.pallas_call(kernel, in_specs=[pl.BlockSpec(memory_space=pl.ANY)] * 2,...]
    ppermute x6, waiting for transfers between devices: 28.3 us -> 16 us  [from_behind(): return lax.ppermute(block, axis, route)]
    another operation x1 -> x0, local copies, waits for them, and re-layouts: 1.66 us -> none  [shards(): jnp.stack([att_key[:, cols], att_value[:, cols]])]
  transfers between devices with their start and end apart: 8 -> 8, of which waited for: 5 -> 3; matrix products, arithmetic and copies ran while one was open for 2% -> 1% of each run, Pallas kernels for 19% -> 35%
where the time goes in v13:
time: 151 us; the launch traced here: 149 us
  Pallas kernels  87.9 us (58%)
  starting transfers between devices  31.2 us (21%)
  waiting for transfers between devices  24.3 us (16%)
  local copies, waits for them, and re-layouts  4.91 us (3%)
    pallas_call x2, Pallas kernels, stacked_chunk(): pl.pallas_call(kernel, in_specs=[pl.BlockSpec(memory_space=pl.ANY)] * 2,...  65.8 us
    ppermute x2, starting transfers between devices, from_ahead(): return lax.ppermute(block, axis, route)  16.7 us
    ppermute x6, waiting for transfers between devices, from_behind(): return lax.ppermute(block, axis, route)  16 us
    ppermute x6, starting transfers between devices, from_behind(): return lax.ppermute(block, axis, route)  14.6 us
    pallas_call x2, Pallas kernels, near_attention(): pl.pallas_call(near_kernel, grid_spec=pltpu.PrefetchScalarGridSpec(num_sc...  9.05 us
    ppermute x2, waiting for transfers between devices, from_ahead(): return lax.ppermute(block, axis, route)  8.38 us
    pallas_call x2, Pallas kernels, partial_attention(): pl.pallas_call(partial_kernel, grid=(steps,), in_specs=[block, key_block,...  6.71 us
    pallas_call x2, Pallas kernels, merged_output(): pl.pallas_call(merge_kernel, grid_spec=pltpu.PrefetchScalarGridSpec(num_s...  6.38 us
  transfers between devices with their start and end apart: 8, of which 3 were waited for; matrix products, arithmetic and copies ran while one was open for 1% of the time, Pallas kernels for 35%

profile of v13, /device:TPU:56, one launch (start us, length us, event | category | flops | bytes accessed | tf_op | source)
XLA Modules:
  0.0 149.2 jit_solution(4758757887968501765)
XLA Ops:
  0.6 32.9 %shard_map.52 = bf16[2,128,2048]{2,1,0:T(8,128)(2,1)} custom-call(bf16[128,4096]{1,0:T(8,128)(2,1)} %k_ref.3, bf16[128,4096]{1,0:T(8,128)(2,1)} %v_ref.3), custom_call_target="tpu_custom_call" | custom-call | tf_op jit(solution)/shard_map/pallas_call | solution.py:185
  33.5 0.0 copy-start.2
  33.5 3.5 %collective-permute-start.2 = (bf16[2,128,2048]{2,1,0:T(8,128)(2,1)}, bf16[2,128,2048]{2,1,0:T(8,128)(2,1)S(1)}, u32[]{:S(2)}, u32[]{:S(2)}) collective-permute-start(bf16[2,128,2048]{2,1,0:T(8,128)(2,1)} %shard_map.52), channel_id=1, source_target_pairs={{0,4},{4,8},{8,12},{12,16},{16,20},{20,24},{24,28},{28,32},{32,36}... | collective-permute-start | bytes 3145736 | tf_op jit(solution)/shard_map/ppermute | solution.py:20
  37.1 32.9 %shard_map.50 = bf16[2,128,2048]{2,1,0:T(8,128)(2,1)} custom-call(bf16[128,4096]{1,0:T(8,128)(2,1)} %k_ref.3, bf16[128,4096]{1,0:T(8,128)(2,1)} %v_ref.3), custom_call_target="tpu_custom_call" | custom-call | tf_op jit(solution)/shard_map/pallas_call | solution.py:185
  70.0 3.4 %collective-permute-start = (bf16[2,128,2048]{2,1,0:T(8,128)(2,1)}, bf16[2,128,2048]{2,1,0:T(8,128)(2,1)S(1)}, u32[]{:S(2)}, u32[]{:S(2)}) collective-permute-start(bf16[2,128,2048]{2,1,0:T(8,128)(2,1)} %shard_map.50), channel_id=1, source_target_pairs={{0,4},{4,8},{8,12},{12,16},{16,20},{20,24},{24,28},{28,32},{32,36}... | collective-permute-start | bytes 3145736 | tf_op jit(solution)/shard_map/ppermute | solution.py:20
  73.4 0.9 fusion
  74.3 12.7 %collective-permute-start.3 = (bf16[128,2048]{1,0:T(8,128)(2,1)S(1)}, bf16[128,2048]{1,0:T(8,128)(2,1)S(1)}, u32[]{:S(2)}, u32[]{:S(2)}) collective-permute-start(bf16[128,2048]{1,0:T(8,128)(2,1)S(1)} %get-tuple-element.22), channel_id=1, source_target_pairs={{4,0},{8,4},{12,8},{16,12},{20,16},{24,20},{28,24},{32,28},{36,32}... | collective-permute-start | bytes 1572872 | tf_op jit(solution)/shard_map/ppermute | solution.py:26
  87.0 3.9 %collective-permute-start.1 = (bf16[128,2048]{1,0:T(8,128)(2,1)}, bf16[128,2048]{1,0:T(8,128)(2,1)S(1)}, u32[]{:S(2)}, u32[]{:S(2)}) collective-permute-start(bf16[128,2048]{1,0:T(8,128)(2,1)} %get-tuple-element.23), channel_id=1, source_target_pairs={{4,0},{8,4},{12,8},{16,12},{20,16},{24,20},{28,24},{32,28},{36,32}... | collective-permute-start | bytes 1572872 | tf_op jit(solution)/shard_map/ppermute | solution.py:26
  90.9 8.4 %collective-permute-done.3.q_ref = bf16[128,2048]{1,0:T(8,128)(2,1)S(1)} collective-permute-done((bf16[128,2048]{1,0:T(8,128)(2,1)S(1)}, bf16[128,2048]{1,0:T(8,128)(2,1)S(1)}, u32[]{:S(2)}, u32[]{:S(2)}) %collective-permute-start.3) | collective-permute-done | bytes 524320 | tf_op jit(solution)/shard_map/ppermute | solution.py:26
  99.3 0.0 collective-permute-done.2.kp_ref.vp_ref.k_ref.v_ref
  99.3 0.8 copy-done.3
  100.1 1.0 copy-done.1
  101.1 3.4 %shard_map.54 = (bf16[128,2048]{1,0:T(8,128)(2,1)}, f32[1,128,32]{2,1,0:T(8,128)}) custom-call(bf16[128,2048]{1,0:T(8,128)(2,1)} %copy-done.3, bf16[2,128,2048]{2,1,0:T(8,128)(2,1)} %copy-done.1, bf16[2,128,2048]{2,1,0:T(8,128)(2,1)} %copy-done.1), custom_call_target="tpu_custom_call" | custom-call | tf_op jit(solution)/shard_map/pallas_call | solution.py:80
  104.5 1.9 %collective-permute-start.4 = (f32[1,128,32]{2,1,0:T(8,128)}, f32[1,128,32]{2,1,0:T(8,128)S(1)}, u32[]{:S(2)}, u32[]{:S(2)}) collective-permute-start(f32[1,128,32]{2,1,0:T(8,128)} %get-tuple-element.15), channel_id=1, source_target_pairs={{0,4},{4,8},{8,12},{12,16},{16,20},{20,24},{24,28},{28,32},{32,36}... | collective-permute-start | bytes 49160 | tf_op jit(solution)/shard_map/ppermute | solution.py:20
  106.4 1.9 %collective-permute-start.7 = (bf16[128,2048]{1,0:T(8,128)(2,1)}, bf16[128,2048]{1,0:T(8,128)(2,1)S(1)}, u32[]{:S(2)}, u32[]{:S(2)}) collective-permute-start(bf16[128,2048]{1,0:T(8,128)(2,1)} %get-tuple-element.19), channel_id=1, source_target_pairs={{0,4},{4,8},{8,12},{12,16},{16,20},{20,24},{24,28},{28,32},{32,36}... | collective-permute-start | bytes 1572872 | tf_op jit(solution)/shard_map/ppermute | solution.py:20
  108.3 4.5 %shard_map.53 = (f32[128,2048]{1,0:T(8,128)}, f32[1,128,32]{2,1,0:T(8,128)}) custom-call(s32[1]{0:T(128)} %bitcast.block_ref, bf16[128,4096]{1,0:T(8,128)(2,1)} %q_ref.3, bf16[128,4096]{1,0:T(8,128)(2,1)} %k_ref.3, bf16[128,4096]{1,0:T(8,128)(2,1)} %v_ref.3, bf16[2,128,2048]{2,1,0:T(8,128)(2,1)} %copy-done.1, bf16[2,128,2048]{2,1,0:T(8,128)(2,1)} %copy-done.1), custom_call_target="tpu_custom_call" | custom-call | tf_op jit(solution)/shard_map/pallas_call | solution.py:101
  112.9 0.0 collective-permute-done.1.q_ref
  112.9 0.0 collective-permute-done.kp_ref.vp_ref.k_ref.v_ref
  112.9 0.0 copy-start
  112.9 6.9 %collective-permute-done.4.rest_1_.far_ref = f32[1,128,32]{2,1,0:T(8,128)S(1)} collective-permute-done((f32[1,128,32]{2,1,0:T(8,128)}, f32[1,128,32]{2,1,0:T(8,128)S(1)}, u32[]{:S(2)}, u32[]{:S(2)}) %collective-permute-start.4) | collective-permute-done | bytes 16416 | tf_op jit(solution)/shard_map/ppermute | solution.py:20
  119.8 0.6 copy-done.7
  120.4 3.3 %shard_map.55 = (bf16[128,2048]{1,0:T(8,128)(2,1)}, f32[1,128,32]{2,1,0:T(8,128)}) custom-call(bf16[128,2048]{1,0:T(8,128)(2,1)} %copy-done.5, bf16[2,128,2048]{2,1,0:T(8,128)(2,1)} %copy-done, bf16[2,128,2048]{2,1,0:T(8,128)(2,1)} %copy-done, f32[1,128,32]{2,1,0:T(8,128)} %get-tuple-element.14.rest_0_.near_ref, f32[1,128,32]{2,1,0:T(8,128)} %copy-done.7), custom_call_target="tpu_custom_call" | custom-call | tf_op jit(solution)/shard_map/pallas_call | solution.py:80
  123.8 1.9 %collective-permute-start.5 = (bf16[128,2048]{1,0:T(8,128)(2,1)}, bf16[128,2048]{1,0:T(8,128)(2,1)S(1)}, u32[]{:S(2)}, u32[]{:S(2)}) collective-permute-start(bf16[128,2048]{1,0:T(8,128)(2,1)} %get-tuple-element.16), channel_id=1, source_target_pairs={{0,4},{4,8},{8,12},{12,16},{16,20},{20,24},{24,28},{28,32},{32,36}... | collective-permute-start | bytes 1572872 | tf_op jit(solution)/shard_map/ppermute | solution.py:20
  125.7 1.9 %collective-permute-start.6 = (f32[1,128,32]{2,1,0:T(8,128)}, f32[1,128,32]{2,1,0:T(8,128)S(1)}, u32[]{:S(2)}, u32[]{:S(2)}) collective-permute-start(f32[1,128,32]{2,1,0:T(8,128)} %get-tuple-element.17), channel_id=1, source_target_pairs={{0,4},{4,8},{8,12},{12,16},{16,20},{20,24},{24,28},{28,32},{32,36}... | collective-permute-start | bytes 49160 | tf_op jit(solution)/shard_map/ppermute | solution.py:20
  127.6 4.5 %shard_map.51 = (f32[128,2048]{1,0:T(8,128)}, f32[1,128,32]{2,1,0:T(8,128)}) custom-call(s32[1]{0:T(128)} %bitcast.block_ref, bf16[128,4096]{1,0:T(8,128)(2,1)} %q_ref.3, bf16[128,4096]{1,0:T(8,128)(2,1)} %k_ref.3, bf16[128,4096]{1,0:T(8,128)(2,1)} %v_ref.3, bf16[2,128,2048]{2,1,0:T(8,128)(2,1)} %copy-done, bf16[2,128,2048]{2,1,0:T(8,128)(2,1)} %copy-done), custom_call_target="tpu_custom_call" | custom-call | tf_op jit(solution)/shard_map/pallas_call | solution.py:101
  132.1 0.8 copy-done.4
  132.9 3.2 %shard_map.56 = (bf16[128,4096]{1,0:T(8,128)(2,1)}, f32[32,128]{1,0:T(8,128)}) custom-call(s32[1]{0:T(128)} %bitcast.block_ref, f32[128,2048]{1,0:T(8,128)} %get-tuple-element.18.mixed_ref, f32[1,128,32]{2,1,0:T(8,128)} %get-tuple-element.14.rest_0_.near_ref, bf16[128,2048]{1,0:T(8,128)(2,1)} %copy-done.4, f32[1,128,32]{2,1,0:T(8,128)} %copy-done.7), custom_call_target="tpu_custom_call" | custom-call | tf_op jit(solution)/shard_map/pallas_call | solution.py:158
  136.1 9.0 %collective-permute-done.6.far_ref = f32[1,128,32]{2,1,0:T(8,128)S(1)} collective-permute-done((f32[1,128,32]{2,1,0:T(8,128)}, f32[1,128,32]{2,1,0:T(8,128)S(1)}, u32[]{:S(2)}, u32[]{:S(2)}) %collective-permute-start.6) | collective-permute-done | bytes 16416 | tf_op jit(solution)/shard_map/ppermute | solution.py:20
  145.2 0.0 collective-permute-done.5.o_ref
  145.2 0.6 copy-done.8
  145.8 0.2 copy-done.6
  146.0 3.2 %shard_map.57 = (bf16[128,4096]{1,0:T(8,128)(2,1)}, f32[32,128]{1,0:T(8,128)}) custom-call(s32[1]{0:T(128)} %bitcast.block_ref, f32[128,2048]{1,0:T(8,128)} %get-tuple-element.12.mixed_ref, f32[1,128,32]{2,1,0:T(8,128)} %get-tuple-element.13.near_ref, bf16[128,2048]{1,0:T(8,128)(2,1)} %copy-done.6, ...), custom_call_target="tpu_custom_call", output_to_operand_aliasing={{0}: (5, {}), {1}: (6, {})} | custom-call | tf_op jit(solution)/shard_map/pallas_call | solution.py:158
  (11 shorter events, 0.0 us)
Async XLA Ops:
  33.5 39.9 %copy-start.2 = (bf16[128,4096]{1,0:T(8,128)(2,1)S(1)}, bf16[128,4096]{1,0:T(8,128)(2,1)}, u32[]{:S(2)}) copy-start(bf16[128,4096]{1,0:T(8,128)(2,1)} %q_ref.3) | copy-start | bytes 3145732
  33.5 65.8 %collective-permute-start.2 = (bf16[2,128,2048]{2,1,0:T(8,128)(2,1)}, bf16[2,128,2048]{2,1,0:T(8,128)(2,1)S(1)}, u32[]{:S(2)}, u32[]{:S(2)}) collective-permute-start(bf16[2,128,2048]{2,1,0:T(8,128)(2,1)} %shard_map.52), channel_id=1, source_target_pairs={{0,4},{4,8},{8,12},{12,16},{16,20},{20,24},{24,28},{28,32},{32,36}... | collective-permute-start | bytes 3145736 | tf_op jit(solution)/shard_map/ppermute | solution.py:20
  70.0 42.9 %collective-permute-start = (bf16[2,128,2048]{2,1,0:T(8,128)(2,1)}, bf16[2,128,2048]{2,1,0:T(8,128)(2,1)S(1)}, u32[]{:S(2)}, u32[]{:S(2)}) collective-permute-start(bf16[2,128,2048]{2,1,0:T(8,128)(2,1)} %shard_map.50), channel_id=1, source_target_pairs={{0,4},{4,8},{8,12},{12,16},{16,20},{20,24},{24,28},{28,32},{32,36}... | collective-permute-start | bytes 3145736 | tf_op jit(solution)/shard_map/ppermute | solution.py:20
  74.3 25.0 %collective-permute-start.3 = (bf16[128,2048]{1,0:T(8,128)(2,1)S(1)}, bf16[128,2048]{1,0:T(8,128)(2,1)S(1)}, u32[]{:S(2)}, u32[]{:S(2)}) collective-permute-start(bf16[128,2048]{1,0:T(8,128)(2,1)S(1)} %get-tuple-element.22), channel_id=1, source_target_pairs={{4,0},{8,4},{12,8},{16,12},{20,16},{24,20},{28,24},{32,28},{36,32}... | collective-permute-start | bytes 1572872 | tf_op jit(solution)/shard_map/ppermute | solution.py:26
  87.0 25.9 %collective-permute-start.1 = (bf16[128,2048]{1,0:T(8,128)(2,1)}, bf16[128,2048]{1,0:T(8,128)(2,1)S(1)}, u32[]{:S(2)}, u32[]{:S(2)}) collective-permute-start(bf16[128,2048]{1,0:T(8,128)(2,1)} %get-tuple-element.23), channel_id=1, source_target_pairs={{4,0},{8,4},{12,8},{16,12},{20,16},{24,20},{28,24},{32,28},{36,32}... | collective-permute-start | bytes 1572872 | tf_op jit(solution)/shard_map/ppermute | solution.py:26
  99.3 0.8 copy-start.3
  100.1 1.0 copy-start.1
  104.5 15.3 %collective-permute-start.4 = (f32[1,128,32]{2,1,0:T(8,128)}, f32[1,128,32]{2,1,0:T(8,128)S(1)}, u32[]{:S(2)}, u32[]{:S(2)}) collective-permute-start(f32[1,128,32]{2,1,0:T(8,128)} %get-tuple-element.15), channel_id=1, source_target_pairs={{0,4},{4,8},{8,12},{12,16},{16,20},{20,24},{24,28},{28,32},{32,36}... | collective-permute-start | bytes 49160 | tf_op jit(solution)/shard_map/ppermute | solution.py:20
  106.4 25.7 %collective-permute-start.7 = (bf16[128,2048]{1,0:T(8,128)(2,1)}, bf16[128,2048]{1,0:T(8,128)(2,1)S(1)}, u32[]{:S(2)}, u32[]{:S(2)}) collective-permute-start(bf16[128,2048]{1,0:T(8,128)(2,1)} %get-tuple-element.19), channel_id=1, source_target_pairs={{0,4},{4,8},{8,12},{12,16},{16,20},{20,24},{24,28},{28,32},{32,36}... | collective-permute-start | bytes 1572872 | tf_op jit(solution)/shard_map/ppermute | solution.py:20
  112.9 6.9 %copy-start.5 = (bf16[128,2048]{1,0:T(8,128)(2,1)}, bf16[128,2048]{1,0:T(8,128)(2,1)S(1)}, u32[]{:S(2)}) copy-start(bf16[128,2048]{1,0:T(8,128)(2,1)S(1)} %collective-permute-done.1.q_ref) | copy-start | bytes 1572868
  112.9 6.9 %copy-start = (bf16[2,128,2048]{2,1,0:T(8,128)(2,1)}, bf16[2,128,2048]{2,1,0:T(8,128)(2,1)S(1)}, u32[]{:S(2)}) copy-start(bf16[2,128,2048]{2,1,0:T(8,128)(2,1)S(1)} %collective-permute-done.kp_ref.vp_ref.k_ref.v_ref) | copy-start | bytes 3145732
  119.8 0.6 copy-start.7
  123.8 21.4 %collective-permute-start.5 = (bf16[128,2048]{1,0:T(8,128)(2,1)}, bf16[128,2048]{1,0:T(8,128)(2,1)S(1)}, u32[]{:S(2)}, u32[]{:S(2)}) collective-permute-start(bf16[128,2048]{1,0:T(8,128)(2,1)} %get-tuple-element.16), channel_id=1, source_target_pairs={{0,4},{4,8},{8,12},{12,16},{16,20},{20,24},{24,28},{28,32},{32,36}... | collective-permute-start | bytes 1572872 | tf_op jit(solution)/shard_map/ppermute | solution.py:20
  125.7 19.5 %collective-permute-start.6 = (f32[1,128,32]{2,1,0:T(8,128)}, f32[1,128,32]{2,1,0:T(8,128)S(1)}, u32[]{:S(2)}, u32[]{:S(2)}) collective-permute-start(f32[1,128,32]{2,1,0:T(8,128)} %get-tuple-element.17), channel_id=1, source_target_pairs={{0,4},{4,8},{8,12},{12,16},{16,20},{20,24},{24,28},{28,32},{32,36}... | collective-permute-start | bytes 49160 | tf_op jit(solution)/shard_map/ppermute | solution.py:20
  132.1 0.8 copy-start.4
  145.2 0.6 copy-start.8
  145.2 0.8 copy-start.6

commit v14 on v12

--- a/solution.py
+++ b/solution.py
@@ -171,6 +171,22 @@
     )(*operands)
 
 
+def stacked_chunk(k, v, chunk, size):
+    def kernel(k_ref, v_ref, o_ref):
+        o_ref[0] = k_ref[...]
+        o_ref[1] = v_ref[...]
+
+    rows = k.shape[0]
+    block = pl.BlockSpec((rows, size), lambda i: (0, chunk))
+    return pl.pallas_call(
+        kernel,
+        grid=(1,),
+        in_specs=[block, block],
+        out_specs=pl.BlockSpec((2, rows, size), lambda i: (0, 0, 0)),
+        out_shape=jax.ShapeDtypeStruct((2, rows, size), k.dtype),
+    )(k, v)
+
+
 def shards(att_query, att_key, att_value):
     width = att_query.shape[1]
     chunk_width = width // CHUNKS
@@ -178,7 +194,7 @@
     pieces = []
     for chunk in range(CHUNKS):
         cols = slice(chunk * chunk_width, (chunk + 1) * chunk_width)
-        kv_prev = from_behind(jnp.stack([att_key[:, cols], att_value[:, cols]]), "ctx")
+        kv_prev = from_behind(stacked_chunk(att_key, att_value, chunk, chunk_width), "ctx")
         q_next = from_ahead(att_query[:, cols], "ctx")
         after = (pieces[-1][1], pieces[-1][3]) if pieces else ()
         o_far, stat_far = from_behind(partial_attention(q_next, kv_prev, after), "ctx")

time: 98.3 us -> 99.2 us (level)
  Pallas kernels: 22.1 us -> 26.7 us
  local copies, waits for them, and re-layouts: 5.72 us -> 4.12 us
  other arithmetic: 1.16 us -> 0 us
  waiting for transfers between devices: 36.7 us -> 35.6 us
    pallas_call x0 -> x2, Pallas kernels: none -> 4.5 us  [stacked_chunk(): pl.pallas_call(kernel, grid=(1,), in_specs=[block, block], out_specs=pl.B...]
    another operation x1 -> x0, local copies, waits for them, and re-layouts: 1.66 us -> none  [shards(): jnp.stack([att_key[:, cols], att_value[:, cols]])]
    another operation x2 -> x0, other arithmetic: 1.16 us -> none  [shards(): jnp.stack([att_key[:, cols], att_value[:, cols]])]
    ppermute x6, waiting for transfers between devices: 28.3 us -> 27.3 us  [from_behind(): return lax.ppermute(block, axis, route)]
  transfers between devices with their start and end apart: 8 -> 8, of which waited for: 5 -> 5; matrix products, arithmetic and copies ran while one was open for 2% -> 1% of each run, Pallas kernels for 19% -> 22%
where the time goes in v14:
time: 99.2 us; the launch traced here: 98.4 us
  waiting for transfers between devices  35.6 us (36%)
  starting transfers between devices  31.2 us (31%)
  Pallas kernels  26.7 us (27%)
  local copies, waits for them, and re-layouts  4.12 us (4%)
    ppermute x6, waiting for transfers between devices, from_behind(): return lax.ppermute(block, axis, route)  27.3 us
    ppermute x2, starting transfers between devices, from_ahead(): return lax.ppermute(block, axis, route)  16.7 us
    ppermute x6, starting transfers between devices, from_behind(): return lax.ppermute(block, axis, route)  14.6 us
    pallas_call x2, Pallas kernels, near_attention(): pl.pallas_call(near_kernel, grid_spec=pltpu.PrefetchScalarGridSpec(num_sc...  9.05 us
    ppermute x2, waiting for transfers between devices, from_ahead(): return lax.ppermute(block, axis, route)  8.38 us
    pallas_call x2, Pallas kernels, partial_attention(): pl.pallas_call(partial_kernel, grid=(steps,), in_specs=[block, key_block,...  6.71 us
    pallas_call x2, Pallas kernels, merged_output(): pl.pallas_call(merge_kernel, grid_spec=pltpu.PrefetchScalarGridSpec(num_s...  6.38 us
    pallas_call x2, Pallas kernels, stacked_chunk(): pl.pallas_call(kernel, grid=(1,), in_specs=[block, block], out_specs=pl.B...  4.5 us
  transfers between devices with their start and end apart: 8, of which 5 were waited for; matrix products, arithmetic and copies ran while one was open for 1% of the time, Pallas kernels for 22%

profile of v14, /device:TPU:56, one launch (start us, length us, event | category | flops | bytes accessed | tf_op | source)
XLA Modules:
  0.0 98.4 jit_solution(9618832220163626042)
XLA Ops:
  0.6 2.3 %shard_map.52 = bf16[2,128,2048]{2,1,0:T(8,128)(2,1)} custom-call(bf16[128,4096]{1,0:T(8,128)(2,1)} %k_ref.7, bf16[128,4096]{1,0:T(8,128)(2,1)} %v_ref.7), custom_call_target="tpu_custom_call" | custom-call | tf_op jit(solution)/shard_map/pallas_call | solution.py:181
  2.9 3.5 %collective-permute-start.2 = (bf16[2,128,2048]{2,1,0:T(8,128)(2,1)}, bf16[2,128,2048]{2,1,0:T(8,128)(2,1)S(1)}, u32[]{:S(2)}, u32[]{:S(2)}) collective-permute-start(bf16[2,128,2048]{2,1,0:T(8,128)(2,1)} %shard_map.52), channel_id=1, source_target_pairs={{0,4},{4,8},{8,12},{12,16},{16,20},{20,24},{24,28},{28,32},{32,36}... | collective-permute-start | bytes 3145736 | tf_op jit(solution)/shard_map/ppermute | solution.py:20
  6.4 2.2 %shard_map.50 = bf16[2,128,2048]{2,1,0:T(8,128)(2,1)} custom-call(bf16[128,4096]{1,0:T(8,128)(2,1)} %k_ref.7, bf16[128,4096]{1,0:T(8,128)(2,1)} %v_ref.7), custom_call_target="tpu_custom_call" | custom-call | tf_op jit(solution)/shard_map/pallas_call | solution.py:181
  8.7 3.4 %collective-permute-start = (bf16[2,128,2048]{2,1,0:T(8,128)(2,1)}, bf16[2,128,2048]{2,1,0:T(8,128)(2,1)S(1)}, u32[]{:S(2)}, u32[]{:S(2)}) collective-permute-start(bf16[2,128,2048]{2,1,0:T(8,128)(2,1)} %shard_map.50), channel_id=1, source_target_pairs={{0,4},{4,8},{8,12},{12,16},{16,20},{20,24},{24,28},{28,32},{32,36}... | collective-permute-start | bytes 3145736 | tf_op jit(solution)/shard_map/ppermute | solution.py:20
  12.1 0.9 fusion
  12.9 12.7 %collective-permute-start.3 = (bf16[128,2048]{1,0:T(8,128)(2,1)S(1)}, bf16[128,2048]{1,0:T(8,128)(2,1)S(1)}, u32[]{:S(2)}, u32[]{:S(2)}) collective-permute-start(bf16[128,2048]{1,0:T(8,128)(2,1)S(1)} %get-tuple-element.22), channel_id=1, source_target_pairs={{4,0},{8,4},{12,8},{16,12},{20,16},{24,20},{28,24},{32,28},{36,32}... | collective-permute-start | bytes 1572872 | tf_op jit(solution)/shard_map/ppermute | solution.py:26
  25.7 3.9 %collective-permute-start.1 = (bf16[128,2048]{1,0:T(8,128)(2,1)}, bf16[128,2048]{1,0:T(8,128)(2,1)S(1)}, u32[]{:S(2)}, u32[]{:S(2)}) collective-permute-start(bf16[128,2048]{1,0:T(8,128)(2,1)} %get-tuple-element.23), channel_id=1, source_target_pairs={{4,0},{8,4},{12,8},{16,12},{20,16},{24,20},{28,24},{32,28},{36,32}... | collective-permute-start | bytes 1572872 | tf_op jit(solution)/shard_map/ppermute | solution.py:26
  29.6 8.4 %collective-permute-done.3.q_ref = bf16[128,2048]{1,0:T(8,128)(2,1)S(1)} collective-permute-done((bf16[128,2048]{1,0:T(8,128)(2,1)S(1)}, bf16[128,2048]{1,0:T(8,128)(2,1)S(1)}, u32[]{:S(2)}, u32[]{:S(2)}) %collective-permute-start.3) | collective-permute-done | bytes 524320 | tf_op jit(solution)/shard_map/ppermute | solution.py:26
  38.0 4.9 %collective-permute-done.2.kp_ref.vp_ref.k_ref.v_ref = bf16[2,128,2048]{2,1,0:T(8,128)(2,1)S(1)} collective-permute-done((bf16[2,128,2048]{2,1,0:T(8,128)(2,1)}, bf16[2,128,2048]{2,1,0:T(8,128)(2,1)S(1)}, u32[]{:S(2)}, u32[]{:S(2)}) %collective-permute-start.2) | collective-permute-done | bytes 1048608 | tf_op jit(solution)/shard_map/ppermute | solution.py:20
  42.9 0.0 copy-done.3
  42.9 1.0 %copy-done.1 = bf16[2,128,2048]{2,1,0:T(8,128)(2,1)} copy-done((bf16[2,128,2048]{2,1,0:T(8,128)(2,1)}, bf16[2,128,2048]{2,1,0:T(8,128)(2,1)S(1)}, u32[]{:S(2)}) %copy-start.1) | copy-done | bytes 1048600
  43.9 3.4 %shard_map.54 = (bf16[128,2048]{1,0:T(8,128)(2,1)}, f32[1,128,32]{2,1,0:T(8,128)}) custom-call(bf16[128,2048]{1,0:T(8,128)(2,1)} %copy-done.3, bf16[2,128,2048]{2,1,0:T(8,128)(2,1)} %copy-done.1, bf16[2,128,2048]{2,1,0:T(8,128)(2,1)} %copy-done.1), custom_call_target="tpu_custom_call" | custom-call | tf_op jit(solution)/shard_map/pallas_call | solution.py:80
  47.3 1.9 %collective-permute-start.4 = (f32[1,128,32]{2,1,0:T(8,128)}, f32[1,128,32]{2,1,0:T(8,128)S(1)}, u32[]{:S(2)}, u32[]{:S(2)}) collective-permute-start(f32[1,128,32]{2,1,0:T(8,128)} %get-tuple-element.15), channel_id=1, source_target_pairs={{0,4},{4,8},{8,12},{12,16},{16,20},{20,24},{24,28},{28,32},{32,36}... | collective-permute-start | bytes 49160 | tf_op jit(solution)/shard_map/ppermute | solution.py:20
  49.2 1.9 %collective-permute-start.7 = (bf16[128,2048]{1,0:T(8,128)(2,1)}, bf16[128,2048]{1,0:T(8,128)(2,1)S(1)}, u32[]{:S(2)}, u32[]{:S(2)}) collective-permute-start(bf16[128,2048]{1,0:T(8,128)(2,1)} %get-tuple-element.19), channel_id=1, source_target_pairs={{0,4},{4,8},{8,12},{12,16},{16,20},{20,24},{24,28},{28,32},{32,36}... | collective-permute-start | bytes 1572872 | tf_op jit(solution)/shard_map/ppermute | solution.py:20
  51.1 4.5 %shard_map.53 = (f32[128,2048]{1,0:T(8,128)}, f32[1,128,32]{2,1,0:T(8,128)}) custom-call(s32[1]{0:T(128)} %bitcast.block_ref, bf16[128,4096]{1,0:T(8,128)(2,1)} %q_ref.3, bf16[128,4096]{1,0:T(8,128)(2,1)} %k_ref.7, bf16[128,4096]{1,0:T(8,128)(2,1)} %v_ref.7, bf16[2,128,2048]{2,1,0:T(8,128)(2,1)} %copy-done.1, bf16[2,128,2048]{2,1,0:T(8,128)(2,1)} %copy-done.1), custom_call_target="tpu_custom_call" | custom-call | tf_op jit(solution)/shard_map/pallas_call | solution.py:101
  55.7 0.0 collective-permute-done.1.q_ref
  55.7 9.7 %collective-permute-done.kp_ref.vp_ref.k_ref.v_ref = bf16[2,128,2048]{2,1,0:T(8,128)(2,1)S(1)} collective-permute-done((bf16[2,128,2048]{2,1,0:T(8,128)(2,1)}, bf16[2,128,2048]{2,1,0:T(8,128)(2,1)S(1)}, u32[]{:S(2)}, u32[]{:S(2)}) %collective-permute-start) | collective-permute-done | bytes 1048608 | tf_op jit(solution)/shard_map/ppermute | solution.py:20
  65.4 1.4 %collective-permute-done.4.rest_1_.far_ref = f32[1,128,32]{2,1,0:T(8,128)S(1)} collective-permute-done((f32[1,128,32]{2,1,0:T(8,128)}, f32[1,128,32]{2,1,0:T(8,128)S(1)}, u32[]{:S(2)}, u32[]{:S(2)}) %collective-permute-start.4) | collective-permute-done | bytes 16416 | tf_op jit(solution)/shard_map/ppermute | solution.py:20
  66.8 0.0 copy-done
  66.8 0.6 copy-done.7
  67.4 3.3 %shard_map.55 = (bf16[128,2048]{1,0:T(8,128)(2,1)}, f32[1,128,32]{2,1,0:T(8,128)}) custom-call(bf16[128,2048]{1,0:T(8,128)(2,1)} %copy-done.5, bf16[2,128,2048]{2,1,0:T(8,128)(2,1)} %copy-done, bf16[2,128,2048]{2,1,0:T(8,128)(2,1)} %copy-done, f32[1,128,32]{2,1,0:T(8,128)} %get-tuple-element.14.rest_0_.near_ref, f32[1,128,32]{2,1,0:T(8,128)} %copy-done.7), custom_call_target="tpu_custom_call" | custom-call | tf_op jit(solution)/shard_map/pallas_call | solution.py:80
  70.7 1.9 %collective-permute-start.5 = (bf16[128,2048]{1,0:T(8,128)(2,1)}, bf16[128,2048]{1,0:T(8,128)(2,1)S(1)}, u32[]{:S(2)}, u32[]{:S(2)}) collective-permute-start(bf16[128,2048]{1,0:T(8,128)(2,1)} %get-tuple-element.16), channel_id=1, source_target_pairs={{0,4},{4,8},{8,12},{12,16},{16,20},{20,24},{24,28},{28,32},{32,36}... | collective-permute-start | bytes 1572872 | tf_op jit(solution)/shard_map/ppermute | solution.py:20
  72.7 1.9 %collective-permute-start.6 = (f32[1,128,32]{2,1,0:T(8,128)}, f32[1,128,32]{2,1,0:T(8,128)S(1)}, u32[]{:S(2)}, u32[]{:S(2)}) collective-permute-start(f32[1,128,32]{2,1,0:T(8,128)} %get-tuple-element.17), channel_id=1, source_target_pairs={{0,4},{4,8},{8,12},{12,16},{16,20},{20,24},{24,28},{28,32},{32,36}... | collective-permute-start | bytes 49160 | tf_op jit(solution)/shard_map/ppermute | solution.py:20
  74.6 4.5 %shard_map.51 = (f32[128,2048]{1,0:T(8,128)}, f32[1,128,32]{2,1,0:T(8,128)}) custom-call(s32[1]{0:T(128)} %bitcast.block_ref, bf16[128,4096]{1,0:T(8,128)(2,1)} %q_ref.3, bf16[128,4096]{1,0:T(8,128)(2,1)} %k_ref.7, bf16[128,4096]{1,0:T(8,128)(2,1)} %v_ref.7, bf16[2,128,2048]{2,1,0:T(8,128)(2,1)} %copy-done, bf16[2,128,2048]{2,1,0:T(8,128)(2,1)} %copy-done), custom_call_target="tpu_custom_call" | custom-call | tf_op jit(solution)/shard_map/pallas_call | solution.py:101
  79.1 0.0 collective-permute-done.7.o_ref
  79.1 0.8 copy-done.4
  79.9 3.2 %shard_map.56 = (bf16[128,4096]{1,0:T(8,128)(2,1)}, f32[32,128]{1,0:T(8,128)}) custom-call(s32[1]{0:T(128)} %bitcast.block_ref, f32[128,2048]{1,0:T(8,128)} %get-tuple-element.18.mixed_ref, f32[1,128,32]{2,1,0:T(8,128)} %get-tuple-element.14.rest_0_.near_ref, bf16[128,2048]{1,0:T(8,128)(2,1)} %copy-done.4, f32[1,128,32]{2,1,0:T(8,128)} %copy-done.7), custom_call_target="tpu_custom_call" | custom-call | tf_op jit(solution)/shard_map/pallas_call | solution.py:158
  83.1 11.2 %collective-permute-done.6.far_ref = f32[1,128,32]{2,1,0:T(8,128)S(1)} collective-permute-done((f32[1,128,32]{2,1,0:T(8,128)}, f32[1,128,32]{2,1,0:T(8,128)S(1)}, u32[]{:S(2)}, u32[]{:S(2)}) %collective-permute-start.6) | collective-permute-done | bytes 16416 | tf_op jit(solution)/shard_map/ppermute | solution.py:20
  94.3 0.0 collective-permute-done.5.o_ref
  94.3 0.6 copy-done.8
  95.0 0.2 copy-done.6
  95.2 3.2 %shard_map.57 = (bf16[128,4096]{1,0:T(8,128)(2,1)}, f32[32,128]{1,0:T(8,128)}) custom-call(s32[1]{0:T(128)} %bitcast.block_ref, f32[128,2048]{1,0:T(8,128)} %get-tuple-element.12.mixed_ref, f32[1,128,32]{2,1,0:T(8,128)} %get-tuple-element.13.near_ref, bf16[128,2048]{1,0:T(8,128)(2,1)} %copy-done.6, ...), custom_call_target="tpu_custom_call", output_to_operand_aliasing={{0}: (5, {}), {1}: (6, {})} | custom-call | tf_op jit(solution)/shard_map/pallas_call | solution.py:158
  (11 shorter events, 0.0 us)
Async XLA Ops:
  2.9 9.2 %copy-start.2 = (bf16[128,4096]{1,0:T(8,128)(2,1)S(1)}, bf16[128,4096]{1,0:T(8,128)(2,1)}, u32[]{:S(2)}) copy-start(bf16[128,4096]{1,0:T(8,128)(2,1)} %q_ref.3) | copy-start | bytes 3145732
  2.9 40.0 %collective-permute-start.2 = (bf16[2,128,2048]{2,1,0:T(8,128)(2,1)}, bf16[2,128,2048]{2,1,0:T(8,128)(2,1)S(1)}, u32[]{:S(2)}, u32[]{:S(2)}) collective-permute-start(bf16[2,128,2048]{2,1,0:T(8,128)(2,1)} %shard_map.52), channel_id=1, source_target_pairs={{0,4},{4,8},{8,12},{12,16},{16,20},{20,24},{24,28},{28,32},{32,36}... | collective-permute-start | bytes 3145736 | tf_op jit(solution)/shard_map/ppermute | solution.py:20
  8.7 56.7 %collective-permute-start = (bf16[2,128,2048]{2,1,0:T(8,128)(2,1)}, bf16[2,128,2048]{2,1,0:T(8,128)(2,1)S(1)}, u32[]{:S(2)}, u32[]{:S(2)}) collective-permute-start(bf16[2,128,2048]{2,1,0:T(8,128)(2,1)} %shard_map.50), channel_id=1, source_target_pairs={{0,4},{4,8},{8,12},{12,16},{16,20},{20,24},{24,28},{28,32},{32,36}... | collective-permute-start | bytes 3145736 | tf_op jit(solution)/shard_map/ppermute | solution.py:20
  12.9 25.0 %collective-permute-start.3 = (bf16[128,2048]{1,0:T(8,128)(2,1)S(1)}, bf16[128,2048]{1,0:T(8,128)(2,1)S(1)}, u32[]{:S(2)}, u32[]{:S(2)}) collective-permute-start(bf16[128,2048]{1,0:T(8,128)(2,1)S(1)} %get-tuple-element.22), channel_id=1, source_target_pairs={{4,0},{8,4},{12,8},{16,12},{20,16},{24,20},{28,24},{32,28},{36,32}... | collective-permute-start | bytes 1572872 | tf_op jit(solution)/shard_map/ppermute | solution.py:26
  25.7 30.0 %collective-permute-start.1 = (bf16[128,2048]{1,0:T(8,128)(2,1)}, bf16[128,2048]{1,0:T(8,128)(2,1)S(1)}, u32[]{:S(2)}, u32[]{:S(2)}) collective-permute-start(bf16[128,2048]{1,0:T(8,128)(2,1)} %get-tuple-element.23), channel_id=1, source_target_pairs={{4,0},{8,4},{12,8},{16,12},{20,16},{24,20},{28,24},{32,28},{36,32}... | collective-permute-start | bytes 1572872 | tf_op jit(solution)/shard_map/ppermute | solution.py:26
  38.0 4.9 %copy-start.3 = (bf16[128,2048]{1,0:T(8,128)(2,1)}, bf16[128,2048]{1,0:T(8,128)(2,1)S(1)}, u32[]{:S(2)}) copy-start(bf16[128,2048]{1,0:T(8,128)(2,1)S(1)} %collective-permute-done.3.q_ref) | copy-start | bytes 1572868
  42.9 1.0 %copy-start.1 = (bf16[2,128,2048]{2,1,0:T(8,128)(2,1)}, bf16[2,128,2048]{2,1,0:T(8,128)(2,1)S(1)}, u32[]{:S(2)}) copy-start(bf16[2,128,2048]{2,1,0:T(8,128)(2,1)S(1)} %collective-permute-done.2.kp_ref.vp_ref.k_ref.v_ref) | copy-start | bytes 3145732
  47.3 19.5 %collective-permute-start.4 = (f32[1,128,32]{2,1,0:T(8,128)}, f32[1,128,32]{2,1,0:T(8,128)S(1)}, u32[]{:S(2)}, u32[]{:S(2)}) collective-permute-start(f32[1,128,32]{2,1,0:T(8,128)} %get-tuple-element.15), channel_id=1, source_target_pairs={{0,4},{4,8},{8,12},{12,16},{16,20},{20,24},{24,28},{28,32},{32,36}... | collective-permute-start | bytes 49160 | tf_op jit(solution)/shard_map/ppermute | solution.py:20
  49.2 29.9 %collective-permute-start.7 = (bf16[128,2048]{1,0:T(8,128)(2,1)}, bf16[128,2048]{1,0:T(8,128)(2,1)S(1)}, u32[]{:S(2)}, u32[]{:S(2)}) collective-permute-start(bf16[128,2048]{1,0:T(8,128)(2,1)} %get-tuple-element.19), channel_id=1, source_target_pairs={{0,4},{4,8},{8,12},{12,16},{16,20},{20,24},{24,28},{28,32},{32,36}... | collective-permute-start | bytes 1572872 | tf_op jit(solution)/shard_map/ppermute | solution.py:20
  55.7 11.1 %copy-start.5 = (bf16[128,2048]{1,0:T(8,128)(2,1)}, bf16[128,2048]{1,0:T(8,128)(2,1)S(1)}, u32[]{:S(2)}) copy-start(bf16[128,2048]{1,0:T(8,128)(2,1)S(1)} %collective-permute-done.1.q_ref) | copy-start | bytes 1572868
  65.4 1.4 %copy-start = (bf16[2,128,2048]{2,1,0:T(8,128)(2,1)}, bf16[2,128,2048]{2,1,0:T(8,128)(2,1)S(1)}, u32[]{:S(2)}) copy-start(bf16[2,128,2048]{2,1,0:T(8,128)(2,1)S(1)} %collective-permute-done.kp_ref.vp_ref.k_ref.v_ref) | copy-start | bytes 3145732
  66.8 0.6 copy-start.7
  70.7 23.6 %collective-permute-start.5 = (bf16[128,2048]{1,0:T(8,128)(2,1)}, bf16[128,2048]{1,0:T(8,128)(2,1)S(1)}, u32[]{:S(2)}, u32[]{:S(2)}) collective-permute-start(bf16[128,2048]{1,0:T(8,128)(2,1)} %get-tuple-element.16), channel_id=1, source_target_pairs={{0,4},{4,8},{8,12},{12,16},{16,20},{20,24},{24,28},{28,32},{32,36}... | collective-permute-start | bytes 1572872 | tf_op jit(solution)/shard_map/ppermute | solution.py:20
  72.7 21.7 %collective-permute-start.6 = (f32[1,128,32]{2,1,0:T(8,128)}, f32[1,128,32]{2,1,0:T(8,128)S(1)}, u32[]{:S(2)}, u32[]{:S(2)}) collective-permute-start(f32[1,128,32]{2,1,0:T(8,128)} %get-tuple-element.17), channel_id=1, source_target_pairs={{0,4},{4,8},{8,12},{12,16},{16,20},{20,24},{24,28},{28,32},{32,36}... | collective-permute-start | bytes 49160 | tf_op jit(solution)/shard_map/ppermute | solution.py:20
  79.1 0.8 copy-start.4
  94.3 0.6 copy-start.8
  94.3 0.8 copy-start.6

commit v15 on v12

--- a/solution.py
+++ b/solution.py
@@ -130,14 +130,18 @@
     inverse = 1.0 / total
     near_scale = near_scale * inverse
     far_scale = far_scale * inverse
-    diagonal = lax.broadcasted_iota(jnp.int32, (rows, rows), 0) == lax.broadcasted_iota(jnp.int32, (rows, rows), 1)
+    identity = (lax.broadcasted_iota(jnp.int32, (n, n), 0) == lax.broadcasted_iota(jnp.int32, (n, n), 1)).astype(
+        jnp.float32
+    )
     for h in range(n):
         cols = slice(h * HEAD_DIM, (h + 1) * HEAD_DIM)
         mixed = near_scale[:, h : h + 1] * mixed_ref[:, cols] + far_scale[:, h : h + 1] * o_ref[:, cols].astype(
             jnp.float32
         )
         out_ref[:, cols] = mixed.astype(out_ref.dtype)
-        lse_ref[h : h + 1, :] = jnp.sum(jnp.where(diagonal, lse[:, h : h + 1], 0.0), axis=0, keepdims=True)
+    lse_ref[...] = lax.dot_general(
+        identity, lse, NT_DIMS, precision=lax.Precision.HIGHEST, preferred_element_type=jnp.float32
+    )
 
 
 def merged_output(block_index, chunk, width, mixed_near, stat_near, o_far, stat_far, previous):

time: 98.3 us -> 98.1 us (level)
  no operation moved by 1% of the time
where the time goes in v15:
time: 98.1 us; the launch traced here: 97.3 us
  waiting for transfers between devices  37 us (38%)
  starting transfers between devices  31.1 us (32%)
  Pallas kernels  21.6 us (22%)
  local copies, waits for them, and re-layouts  5.72 us (6%)
  other arithmetic  1.16 us (1%)
    ppermute x6, waiting for transfers between devices, from_behind(): return lax.ppermute(block, axis, route)  28.6 us
    ppermute x2, starting transfers between devices, from_ahead(): return lax.ppermute(block, axis, route)  16.7 us
    ppermute x6, starting transfers between devices, from_behind(): return lax.ppermute(block, axis, route)  14.4 us
    pallas_call x2, Pallas kernels, near_attention(): pl.pallas_call(near_kernel, grid_spec=pltpu.PrefetchScalarGridSpec(num_sc...  9.02 us
    ppermute x2, waiting for transfers between devices, from_ahead(): return lax.ppermute(block, axis, route)  8.38 us
    pallas_call x2, Pallas kernels, partial_attention(): pl.pallas_call(partial_kernel, grid=(steps,), in_specs=[block, key_block,...  6.7 us
    pallas_call x2, Pallas kernels, merged_output(): pl.pallas_call(merge_kernel, grid_spec=pltpu.PrefetchScalarGridSpec(num_s...  5.86 us
    unnamed x18, local copies, waits for them, and re-layouts  3.19 us
  transfers between devices with their start and end apart: 8, of which 5 were waited for; matrix products, arithmetic and copies ran while one was open for 2% of the time, Pallas kernels for 19%

profile of v15, /device:TPU:56, one launch (start us, length us, event | category | flops | bytes accessed | tf_op | source)
XLA Modules:
  0.0 97.3 jit_solution(17768093484829600715)
XLA Ops:
  0.6 1.7 %slice_bitcast_fusion = (bf16[1,128,2048]{2,1,0:T(8,128)(2,1)S(1)}, bf16[1,128,2048]{2,1,0:T(8,128)(2,1)S(1)}, bf16[1,128,2048]{2,1,0:T(8,128)(2,1)S(1)}, bf16[1,128,2048]{2,1,0:T(8,128)(2,1)S(1)}) fusion(bf16[128,4096]{1,0:T(8,128)(2,1)} %v_ref.3, bf16[128,4096]{1,0:T(8,128)(2,1)} %k_ref.3), kind=kLoop, calls=%fused_computation.2 | loop fusion | bytes 4194304 | tf_op jit(solution)/shard_map/stack | solution.py:185
  2.3 0.1 pad_maximum_fusion.1
  2.4 3.4 %collective-permute-start.2 = (bf16[2,128,2048]{2,1,0:T(8,128)(2,1)S(1)}, bf16[2,128,2048]{2,1,0:T(8,128)(2,1)S(1)}, u32[]{:S(2)}, u32[]{:S(2)}) collective-permute-start(bf16[2,128,2048]{2,1,0:T(8,128)(2,1)S(1)} %pad_maximum_fusion.1), channel_id=1, source_target_pairs={{0,4},{4,8},{8,12},{12,16},{16,20},{20,24},{24,28},{28,32},{32,36}... | collective-permute-start | bytes 3145736 | tf_op jit(solution)/shard_map/ppermute | solution.py:20
  5.8 0.0 copy-start.2
  5.8 1.1 %pad_maximum_fusion = bf16[2,128,2048]{2,1,0:T(8,128)(2,1)} fusion(bf16[1,128,2048]{2,1,0:T(8,128)(2,1)S(1)} %get-tuple-element.27, bf16[1,128,2048]{2,1,0:T(8,128)(2,1)S(1)} %get-tuple-element.28), kind=kLoop, calls=%fused_computation | loop fusion | flops 524288 | bytes 2097152 | tf_op jit(solution)/shard_map/stack | solution.py:185
  6.9 3.4 %collective-permute-start = (bf16[2,128,2048]{2,1,0:T(8,128)(2,1)}, bf16[2,128,2048]{2,1,0:T(8,128)(2,1)S(1)}, u32[]{:S(2)}, u32[]{:S(2)}) collective-permute-start(bf16[2,128,2048]{2,1,0:T(8,128)(2,1)} %pad_maximum_fusion), channel_id=1, source_target_pairs={{0,4},{4,8},{8,12},{12,16},{16,20},{20,24},{24,28},{28,32},{32,36}... | collective-permute-start | bytes 3145736 | tf_op jit(solution)/shard_map/ppermute | solution.py:20
  10.3 0.9 fusion
  11.2 12.7 %collective-permute-start.3 = (bf16[128,2048]{1,0:T(8,128)(2,1)S(1)}, bf16[128,2048]{1,0:T(8,128)(2,1)S(1)}, u32[]{:S(2)}, u32[]{:S(2)}) collective-permute-start(bf16[128,2048]{1,0:T(8,128)(2,1)S(1)} %get-tuple-element.22), channel_id=1, source_target_pairs={{4,0},{8,4},{12,8},{16,12},{20,16},{24,20},{28,24},{32,28},{36,32}... | collective-permute-start | bytes 1572872 | tf_op jit(solution)/shard_map/ppermute | solution.py:26
  23.9 3.9 %collective-permute-start.1 = (bf16[128,2048]{1,0:T(8,128)(2,1)}, bf16[128,2048]{1,0:T(8,128)(2,1)S(1)}, u32[]{:S(2)}, u32[]{:S(2)}) collective-permute-start(bf16[128,2048]{1,0:T(8,128)(2,1)} %get-tuple-element.23), channel_id=1, source_target_pairs={{4,0},{8,4},{12,8},{16,12},{20,16},{24,20},{28,24},{32,28},{36,32}... | collective-permute-start | bytes 1572872 | tf_op jit(solution)/shard_map/ppermute | solution.py:26
  27.8 8.4 %collective-permute-done.3.q_ref = bf16[128,2048]{1,0:T(8,128)(2,1)S(1)} collective-permute-done((bf16[128,2048]{1,0:T(8,128)(2,1)S(1)}, bf16[128,2048]{1,0:T(8,128)(2,1)S(1)}, u32[]{:S(2)}, u32[]{:S(2)}) %collective-permute-start.3) | collective-permute-done | bytes 524320 | tf_op jit(solution)/shard_map/ppermute | solution.py:26
  36.2 5.9 %collective-permute-done.2.kp_ref.vp_ref.k_ref.v_ref = bf16[2,128,2048]{2,1,0:T(8,128)(2,1)S(1)} collective-permute-done((bf16[2,128,2048]{2,1,0:T(8,128)(2,1)S(1)}, bf16[2,128,2048]{2,1,0:T(8,128)(2,1)S(1)}, u32[]{:S(2)}, u32[]{:S(2)}) %collective-permute-start.2) | collective-permute-done | bytes 1048608 | tf_op jit(solution)/shard_map/ppermute | solution.py:20
  42.1 1.0 copy-done.1
  43.0 3.3 %shard_map.52 = (bf16[128,2048]{1,0:T(8,128)(2,1)}, f32[1,128,32]{2,1,0:T(8,128)}) custom-call(bf16[128,2048]{1,0:T(8,128)(2,1)} %copy-done.3, bf16[2,128,2048]{2,1,0:T(8,128)(2,1)} %copy-done.1, bf16[2,128,2048]{2,1,0:T(8,128)(2,1)} %copy-done.1), custom_call_target="tpu_custom_call" | custom-call | tf_op jit(solution)/shard_map/pallas_call | solution.py:80
  46.4 1.9 %collective-permute-start.4 = (f32[1,128,32]{2,1,0:T(8,128)}, f32[1,128,32]{2,1,0:T(8,128)S(1)}, u32[]{:S(2)}, u32[]{:S(2)}) collective-permute-start(f32[1,128,32]{2,1,0:T(8,128)} %get-tuple-element.15), channel_id=1, source_target_pairs={{0,4},{4,8},{8,12},{12,16},{16,20},{20,24},{24,28},{28,32},{32,36}... | collective-permute-start | bytes 49160 | tf_op jit(solution)/shard_map/ppermute | solution.py:20
  48.3 1.9 %collective-permute-start.7 = (bf16[128,2048]{1,0:T(8,128)(2,1)}, bf16[128,2048]{1,0:T(8,128)(2,1)S(1)}, u32[]{:S(2)}, u32[]{:S(2)}) collective-permute-start(bf16[128,2048]{1,0:T(8,128)(2,1)} %get-tuple-element.19), channel_id=1, source_target_pairs={{0,4},{4,8},{8,12},{12,16},{16,20},{20,24},{24,28},{28,32},{32,36}... | collective-permute-start | bytes 1572872 | tf_op jit(solution)/shard_map/ppermute | solution.py:20
  50.2 4.5 %shard_map.51 = (f32[128,2048]{1,0:T(8,128)}, f32[1,128,32]{2,1,0:T(8,128)}) custom-call(s32[1]{0:T(128)} %bitcast.block_ref, bf16[128,4096]{1,0:T(8,128)(2,1)} %q_ref.3, bf16[128,4096]{1,0:T(8,128)(2,1)} %k_ref.3, bf16[128,4096]{1,0:T(8,128)(2,1)} %v_ref.3, bf16[2,128,2048]{2,1,0:T(8,128)(2,1)} %copy-done.1, bf16[2,128,2048]{2,1,0:T(8,128)(2,1)} %copy-done.1), custom_call_target="tpu_custom_call" | custom-call | tf_op jit(solution)/shard_map/pallas_call | solution.py:101
  54.8 0.0 collective-permute-done.1.q_ref
  54.8 9.8 %collective-permute-done.kp_ref.vp_ref.k_ref.v_ref = bf16[2,128,2048]{2,1,0:T(8,128)(2,1)S(1)} collective-permute-done((bf16[2,128,2048]{2,1,0:T(8,128)(2,1)}, bf16[2,128,2048]{2,1,0:T(8,128)(2,1)S(1)}, u32[]{:S(2)}, u32[]{:S(2)}) %collective-permute-start) | collective-permute-done | bytes 1048608 | tf_op jit(solution)/shard_map/ppermute | solution.py:20
  64.6 1.4 %collective-permute-done.4.rest_1_.far_ref = f32[1,128,32]{2,1,0:T(8,128)S(1)} collective-permute-done((f32[1,128,32]{2,1,0:T(8,128)}, f32[1,128,32]{2,1,0:T(8,128)S(1)}, u32[]{:S(2)}, u32[]{:S(2)}) %collective-permute-start.4) | collective-permute-done | bytes 16416 | tf_op jit(solution)/shard_map/ppermute | solution.py:20
  66.0 0.6 copy-done.7
  66.6 3.4 %shard_map.53 = (bf16[128,2048]{1,0:T(8,128)(2,1)}, f32[1,128,32]{2,1,0:T(8,128)}) custom-call(bf16[128,2048]{1,0:T(8,128)(2,1)} %copy-done.5, bf16[2,128,2048]{2,1,0:T(8,128)(2,1)} %copy-done, bf16[2,128,2048]{2,1,0:T(8,128)(2,1)} %copy-done, f32[1,128,32]{2,1,0:T(8,128)} %get-tuple-element.14.rest_0_.near_ref, f32[1,128,32]{2,1,0:T(8,128)} %copy-done.7), custom_call_target="tpu_custom_call" | custom-call | tf_op jit(solution)/shard_map/pallas_call | solution.py:80
  69.9 1.9 %collective-permute-start.5 = (bf16[128,2048]{1,0:T(8,128)(2,1)}, bf16[128,2048]{1,0:T(8,128)(2,1)S(1)}, u32[]{:S(2)}, u32[]{:S(2)}) collective-permute-start(bf16[128,2048]{1,0:T(8,128)(2,1)} %get-tuple-element.16), channel_id=1, source_target_pairs={{0,4},{4,8},{8,12},{12,16},{16,20},{20,24},{24,28},{28,32},{32,36}... | collective-permute-start | bytes 1572872 | tf_op jit(solution)/shard_map/ppermute | solution.py:20
  71.8 1.9 %collective-permute-start.6 = (f32[1,128,32]{2,1,0:T(8,128)}, f32[1,128,32]{2,1,0:T(8,128)S(1)}, u32[]{:S(2)}, u32[]{:S(2)}) collective-permute-start(f32[1,128,32]{2,1,0:T(8,128)} %get-tuple-element.17), channel_id=1, source_target_pairs={{0,4},{4,8},{8,12},{12,16},{16,20},{20,24},{24,28},{28,32},{32,36}... | collective-permute-start | bytes 49160 | tf_op jit(solution)/shard_map/ppermute | solution.py:20
  73.8 4.5 %shard_map.50 = (f32[128,2048]{1,0:T(8,128)}, f32[1,128,32]{2,1,0:T(8,128)}) custom-call(s32[1]{0:T(128)} %bitcast.block_ref, bf16[128,4096]{1,0:T(8,128)(2,1)} %q_ref.3, bf16[128,4096]{1,0:T(8,128)(2,1)} %k_ref.3, bf16[128,4096]{1,0:T(8,128)(2,1)} %v_ref.3, bf16[2,128,2048]{2,1,0:T(8,128)(2,1)} %copy-done, bf16[2,128,2048]{2,1,0:T(8,128)(2,1)} %copy-done), custom_call_target="tpu_custom_call" | custom-call | tf_op jit(solution)/shard_map/pallas_call | solution.py:101
  78.3 0.0 collective-permute-done.7.o_ref
  78.3 0.8 copy-done.4
  79.1 2.9 %shard_map.54 = (bf16[128,4096]{1,0:T(8,128)(2,1)}, f32[32,128]{1,0:T(8,128)}) custom-call(s32[1]{0:T(128)} %bitcast.block_ref, f32[128,2048]{1,0:T(8,128)} %get-tuple-element.18.mixed_ref, f32[1,128,32]{2,1,0:T(8,128)} %get-tuple-element.14.rest_0_.near_ref, bf16[128,2048]{1,0:T(8,128)(2,1)} %copy-done.4, f32[1,128,32]{2,1,0:T(8,128)} %copy-done.7), custom_call_target="tpu_custom_call" | custom-call | tf_op jit(solution)/shard_map/pallas_call | solution.py:162
  82.0 11.5 %collective-permute-done.6.far_ref = f32[1,128,32]{2,1,0:T(8,128)S(1)} collective-permute-done((f32[1,128,32]{2,1,0:T(8,128)}, f32[1,128,32]{2,1,0:T(8,128)S(1)}, u32[]{:S(2)}, u32[]{:S(2)}) %collective-permute-start.6) | collective-permute-done | bytes 16416 | tf_op jit(solution)/shard_map/ppermute | solution.py:20
  93.5 0.0 collective-permute-done.5.o_ref
  93.5 0.6 copy-done.8
  94.1 0.2 copy-done.6
  94.3 2.9 %shard_map.55 = (bf16[128,4096]{1,0:T(8,128)(2,1)}, f32[32,128]{1,0:T(8,128)}) custom-call(s32[1]{0:T(128)} %bitcast.block_ref, f32[128,2048]{1,0:T(8,128)} %get-tuple-element.12.mixed_ref, f32[1,128,32]{2,1,0:T(8,128)} %get-tuple-element.13.near_ref, bf16[128,2048]{1,0:T(8,128)(2,1)} %copy-done.6, ...), custom_call_target="tpu_custom_call", output_to_operand_aliasing={{0}: (5, {}), {1}: (6, {})} | custom-call | tf_op jit(solution)/shard_map/pallas_call | solution.py:162
  (12 shorter events, 0.0 us)
Async XLA Ops:
  2.4 39.7 %collective-permute-start.2 = (bf16[2,128,2048]{2,1,0:T(8,128)(2,1)S(1)}, bf16[2,128,2048]{2,1,0:T(8,128)(2,1)S(1)}, u32[]{:S(2)}, u32[]{:S(2)}) collective-permute-start(bf16[2,128,2048]{2,1,0:T(8,128)(2,1)S(1)} %pad_maximum_fusion.1), channel_id=1, source_target_pairs={{0,4},{4,8},{8,12},{12,16},{16,20},{20,24},{24,28},{28,32},{32,36}... | collective-permute-start | bytes 3145736 | tf_op jit(solution)/shard_map/ppermute | solution.py:20
  5.8 4.5 %copy-start.2 = (bf16[128,4096]{1,0:T(8,128)(2,1)S(1)}, bf16[128,4096]{1,0:T(8,128)(2,1)}, u32[]{:S(2)}) copy-start(bf16[128,4096]{1,0:T(8,128)(2,1)} %q_ref.3) | copy-start | bytes 3145732
  6.9 57.7 %collective-permute-start = (bf16[2,128,2048]{2,1,0:T(8,128)(2,1)}, bf16[2,128,2048]{2,1,0:T(8,128)(2,1)S(1)}, u32[]{:S(2)}, u32[]{:S(2)}) collective-permute-start(bf16[2,128,2048]{2,1,0:T(8,128)(2,1)} %pad_maximum_fusion), channel_id=1, source_target_pairs={{0,4},{4,8},{8,12},{12,16},{16,20},{20,24},{24,28},{28,32},{32,36}... | collective-permute-start | bytes 3145736 | tf_op jit(solution)/shard_map/ppermute | solution.py:20
  11.2 25.0 %collective-permute-start.3 = (bf16[128,2048]{1,0:T(8,128)(2,1)S(1)}, bf16[128,2048]{1,0:T(8,128)(2,1)S(1)}, u32[]{:S(2)}, u32[]{:S(2)}) collective-permute-start(bf16[128,2048]{1,0:T(8,128)(2,1)S(1)} %get-tuple-element.22), channel_id=1, source_target_pairs={{4,0},{8,4},{12,8},{16,12},{20,16},{24,20},{28,24},{32,28},{36,32}... | collective-permute-start | bytes 1572872 | tf_op jit(solution)/shard_map/ppermute | solution.py:26
  23.9 30.9 %collective-permute-start.1 = (bf16[128,2048]{1,0:T(8,128)(2,1)}, bf16[128,2048]{1,0:T(8,128)(2,1)S(1)}, u32[]{:S(2)}, u32[]{:S(2)}) collective-permute-start(bf16[128,2048]{1,0:T(8,128)(2,1)} %get-tuple-element.23), channel_id=1, source_target_pairs={{4,0},{8,4},{12,8},{16,12},{20,16},{24,20},{28,24},{32,28},{36,32}... | collective-permute-start | bytes 1572872 | tf_op jit(solution)/shard_map/ppermute | solution.py:26
  36.2 5.9 %copy-start.3 = (bf16[128,2048]{1,0:T(8,128)(2,1)}, bf16[128,2048]{1,0:T(8,128)(2,1)S(1)}, u32[]{:S(2)}) copy-start(bf16[128,2048]{1,0:T(8,128)(2,1)S(1)} %collective-permute-done.3.q_ref) | copy-start | bytes 1572868
  42.1 1.0 copy-start.1
  46.4 19.6 %collective-permute-start.4 = (f32[1,128,32]{2,1,0:T(8,128)}, f32[1,128,32]{2,1,0:T(8,128)S(1)}, u32[]{:S(2)}, u32[]{:S(2)}) collective-permute-start(f32[1,128,32]{2,1,0:T(8,128)} %get-tuple-element.15), channel_id=1, source_target_pairs={{0,4},{4,8},{8,12},{12,16},{16,20},{20,24},{24,28},{28,32},{32,36}... | collective-permute-start | bytes 49160 | tf_op jit(solution)/shard_map/ppermute | solution.py:20
  48.3 30.0 %collective-permute-start.7 = (bf16[128,2048]{1,0:T(8,128)(2,1)}, bf16[128,2048]{1,0:T(8,128)(2,1)S(1)}, u32[]{:S(2)}, u32[]{:S(2)}) collective-permute-start(bf16[128,2048]{1,0:T(8,128)(2,1)} %get-tuple-element.19), channel_id=1, source_target_pairs={{0,4},{4,8},{8,12},{12,16},{16,20},{20,24},{24,28},{28,32},{32,36}... | collective-permute-start | bytes 1572872 | tf_op jit(solution)/shard_map/ppermute | solution.py:20
  54.8 11.2 %copy-start.5 = (bf16[128,2048]{1,0:T(8,128)(2,1)}, bf16[128,2048]{1,0:T(8,128)(2,1)S(1)}, u32[]{:S(2)}) copy-start(bf16[128,2048]{1,0:T(8,128)(2,1)S(1)} %collective-permute-done.1.q_ref) | copy-start | bytes 1572868
  64.6 1.4 %copy-start = (bf16[2,128,2048]{2,1,0:T(8,128)(2,1)}, bf16[2,128,2048]{2,1,0:T(8,128)(2,1)S(1)}, u32[]{:S(2)}) copy-start(bf16[2,128,2048]{2,1,0:T(8,128)(2,1)S(1)} %collective-permute-done.kp_ref.vp_ref.k_ref.v_ref) | copy-start | bytes 3145732
  66.0 0.6 copy-start.7
  69.9 23.6 %collective-permute-start.5 = (bf16[128,2048]{1,0:T(8,128)(2,1)}, bf16[128,2048]{1,0:T(8,128)(2,1)S(1)}, u32[]{:S(2)}, u32[]{:S(2)}) collective-permute-start(bf16[128,2048]{1,0:T(8,128)(2,1)} %get-tuple-element.16), channel_id=1, source_target_pairs={{0,4},{4,8},{8,12},{12,16},{16,20},{20,24},{24,28},{28,32},{32,36}... | collective-permute-start | bytes 1572872 | tf_op jit(solution)/shard_map/ppermute | solution.py:20
  71.8 21.7 %collective-permute-start.6 = (f32[1,128,32]{2,1,0:T(8,128)}, f32[1,128,32]{2,1,0:T(8,128)S(1)}, u32[]{:S(2)}, u32[]{:S(2)}) collective-permute-start(f32[1,128,32]{2,1,0:T(8,128)} %get-tuple-element.17), channel_id=1, source_target_pairs={{0,4},{4,8},{8,12},{12,16},{16,20},{20,24},{24,28},{28,32},{32,36}... | collective-permute-start | bytes 49160 | tf_op jit(solution)/shard_map/ppermute | solution.py:20
  78.3 0.8 copy-start.4
  93.5 0.6 copy-start.8
  93.5 0.8 copy-start.6
